TPU v7x, 256 devices: a whole 4x4x8 slice. The times are simulated.
256 devices in a mesh: section: 2 (over core), dp: 16 (over y_hi, z), cls: 8 (over x, y_lo).
Axes of the slice: x: 4, y: 4 (y_hi: 2, y_lo: 2; y = y_hi * 2 + y_lo), z: 8, core: 2. Of those that a mesh axis runs over, the one named last changes fastest.
Arguments:
- embeddings: bfloat16 [2048, 512], P('dp')
- centers: bfloat16 [1048576, 512], P(('section', 'dp', 'cls'))
- sample_ids: int32 [256, 1536], P(('section', 'dp', 'cls')), may hold values from 0 to 4095, as said below
- labels: int32 [2048], P('dp'), may hold values from 0 to 1048575, as said below
Outputs:
- feature_grad: float32 [2048, 512], P(('section', 'dp', 'cls'))
- row_loss: float32 [2048], P('dp')
Inputs may be any that keep to these rules, and one draw needn't show every extreme that they name: `sample_ids`: the 1536 entries of each row are distinct. For each row, labels // 4096 names a shard j, and labels % 4096 is among sample_ids[j].
All inputs are finite; a program needn't handle non-finite values.
Results may differ from a plain program's by a relative error of at most 0.0033.
Values may be sent and summed in bfloat16 or wider, within the bound.
No kernel may reach another device: no remote copies, remote signals or barrier semaphores. Data moves between devices by JAX's collectives and lax.ppermute only.
A program may use at most 64 MiB of HBM per device.

v0:
```python
import jax
import jax.numpy as jnp
from jax import lax
from jax.sharding import PartitionSpec as P

LOGIT_SCALE = 64.0
MARGIN = 0.35
EPSILON = 1e-06


def on_device(embeddings, centers, sample_ids, labels):
    shard_index = lax.axis_index(("section", "dp", "cls"))
    per_shard = centers.shape[0]
    gathered, label_all = (
        lax.all_gather(embeddings, "dp", axis=0, tiled=True),
        lax.all_gather(labels, "dp", axis=0, tiled=True),
    )
    total_rows = gathered.shape[0]
    emb_float = gathered.astype(jnp.float32)
    row_norm = jnp.sqrt(jnp.sum(emb_float * emb_float, axis=1) + EPSILON)
    unit_rows = (emb_float / row_norm[:, None]).astype(jnp.bfloat16)
    local_ids = sample_ids[0]
    chosen = jnp.take(centers, local_ids, axis=0).astype(jnp.float32)
    center_norm = jnp.sqrt(jnp.sum(chosen * chosen, axis=1) + EPSILON)
    unit_centers = (chosen / center_norm[:, None]).astype(jnp.bfloat16)
    cosine = lax.dot_general(
        unit_rows, unit_centers, (((1,), (1,)), ((), ())), preferred_element_type=jnp.float32
    )
    local_labels = label_all - shard_index * per_shard
    matches = local_ids[None, :] == local_labels[:, None]
    logits = LOGIT_SCALE * cosine - LOGIT_SCALE * MARGIN * matches.astype(jnp.float32)
    exponent = jnp.exp(logits)
    total_part = jnp.sum(exponent, axis=1)
    target_part = jnp.sum(jnp.where(matches, logits, jnp.float32(0.0)), axis=1)
    total, target = lax.psum((total_part, target_part), ("section", "dp", "cls"))
    weights = exponent.astype(jnp.bfloat16)
    column_ids = jnp.arange(local_ids.shape[0], dtype=jnp.int32)
    position = jnp.sum(jnp.where(matches, column_ids[None, :], 0), axis=1)
    owned = jnp.any(matches, axis=1).astype(jnp.float32)
    own_center = jnp.take(unit_centers, position, axis=0).astype(jnp.float32) * owned[:, None]
    section_count = lax.axis_size("section")
    batch_count = lax.axis_size("dp")
    class_count = lax.axis_size("cls")
    rows_here = total_rows // (section_count * batch_count * class_count)
    unscaled = jnp.dot(weights, unit_centers, preferred_element_type=jnp.float32)
    unit_grad = lax.psum_scatter(
        LOGIT_SCALE * (unscaled / total[:, None] - own_center),
        ("section", "dp", "cls"),
        scatter_dimension=0,
        tiled=True,
    )
    emb_rows = lax.dynamic_slice_in_dim(emb_float, shard_index * rows_here, rows_here, 0)
    norm_rows = lax.dynamic_slice_in_dim(row_norm, shard_index * rows_here, rows_here, 0)
    unit_float = emb_rows / norm_rows[:, None]
    along = jnp.sum(unit_float * unit_grad, axis=1, keepdims=True)
    feature_grad = (unit_grad - unit_float * along) / norm_rows[:, None]
    loss_all = jnp.log(total) - target
    own_rows = embeddings.shape[0]
    row_loss = lax.dynamic_slice_in_dim(loss_all, lax.axis_index("dp") * own_rows, own_rows, 0)
    return (feature_grad, row_loss)


def solution(mesh):
    return jax.shard_map(
        on_device,
        mesh=mesh,
        in_specs=(
            P("dp", None),
            P(("section", "dp", "cls"), None),
            P(("section", "dp", "cls"), None),
            P("dp"),
        ),
        out_specs=(P(("section", "dp", "cls"), None), P("dp")),
        check_vma=False,
    )
```

profile of v0, /device:TPU:1, one launch (start us, length us, event | category | flops | bytes accessed | tf_op | source)
XLA Modules:
  0.0 1521.3 jit_solution(12789887926903769523)
XLA Ops:
  7.2 0.0 all-gather.3.cloned.1.call-start
  7.2 0.7 all-gather.3.cloned.1.call-update
  7.9 0.0 reduce-scatter.2.cloned.1.call-start
  8.0 0.7 reduce
  8.7 37.8 %all-gather = s32[16,1,128]{2,1,0:T(1,128)S(1)} all-gather(s32[1,1,128]{2,1,0:T(1,128)} %bitcast.16), channel_id=1, replica_groups=mesh['section'=2,'dp'=16,'cls'=8] {'dp'}, dimensions={0}, use_global_device_ids=true | all-gather | bytes 8704 | tf_op jit(solution)/shard_map/all_gather | solution.py:16
  46.5 1.7 compare_reduce_fusion
  48.2 0.7 fusion.8
  48.9 7.6 gather_fusion
  56.5 0.8 fusion.4
  57.3 1.3 fusion.1
  58.7 1.1 fusion.5
  59.8 9.2 gather_fusion.1
  69.0 27.1 %all-gather.3.cloned.1.call-done = bf16[2048,512]{1,0:T(8,128)(2,1)} async-done(((bf16[128,512]{1,0:T(8,128)(2,1)}), bf16[2048,512]{1,0:T(8,128)(2,1)}) %all-gather.3.cloned.1.call-update) | async-done | bytes 2097168 | tf_op jit(solution)/shard_map/all_gather | solution.py:15
  96.1 2.1 multiply_reduce_fusion
  98.2 9.7 fusion.2
  107.9 78.5 %all-reduce = (f32[2048]{0:T(1024)S(1)}, f32[2048]{0:T(1024)S(1)}) all-reduce(f32[2048]{0:T(1024)S(1)} %get-tuple-element.3, f32[2048]{0:T(1024)S(1)} %get-tuple-element.2), channel_id=1, replica_groups=mesh['section'=2,'dp'=16,'cls'=8] {'section','dp','cls'}, use_global_device_ids=true, to_apply=%region_3.4 | all-reduce | flops 4096 | bytes 32768 | tf_op jit(solution)/shard_map/psum | solution.py:35
  186.4 8.4 subtract_multiply_fusion
  194.8 0.0 copy-start
  194.8 0.0 reduce-scatter.2.cloned.1.call-update
  194.8 0.1 dynamic_slice.10
  194.9 1.5 copy-done
  196.4 2.5 convert_element_type.26
  198.9 0.6 dynamic-slice_subtract_fusion
  199.5 1312.6 %reduce-scatter.2.cloned.1.call-done = f32[8,512]{1,0:T(8,128)} async-done(((f32[2048,512]{1,0:T(8,128)}), f32[8,512]{1,0:T(8,128)}) %reduce-scatter.2.cloned.1.call-update) | async-done | bytes 16400 | tf_op jit(solution)/shard_map/reduce_scatter | solution.py:46
  1512.2 0.9 multiply_reduce_fusion.1
  1513.1 1.4 subtract_divide_fusion
  (9 shorter events, 0.1 us)
Async XLA Ops:
  7.2 88.9 %all-gather.3.cloned.1.call-start = ((), (), s32[]{:S(2)}) async-start(), calls=%async_computation.1 | async-start | bytes 2228224 | tf_op jit(solution)/shard_map/all_gather | solution.py:15
  7.9 1504.3 %reduce-scatter.2.cloned.1.call-start = ((), (), s32[]{:S(2)}) async-start(), calls=%async_computation.2 | async-start | bytes 4210688 | tf_op jit(solution)/shard_map/reduce_scatter | solution.py:46
  194.8 1.6 copy-start
Sparse Core Ops, SparseCore 0:
  10.6 85.4 all-gather.2
  195.0 1317.1 reduce-scatter.1
where the time goes:
time: 1520 us
  waiting for transfers between devices  1340 us (88%)
  blocking collectives  116 us (8%)
  local copies, waits for them, and re-layouts  18.3 us (1%)
  matrix products  18.1 us (1%)
    reduce_scatter x1, waiting for transfers between devices, on_device(): lax.psum_scatter(LOGIT_SCALE * (unscaled / total[:, None] - own_center),...  1310 us
    psum x1, blocking collectives, on_device(): lax.psum((total_part, target_part), ('section', 'dp', 'cls'))  78.5 us
    all_gather x1, blocking collectives, on_device(): lax.all_gather(labels, 'dp', axis=0, tiled=True)  37.8 us
  transfers between devices with their start and end apart: 2, of which 2 were waited for; matrix products, arithmetic and copies ran while one was open for 2% of the time, Pallas kernels for 0%

commit v1 on v0

--- a/solution.py
+++ b/solution.py
@@ -32,7 +32,9 @@
     exponent = jnp.exp(logits)
     total_part = jnp.sum(exponent, axis=1)
     target_part = jnp.sum(jnp.where(matches, logits, jnp.float32(0.0)), axis=1)
-    total, target = lax.psum((total_part, target_part), ("section", "dp", "cls"))
+    total, target = (total_part, target_part)
+    for axis in ("section", "cls", "dp"):
+        total, target = lax.psum((total, target), axis)
     weights = exponent.astype(jnp.bfloat16)
     column_ids = jnp.arange(local_ids.shape[0], dtype=jnp.int32)
     position = jnp.sum(jnp.where(matches, column_ids[None, :], 0), axis=1)
@@ -43,12 +45,11 @@
     class_count = lax.axis_size("cls")
     rows_here = total_rows // (section_count * batch_count * class_count)
     unscaled = jnp.dot(weights, unit_centers, preferred_element_type=jnp.float32)
-    unit_grad = lax.psum_scatter(
-        LOGIT_SCALE * (unscaled / total[:, None] - own_center),
-        ("section", "dp", "cls"),
-        scatter_dimension=0,
-        tiled=True,
-    )
+    partial = LOGIT_SCALE * (unscaled / total[:, None] - own_center)
+    partial = partial.reshape(section_count, batch_count, class_count, rows_here, partial.shape[-1])
+    for axis in ("section", "dp", "cls"):
+        partial = lax.psum_scatter(partial, axis, scatter_dimension=0, tiled=False)
+    unit_grad = partial
     emb_rows = lax.dynamic_slice_in_dim(emb_float, shard_index * rows_here, rows_here, 0)
     norm_rows = lax.dynamic_slice_in_dim(row_norm, shard_index * rows_here, rows_here, 0)
     unit_float = emb_rows / norm_rows[:, None]

time: 1520 us -> 504 us (0.33)
  waiting for transfers between devices: 1340 us -> 304 us
  blocking collectives: 116 us -> 132 us
    reduce_scatter x1 -> x3, waiting for transfers between devices: 1310 us -> 276 us  [on_device(): partial = lax.psum_scatter(partial, axis, scatter_dimension=0, tiled=False)]
    psum x1 -> x3, blocking collectives: 78.5 us -> 94.2 us  [on_device(): total, target = lax.psum((total, target), axis)]
  transfers between devices with their start and end apart: 2 -> 4, of which waited for: 2 -> 4; matrix products, arithmetic and copies ran while one was open for 2% -> 5% of each run, Pallas kernels for 0% -> 0%
where the time goes in v1:
time: 504 us; the launch traced here: 499 us
  waiting for transfers between devices  304 us (60%)
  blocking collectives  132 us (26%)
  matrix products  18.1 us (4%)
  local copies, waits for them, and re-layouts  16.8 us (3%)
  other arithmetic  13.9 us (3%)
  between operations  13.9 us (3%)
    reduce_scatter x3, waiting for transfers between devices, on_device(): partial = lax.psum_scatter(partial, axis, scatter_dimension=0, tiled=False)  276 us
    psum x3, blocking collectives, on_device(): total, target = lax.psum((total, target), axis)  94.2 us
    all_gather x1, blocking collectives, on_device(): lax.all_gather(labels, 'dp', axis=0, tiled=True)  37.8 us
    all_gather x1, waiting for transfers between devices, on_device(): lax.all_gather(embeddings, 'dp', axis=0, tiled=True)  27.1 us
  transfers between devices with their start and end apart: 4, of which 4 were waited for; matrix products, arithmetic and copies ran while one was open for 5% of the time, Pallas kernels for 0%

profile of v1, /device:TPU:1, one launch (start us, length us, event | category | flops | bytes accessed | tf_op | source)
XLA Modules:
  0.0 499.1 jit_solution(4921590129025864350)
XLA Ops:
  7.2 0.0 all-gather.3.cloned.1.call-start
  7.2 0.7 all-gather.3.cloned.1.call-update
  7.9 0.0 reduce-scatter.4.cloned.1.call-start
  8.0 0.7 reduce
  8.7 37.8 %all-gather = s32[16,1,128]{2,1,0:T(1,128)S(1)} all-gather(s32[1,1,128]{2,1,0:T(1,128)} %bitcast.29), channel_id=1, replica_groups=mesh['section'=2,'dp'=16,'cls'=8] {'dp'}, dimensions={0}, use_global_device_ids=true | all-gather | bytes 8704 | tf_op jit(solution)/shard_map/all_gather | solution.py:16
  46.5 1.7 compare_reduce_fusion
  48.2 0.7 fusion.10
  48.9 7.6 %gather_fusion = bf16[1536,512]{1,0:T(8,128)(2,1)S(1)} fusion(bf16[4096,512]{1,0:T(8,128)(2,1)} %param.5, s32[2048]{0:T(1024)S(1)} %pad_clamp_fusion), kind=kCustom, calls=%fused_computation | custom fusion | bytes 3151872 | tf_op jit(solution)/shard_map/jit(_take)/gather | solution.py:23
  56.5 0.8 fusion.4
  57.3 1.3 fusion.1
  58.7 1.1 fusion.5
  59.8 9.2 %gather_fusion.1 = bf16[2048,512]{1,0:T(8,128)(2,1)} fusion(bf16[1536,512]{1,0:T(8,128)(2,1)S(1)} %fusion.5, s32[2048]{0:T(1024)S(1)} %broadcast_clamp_fusion), kind=kCustom, calls=%fused_computation.1 | custom fusion | bytes 4202496 | tf_op jit(solution)/shard_map/jit(_take)/gather | solution.py:42
  69.0 27.1 %all-gather.3.cloned.1.call-done = bf16[2048,512]{1,0:T(8,128)(2,1)} async-done(((bf16[128,512]{1,0:T(8,128)(2,1)}), bf16[2048,512]{1,0:T(8,128)(2,1)}) %all-gather.3.cloned.1.call-update) | async-done | bytes 2097168 | tf_op jit(solution)/shard_map/all_gather | solution.py:15
  96.1 2.1 multiply_reduce_fusion
  98.2 9.7 %fusion.2 = (f32[2048]{0:T(1024)S(1)}, f32[2048]{0:T(1024)S(1)}, f32[2048,1536]{0,1:T(8,128)}) fusion(s32[2048]{0:T(1024)S(1)} %bitcast.28, s32[1536]{0:T(1024)S(1)} %reduce, bf16[1536,512]{1,0:T(8,128)(2,1)S(1)} %fusion.5, f32[2048]{0:T(1024)S(1)} %add_sqrt_fusion.1, bf16[2048,512]{1,0:T(8,128)(2,1)} %all-gather.3.cloned.1.call-done), kind=kOutput, calls=%fused_computation.8 | convolution fusion | flops 3246387200 | bytes 16291840 | tf_op jit(solution)/shard_map/dot_general | solution.py:26
  107.9 7.4 %all-reduce.2 = (f32[2048]{0:T(1024)S(1)}, f32[2048]{0:T(1024)S(1)}) all-reduce(f32[2048]{0:T(1024)S(1)} %get-tuple-element.3, f32[2048]{0:T(1024)S(1)} %get-tuple-element.2), channel_id=1, replica_groups=mesh['section'=2,'dp'=16,'cls'=8] {'section'}, use_global_device_ids=true, to_apply=%region_3.4 | all-reduce | flops 4096 | bytes 32768 | tf_op jit(solution)/shard_map/psum | solution.py:37
  115.3 26.1 %all-reduce.1 = (f32[2048]{0:T(1024)S(1)}, f32[2048]{0:T(1024)S(1)}) all-reduce(f32[2048]{0:T(1024)S(1)} %get-tuple-element.8, f32[2048]{0:T(1024)S(1)} %get-tuple-element.9), channel_id=1, replica_groups=mesh['section'=2,'dp'=16,'cls'=8] {'cls'}, use_global_device_ids=true, to_apply=%region_4.5 | all-reduce | flops 4096 | bytes 32768 | tf_op jit(solution)/shard_map/psum | solution.py:37
  141.4 60.6 %all-reduce = (f32[2048]{0:T(1024)S(1)}, f32[2048]{0:T(1024)S(1)}) all-reduce(f32[2048]{0:T(1024)S(1)} %get-tuple-element.6, f32[2048]{0:T(1024)S(1)} %get-tuple-element.7), channel_id=1, replica_groups=mesh['section'=2,'dp'=16,'cls'=8] {'dp'}, use_global_device_ids=true, to_apply=%region_5.6 | all-reduce | flops 4096 | bytes 32768 | tf_op jit(solution)/shard_map/psum | solution.py:37
  202.1 8.4 %subtract_multiply_fusion = f32[2048,512]{1,0:T(8,128)} fusion(bf16[1536,512]{1,0:T(8,128)(2,1)S(1)} %fusion.5, f32[2048,1536]{0,1:T(8,128)} %get-tuple-element.10, f32[2048]{0:T(1024)S(1)} %convert_element_type.32, bf16[2048,512]{1,0:T(8,128)(2,1)} %gather_fusion.1, f32[2048]{0:T(1024)S(1)} %get-tuple-element.4, pred[2048]{0:T(1024)(128)(4,1)S(1)} %compare_and_fusion), kind=kOutput, calls=%fused_computation.12 | convolution fusion | flops 3230662656 | bytes 20465664 | tf_op jit(solution)/shard_map/dot_general | solution.py:47
  210.4 0.0 reduce-scatter.4.cloned.1.call-update
  210.5 0.0 reduce-scatter.6.cloned.1.call-start
  210.5 31.3 %reduce-scatter.4.cloned.1.call-done = f32[1,16,8,8,512]{4,3,2,1,0:T(8,128)} async-done(((f32[2,16,8,8,512]{4,3,2,1,0:T(8,128)}), f32[1,16,8,8,512]{4,3,2,1,0:T(8,128)}) %reduce-scatter.4.cloned.1.call-update) | async-done | bytes 2097168 | tf_op jit(solution)/shard_map/reduce_scatter | solution.py:51
  241.8 0.0 reduce-scatter.6.cloned.1.call-update
  241.8 0.0 reduce-scatter.8.cloned.1.call-start
  241.9 208.4 %reduce-scatter.6.cloned.1.call-done = f32[1,8,8,512]{3,2,1,0:T(8,128)} async-done(((f32[16,8,8,512]{3,2,1,0:T(8,128)}), f32[1,8,8,512]{3,2,1,0:T(8,128)}) %reduce-scatter.6.cloned.1.call-update) | async-done | bytes 131088 | tf_op jit(solution)/shard_map/reduce_scatter | solution.py:51
  450.3 0.0 reduce-scatter.8.cloned.1.call-update
  450.3 0.1 dynamic_slice.10
  450.4 2.5 convert_element_type.26
  452.9 0.6 dynamic-slice_subtract_fusion
  453.5 36.7 %reduce-scatter.8.cloned.1.call-done = f32[1,8,512]{2,1,0:T(8,128)} async-done(((f32[8,8,512]{2,1,0:T(8,128)}), f32[1,8,512]{2,1,0:T(8,128)}) %reduce-scatter.8.cloned.1.call-update) | async-done | bytes 16400 | tf_op jit(solution)/shard_map/reduce_scatter | solution.py:51
  490.2 0.9 fusion.8
  491.2 1.4 fusion.9
  (11 shorter events, 0.1 us)
Async XLA Ops:
  7.2 88.9 %all-gather.3.cloned.1.call-start = ((), (), s32[]{:S(2)}) async-start(), calls=%async_computation.3 | async-start | bytes 2228224 | tf_op jit(solution)/shard_map/all_gather | solution.py:15
  7.9 233.9 %reduce-scatter.4.cloned.1.call-start = ((), (), s32[]{:S(2)}) async-start(), calls=%async_computation.4 | async-start | bytes 6291456 | tf_op jit(solution)/shard_map/reduce_scatter | solution.py:51
  210.4 239.9 %copy-start = (bf16[2048,512]{1,0:T(8,128)(2,1)S(1)}, bf16[2048,512]{1,0:T(8,128)(2,1)}, u32[]{:S(2)}) copy-start(bf16[2048,512]{1,0:T(8,128)(2,1)} %all-gather.3.cloned.1.call-done) | copy-start | bytes 6291460
  210.5 239.8 %reduce-scatter.6.cloned.1.call-start = ((), (), s32[]{:S(2)}) async-start(), calls=%async_computation.5 | async-start | bytes 2228224 | tf_op jit(solution)/shard_map/reduce_scatter | solution.py:51
  241.8 248.4 %reduce-scatter.8.cloned.1.call-start = ((), (), s32[]{:S(2)}) async-start(), calls=%async_computation.6 | async-start | bytes 147456 | tf_op jit(solution)/shard_map/reduce_scatter | solution.py:51
Sparse Core Ops, SparseCore 0:
  10.6 85.4 all-gather.2
  210.6 31.1 reduce-scatter.3
  245.7 204.5 reduce-scatter.5
  452.6 37.5 reduce-scatter.7

commit v2 on v0

--- a/solution.py
+++ b/solution.py
@@ -6,6 +6,17 @@
 LOGIT_SCALE = 64.0
 MARGIN = 0.35
 EPSILON = 1e-06
+EXTRA = 128
+
+
+def reduce_chain(payload, section_count, batch_count, class_count):
+    rows_here, width = payload.shape[1], payload.shape[2]
+    blocks = payload.reshape(section_count, batch_count, class_count, rows_here, width)
+    blocks = blocks.transpose(0, 2, 1, 3, 4)
+    blocks = lax.all_to_all(blocks, "section", 0, 0, tiled=False).sum(0)
+    blocks = lax.all_to_all(blocks, "cls", 0, 0, tiled=False).sum(0)
+    blocks = lax.all_to_all(blocks, "dp", 0, 0, tiled=False).sum(0)
+    return blocks
 
 
 def on_device(embeddings, centers, sample_ids, labels):
@@ -16,6 +27,7 @@
         lax.all_gather(labels, "dp", axis=0, tiled=True),
     )
     total_rows = gathered.shape[0]
+    width = gathered.shape[1]
     emb_float = gathered.astype(jnp.float32)
     row_norm = jnp.sqrt(jnp.sum(emb_float * emb_float, axis=1) + EPSILON)
     unit_rows = (emb_float / row_norm[:, None]).astype(jnp.bfloat16)
@@ -32,7 +44,6 @@
     exponent = jnp.exp(logits)
     total_part = jnp.sum(exponent, axis=1)
     target_part = jnp.sum(jnp.where(matches, logits, jnp.float32(0.0)), axis=1)
-    total, target = lax.psum((total_part, target_part), ("section", "dp", "cls"))
     weights = exponent.astype(jnp.bfloat16)
     column_ids = jnp.arange(local_ids.shape[0], dtype=jnp.int32)
     position = jnp.sum(jnp.where(matches, column_ids[None, :], 0), axis=1)
@@ -41,22 +52,51 @@
     section_count = lax.axis_size("section")
     batch_count = lax.axis_size("dp")
     class_count = lax.axis_size("cls")
-    rows_here = total_rows // (section_count * batch_count * class_count)
+    devices = section_count * batch_count * class_count
+    rows_here = total_rows // devices
+    rows_per_batch = total_rows // batch_count
+    assert rows_here >= 3 and rows_per_batch <= EXTRA and rows_here <= EXTRA
     unscaled = jnp.dot(weights, unit_centers, preferred_element_type=jnp.float32)
-    unit_grad = lax.psum_scatter(
-        LOGIT_SCALE * (unscaled / total[:, None] - own_center),
-        ("section", "dp", "cls"),
-        scatter_dimension=0,
-        tiled=True,
+
+    def block_of(values):
+        per_batch = values.reshape(batch_count, rows_per_batch)
+        per_batch = jnp.pad(per_batch, ((0, 0), (0, EXTRA - rows_per_batch)))
+        spread = jnp.broadcast_to(
+            per_batch[None, :, None, :], (section_count, batch_count, class_count, EXTRA)
+        )
+        return spread.reshape(devices, 1, EXTRA)
+
+    own_totals = jnp.pad(total_part.reshape(devices, 1, rows_here), ((0, 0), (0, 0), (0, EXTRA - rows_here)))
+    extra = jnp.concatenate(
+        [
+            block_of(total_part),
+            block_of(target_part),
+            own_totals,
+            jnp.zeros((devices, rows_here - 3, EXTRA), jnp.float32),
+        ],
+        axis=1,
     )
+    payload = jnp.concatenate(
+        [
+            unscaled.reshape(devices, rows_here, width),
+            own_center.reshape(devices, rows_here, width),
+            extra,
+        ],
+        axis=2,
+    )
+    summed = reduce_chain(payload, section_count, batch_count, class_count)
+    unscaled_rows = summed[:, :width]
+    own_rows = summed[:, width : 2 * width]
+    total_rows_here = summed[2, 2 * width : 2 * width + rows_here]
+    unit_grad = LOGIT_SCALE * (unscaled_rows / total_rows_here[:, None] - own_rows)
     emb_rows = lax.dynamic_slice_in_dim(emb_float, shard_index * rows_here, rows_here, 0)
     norm_rows = lax.dynamic_slice_in_dim(row_norm, shard_index * rows_here, rows_here, 0)
     unit_float = emb_rows / norm_rows[:, None]
     along = jnp.sum(unit_float * unit_grad, axis=1, keepdims=True)
     feature_grad = (unit_grad - unit_float * along) / norm_rows[:, None]
-    loss_all = jnp.log(total) - target
-    own_rows = embeddings.shape[0]
-    row_loss = lax.dynamic_slice_in_dim(loss_all, lax.axis_index("dp") * own_rows, own_rows, 0)
+    batch_total = summed[0, 2 * width : 2 * width + rows_per_batch]
+    batch_target = summed[1, 2 * width : 2 * width + rows_per_batch]
+    row_loss = jnp.log(batch_total) - batch_target
     return (feature_grad, row_loss)
 
 

time: 1520 us -> 236 us (0.16)
  waiting for transfers between devices: 1340 us -> 36.4 us
  other arithmetic: 13.9 us -> 32.3 us
    reduce_scatter x1 -> x0, waiting for transfers between devices: 1310 us -> none  [on_device(): lax.psum_scatter(LOGIT_SCALE * (unscaled / total[:, None] - own_center),...]
    psum x1 -> x0, blocking collectives: 78.5 us -> none  [on_device(): lax.psum((total_part, target_part), ('section', 'dp', 'cls'))]
    all_to_all x0 -> x2, blocking collectives: none -> 74.3 us  [the longest x1 57.6 us: reduce_chain(): blocks = lax.all_to_all(blocks, 'cls', 0, 0, tiled=False).sum(0)]
  transfers between devices with their start and end apart: 2 -> 2, of which waited for: 2 -> 2; matrix products, arithmetic and copies ran while one was open for 2% -> 13% of each run, Pallas kernels for 0% -> 0%
where the time goes in v2:
time: 236 us; the launch traced here: 233 us
  blocking collectives  112 us (47%)
  waiting for transfers between devices  36.4 us (15%)
  other arithmetic  32.3 us (14%)
  local copies, waits for them, and re-layouts  20.1 us (9%)
  between operations  14.2 us (6%)
  matrix products  12.1 us (5%)
  starting transfers between devices  5.62 us (2%)
    all_to_all x1, blocking collectives, reduce_chain(): blocks = lax.all_to_all(blocks, 'cls', 0, 0, tiled=False).sum(0)  57.6 us
    all_gather x1, blocking collectives, on_device(): lax.all_gather(labels, 'dp', axis=0, tiled=True)  37.8 us
    all_gather x1, waiting for transfers between devices, on_device(): lax.all_gather(embeddings, 'dp', axis=0, tiled=True)  23.2 us
    all_to_all x1, blocking collectives, reduce_chain(): blocks = lax.all_to_all(blocks, 'section', 0, 0, tiled=False).sum(0)  16.7 us
    all_to_all x1, waiting for transfers between devices, reduce_chain(): blocks = lax.all_to_all(blocks, 'dp', 0, 0, tiled=False).sum(0)  12.6 us
    gather x1, local copies, waits for them, and re-layouts, on_device(): jnp.take(unit_centers, position, axis=0).astype(jnp.float32)  9.18 us
    gather x1, local copies, waits for them, and re-layouts, on_device(): chosen = jnp.take(centers, local_ids, axis=0).astype(jnp.float32)  7.77 us
    reduce_sum x1, other arithmetic, reduce_chain(): blocks = lax.all_to_all(blocks, 'section', 0, 0, tiled=False).sum(0)  7.08 us
  transfers between devices with their start and end apart: 2, of which 2 were waited for; matrix products, arithmetic and copies ran while one was open for 13% of the time, Pallas kernels for 0%

profile of v2, /device:TPU:1, one launch (start us, length us, event | category | flops | bytes accessed | tf_op | source)
XLA Modules:
  0.0 232.8 jit_solution(7231302334245475391)
XLA Ops:
  7.2 0.7 all-gather.3.cloned.1.call-update
  7.9 0.7 reduce
  8.6 37.8 %all-gather = s32[16,1,128]{2,1,0:T(1,128)S(1)} all-gather(s32[1,1,128]{2,1,0:T(1,128)} %bitcast.34), channel_id=1, replica_groups=mesh['section'=2,'dp'=16,'cls'=8] {'dp'}, dimensions={0}, use_global_device_ids=true | all-gather | bytes 8704 | tf_op jit(solution)/shard_map/all_gather | solution.py:27
  46.4 1.3 fusion.1
  47.7 0.1 reduce_sum.88
  47.9 1.7 compare_reduce_fusion
  49.6 0.1 reshape.115
  49.7 0.7 fusion.9
  50.4 7.8 %gather_fusion = bf16[1536,512]{1,0:T(8,128)(2,1)S(1)} fusion(bf16[4096,512]{1,0:T(8,128)(2,1)} %param.5, s32[2048]{0:T(1024)S(1)} %pad_clamp_fusion), kind=kCustom, calls=%fused_computation | custom fusion | bytes 3151872 | tf_op jit(solution)/shard_map/jit(_take)/gather | solution.py:35
  58.2 0.8 fusion.4
  59.0 1.1 fusion.5
  60.1 9.2 %gather_fusion.1 = bf16[2048,512]{1,0:T(8,128)(2,1)} fusion(bf16[1536,512]{1,0:T(8,128)(2,1)S(1)} %fusion.5, s32[2048]{0:T(1024)S(1)} %broadcast_clamp_fusion), kind=kCustom, calls=%fused_computation.1 | custom fusion | bytes 4202496 | tf_op jit(solution)/shard_map/jit(_take)/gather | solution.py:51
  69.4 3.5 %convert_multiply_fusion = f32[2,16,8,8,512]{4,3,2,1,0:T(8,128)} fusion(f32[2,16,8,8]{3,2,1,0:T(8,128)S(1)} %reshape.115, bf16[2,16,8,8,512]{4,3,2,1,0:T(8,128)(2,1)} %bitcast.23, pred[2,16,8,8]{3,2,1,0:T(8,128)(4,1)S(1)} %compare_and_fusion), kind=kLoop, calls=%fused_computation.13 | loop fusion | flops 3145728 | bytes 6301696 | tf_op jit(solution)/shard_map/mul | solution.py:51
  72.9 23.2 %all-gather.3.cloned.1.call-done = bf16[2048,512]{1,0:T(8,128)(2,1)} async-done(((bf16[128,512]{1,0:T(8,128)(2,1)}), bf16[2048,512]{1,0:T(8,128)(2,1)}) %all-gather.3.cloned.1.call-update) | async-done | bytes 2097168 | tf_op jit(solution)/shard_map/all_gather | solution.py:26
  96.1 2.1 multiply_reduce_fusion
  98.2 7.0 %fusion.2 = (f32[2048]{0:T(1024)S(1)}, f32[2048]{0:T(1024)S(1)}, f32[2048,1536]{0,1:T(8,128)S(1)}) fusion(s32[2048]{0:T(1024)S(1)} %bitcast.33, s32[1536]{0:T(1024)S(1)} %reduce, bf16[1536,512]{1,0:T(8,128)(2,1)S(1)} %fusion.5, f32[2048]{0:T(1024)S(1)} %add_sqrt_fusion.1, bf16[2048,512]{1,0:T(8,128)(2,1)} %all-gather.3.cloned.1.call-done), kind=kOutput, calls=%fused_computation.8 | convolution fusion | flops 3246387200 | bytes 16291840 | tf_op jit(solution)/shard_map/dot_general | solution.py:38
  105.2 5.0 %fusion.3 = f32[2048,512]{1,0:T(8,128)} fusion(bf16[1536,512]{1,0:T(8,128)(2,1)S(1)} %fusion.5, f32[2048,1536]{0,1:T(8,128)S(1)} %get-tuple-element.4), kind=kOutput, calls=%fused_computation.12 | convolution fusion | flops 3224371200 | bytes 18350080 | tf_op jit(solution)/shard_map/dot_general | solution.py:59
  110.2 0.1 reshape.114
  110.4 0.1 concatenate.17
  110.5 4.2 %maximum_bitcast_fusion = f32[2,8,16,8,1152]{4,3,1,2,0:T(8,128)S(1)} fusion(f32[2,16,8,1,128]{4,3,2,1,0:T(1,128)S(1)} %bitcast.25, f32[2,16,8,1,128]{4,3,2,1,0:T(1,128)S(1)} %concatenate.18, f32[2,16,8,1,128]{4,3,2,1,0:T(1,128)S(1)} %concatenate.17, f32[2,16,8,8,512]{4,3,2,1,0:T(8,128)} %convert_multiply_fusion, f32[2,16,8,8,512]{4,3,2,1,0:T(8,128)} %bitcast.24, ...), kind=kLoop, calls=%fused_computation.11 | loop fusion | flops 11796480 | bytes 18255872 | tf_op jit(solution)/shard_map/transpose | solution.py:15
  114.7 16.7 %all_to_all.15 = f32[2,8,16,8,1152]{4,3,1,2,0:T(8,128)} all-to-all(f32[2,8,16,8,1152]{4,3,1,2,0:T(8,128)S(1)} %maximum_bitcast_fusion), channel_id=1, replica_groups=mesh['section'=2,'dp'=16,'cls'=8] {'section'}, dimensions={0} | all-to-all | bytes 18874368 | tf_op jit(solution)/shard_map/all_to_all | solution.py:16
  131.4 7.1 %reduce_sum.92 = f32[8,16,8,1152]{3,2,0,1:T(8,128)} reduce(f32[2,8,16,8,1152]{4,3,1,2,0:T(8,128)} %all_to_all.15, f32[]{:T(128)} %constant.19.clone.1), dimensions={0}, to_apply=%region_6.7 | reduce | flops 1179648 | bytes 14155780 | tf_op jit(solution)/shard_map/reduce_sum | solution.py:16
  138.5 2.6 %copy.11 = f32[8,16,8,1152]{3,2,1,0:T(8,128)S(1)} copy(f32[8,16,8,1152]{3,2,0,1:T(8,128)} %reduce_sum.92) | data formatting | bytes 9437184 | tf_op jit(solution)/shard_map/reduce_sum | solution.py:16
  141.2 57.6 %all_to_all.16 = f32[8,16,8,1152]{3,2,1,0:T(8,128)} all-to-all(f32[8,16,8,1152]{3,2,1,0:T(8,128)S(1)} %copy.11), channel_id=1, replica_groups=mesh['section'=2,'dp'=16,'cls'=8] {'cls'}, dimensions={0} | all-to-all | bytes 9437184 | tf_op jit(solution)/shard_map/all_to_all | solution.py:17
  198.7 3.6 %reduce_sum.93 = f32[16,8,1152]{2,1,0:T(8,128)} reduce(f32[8,16,8,1152]{3,2,1,0:T(8,128)} %all_to_all.16, f32[]{:T(128)} %constant.19.clone.1), dimensions={0}, to_apply=%region_7.8 | reduce | flops 1032192 | bytes 5308420 | tf_op jit(solution)/shard_map/reduce_sum | solution.py:17
  202.3 5.6 %all-to-all-start.2 = ((f32[16,8,1152]{2,1,0:T(8,128)}), f32[16,8,1152]{2,1,0:T(8,128)S(1)}, u32[]{:S(2)}, u32[]{:S(2)}) async-start(f32[16,8,1152]{2,1,0:T(8,128)} %reduce_sum.93), calls=%async_computation.2 | async-start | bytes 1179648 | tf_op jit(solution)/shard_map/all_to_all | solution.py:18
  207.9 0.1 dynamic_slice.7
  208.0 2.5 %convert_element_type.33 = f32[2048,512]{1,0:T(8,128)} convert(bf16[2048,512]{1,0:T(8,128)(2,1)S(1)} %copy-done) | non-fusion elementwise | flops 1048576 | bytes 6291456 | tf_op jit(solution)/shard_map/convert_element_type | solution.py:31
  210.5 12.6 %all-to-all-done.2 = f32[16,8,1152]{2,1,0:T(8,128)S(1)} async-done(((f32[16,8,1152]{2,1,0:T(8,128)}), f32[16,8,1152]{2,1,0:T(8,128)S(1)}, u32[]{:S(2)}, u32[]{:S(2)}) %all-to-all-start.2) | async-done | bytes 589856 | tf_op jit(solution)/shard_map/all_to_all | solution.py:18
  223.1 0.5 fusion.10
  223.7 0.9 multiply_reduce_fusion.1
  224.6 1.4 subtract_divide_fusion
  (18 shorter events, 0.3 us)
Async XLA Ops:
  7.2 88.9 %all-gather.3.cloned.1.call-start = ((), (), s32[]{:S(2)}) async-start(), calls=%async_computation.3 | async-start | bytes 2228224 | tf_op jit(solution)/shard_map/all_gather | solution.py:26
  198.7 9.3 %copy-start = (bf16[2048,512]{1,0:T(8,128)(2,1)S(1)}, bf16[2048,512]{1,0:T(8,128)(2,1)}, u32[]{:S(2)}) copy-start(bf16[2048,512]{1,0:T(8,128)(2,1)} %all-gather.3.cloned.1.call-done) | copy-start | bytes 6291460
  202.3 20.8 %all-to-all-start.2 = ((f32[16,8,1152]{2,1,0:T(8,128)}), f32[16,8,1152]{2,1,0:T(8,128)S(1)}, u32[]{:S(2)}, u32[]{:S(2)}) async-start(f32[16,8,1152]{2,1,0:T(8,128)} %reduce_sum.93), calls=%async_computation.2 | async-start | bytes 1179648 | tf_op jit(solution)/shard_map/all_to_all | solution.py:18
Sparse Core Ops, SparseCore 0:
  10.6 85.4 all-gather.2

commit v3 on v0

v3 whole, which is shorter than its diff:
```python
import jax
import jax.numpy as jnp
from jax import lax
from jax.sharding import PartitionSpec as P

LOGIT_SCALE = 64.0
MARGIN = 0.35
EPSILON = 1e-06
EXTRA = 128


def on_device(embeddings, centers, sample_ids, labels):
    section_count = lax.axis_size("section")
    batch_count = lax.axis_size("dp")
    class_count = lax.axis_size("cls")
    assert section_count == 2
    section = lax.axis_index("section")
    batch = lax.axis_index("dp")
    shard_index = lax.axis_index(("section", "dp", "cls"))
    swap = [(0, 1), (1, 0)]
    per_shard = centers.shape[0]
    width = embeddings.shape[1]

    gathered = lax.all_gather(embeddings, "dp", axis=0, tiled=True)
    label_all = lax.all_to_all(
        jnp.broadcast_to(labels[None], (batch_count,) + labels.shape), "dp", 0, 0, tiled=False
    ).reshape(-1)
    total_rows = gathered.shape[0]
    devices = section_count * batch_count * class_count
    rows_here = total_rows // devices
    rows_section = total_rows // section_count
    rows_per_batch = total_rows // batch_count
    batches_per_section = batch_count // section_count
    assert rows_here >= 3 and rows_per_batch <= EXTRA and rows_here <= EXTRA

    local_ids = sample_ids[0]
    chosen = jnp.take(centers, local_ids, axis=0).astype(jnp.float32)
    center_norm = jnp.sqrt(jnp.sum(chosen * chosen, axis=1) + EPSILON)
    unit_centers = (chosen / center_norm[:, None]).astype(jnp.bfloat16)
    global_ids = local_ids + shard_index * per_shard
    partner_centers = lax.ppermute(unit_centers, "section", swap)
    partner_ids = lax.ppermute(global_ids, "section", swap)
    both_centers = jnp.concatenate([unit_centers, partner_centers], axis=0)
    both_ids = jnp.concatenate([global_ids, partner_ids], axis=0)

    section_rows = lax.dynamic_slice_in_dim(gathered, section * rows_section, rows_section, 0)
    section_labels = lax.dynamic_slice_in_dim(label_all, section * rows_section, rows_section, 0)
    emb_float = section_rows.astype(jnp.float32)
    row_norm = jnp.sqrt(jnp.sum(emb_float * emb_float, axis=1) + EPSILON)
    unit_rows = (emb_float / row_norm[:, None]).astype(jnp.bfloat16)

    cosine = lax.dot_general(
        unit_rows, both_centers, (((1,), (1,)), ((), ())), preferred_element_type=jnp.float32
    )
    matches = both_ids[None, :] == section_labels[:, None]
    logits = LOGIT_SCALE * cosine - LOGIT_SCALE * MARGIN * matches.astype(jnp.float32)
    exponent = jnp.exp(logits)
    total_part = jnp.sum(exponent, axis=1)
    target_part = jnp.sum(jnp.where(matches, logits, jnp.float32(0.0)), axis=1)
    weights = exponent.astype(jnp.bfloat16)
    unscaled = jnp.dot(weights, both_centers, preferred_element_type=jnp.float32)
    own_center = jnp.dot(matches.astype(jnp.bfloat16), both_centers, preferred_element_type=jnp.float32)

    def block_of(values):
        blocks = values.reshape(1, batches_per_section, rows_per_batch)
        mine = jnp.arange(section_count, dtype=jnp.int32)[:, None, None] == section
        blocks = jnp.where(mine, blocks, jnp.float32(0.0)).reshape(batch_count, rows_per_batch)
        blocks = jnp.pad(blocks, ((0, 0), (0, EXTRA - rows_per_batch)))
        spread = jnp.broadcast_to(blocks[:, None, :], (batch_count, class_count, EXTRA))
        return spread.reshape(batch_count * class_count, 1, EXTRA)

    dests = batch_count * class_count
    own_totals = jnp.pad(total_part.reshape(dests, 1, rows_here), ((0, 0), (0, 0), (0, EXTRA - rows_here)))
    extra = jnp.concatenate(
        [
            block_of(total_part),
            block_of(target_part),
            own_totals,
            jnp.zeros((dests, rows_here - 3, EXTRA), jnp.float32),
        ],
        axis=1,
    )
    payload = jnp.concatenate(
        [unscaled.reshape(dests, rows_here, width), own_center.reshape(dests, rows_here, width), extra],
        axis=2,
    )
    payload = payload.reshape(batch_count, class_count, rows_here, payload.shape[-1]).transpose(1, 0, 2, 3)
    payload = lax.all_to_all(payload, "cls", 0, 0, tiled=False).sum(0)
    summed = lax.all_to_all(payload, "dp", 0, 0, tiled=False).sum(0)

    block_total = summed[0, 2 * width : 2 * width + rows_per_batch]
    block_target = summed[1, 2 * width : 2 * width + rows_per_batch]
    other_total, other_target = lax.ppermute((block_total, block_target), "section", swap)
    have = batch // batches_per_section == section
    block_total = jnp.where(have, block_total, other_total)
    block_target = jnp.where(have, block_target, other_target)
    row_loss = jnp.log(block_total) - block_target

    unscaled_rows = summed[:, :width]
    own_rows = summed[:, width : 2 * width]
    totals_here = summed[2, 2 * width : 2 * width + rows_here]
    unit_grad = LOGIT_SCALE * (unscaled_rows / totals_here[:, None] - own_rows)
    offset = (shard_index % dests) * rows_here
    emb_rows = lax.dynamic_slice_in_dim(emb_float, offset, rows_here, 0)
    norm_rows = lax.dynamic_slice_in_dim(row_norm, offset, rows_here, 0)
    unit_float = emb_rows / norm_rows[:, None]
    along = jnp.sum(unit_float * unit_grad, axis=1, keepdims=True)
    feature_grad = (unit_grad - unit_float * along) / norm_rows[:, None]
    return (feature_grad, row_loss)


def solution(mesh):
    return jax.shard_map(
        on_device,
        mesh=mesh,
        in_specs=(
            P("dp", None),
            P(("section", "dp", "cls"), None),
            P(("section", "dp", "cls"), None),
            P("dp"),
        ),
        out_specs=(P(("section", "dp", "cls"), None), P("dp")),
        check_vma=False,
    )
```

time: 1520 us -> 208 us (0.14)
  waiting for transfers between devices: 1340 us -> 70.2 us
  blocking collectives: 116 us -> 53.9 us
  starting transfers between devices: 0.08 us -> 25.4 us
    reduce_scatter x1 -> x0, waiting for transfers between devices: 1310 us -> none  [on_device(): lax.psum_scatter(LOGIT_SCALE * (unscaled / total[:, None] - own_center),...]
    psum x1 -> x0, blocking collectives: 78.5 us -> none  [on_device(): lax.psum((total_part, target_part), ('section', 'dp', 'cls'))]
    all_to_all x0 -> x1, blocking collectives: none -> 53.9 us  [on_device(): payload = lax.all_to_all(payload, 'cls', 0, 0, tiled=False).sum(0)]
    all_gather x1 -> x0, blocking collectives: 37.8 us -> none  [on_device(): lax.all_gather(labels, 'dp', axis=0, tiled=True)]
    all_gather x1, waiting for transfers between devices: 27.1 us -> 49.8 us  [on_device(): gathered = lax.all_gather(embeddings, 'dp', axis=0, tiled=True)]
    all_to_all x0 -> x2, waiting for transfers between devices: none -> 19.5 us  [the longest x1 11 us: on_device(): summed = lax.all_to_all(payload, 'dp', 0, 0, tiled=False).sum(0)]
  transfers between devices with their start and end apart: 2 -> 7, of which waited for: 2 -> 4; matrix products, arithmetic and copies ran while one was open for 2% -> 9% of each run, Pallas kernels for 0% -> 0%
where the time goes in v3:
time: 208 us
  waiting for transfers between devices  70.2 us (34%)
  blocking collectives  53.9 us (26%)
  starting transfers between devices  25.4 us (12%)
  matrix products  23.2 us (11%)
  between operations  14.3 us (7%)
  other arithmetic  12 us (6%)
  local copies, waits for them, and re-layouts  8.69 us (4%)
    all_to_all x1, blocking collectives, on_device(): payload = lax.all_to_all(payload, 'cls', 0, 0, tiled=False).sum(0)  53.9 us
    all_gather x1, waiting for transfers between devices, on_device(): gathered = lax.all_gather(embeddings, 'dp', axis=0, tiled=True)  49.8 us
    all_to_all x1, waiting for transfers between devices, on_device(): summed = lax.all_to_all(payload, 'dp', 0, 0, tiled=False).sum(0)  11 us
    dot_general x1, matrix products, on_device(): lax.dot_general(unit_rows, both_centers, (((1,), (1,)), ((), ())), prefer...  10.3 us
    all_to_all x1, starting transfers between devices, on_device(): lax.all_to_all(jnp.broadcast_to(labels[None], (batch_count,) + labels.sha...  9.22 us
    all_to_all x1, waiting for transfers between devices, on_device(): lax.all_to_all(jnp.broadcast_to(labels[None], (batch_count,) + labels.sha...  8.54 us
    gather x1, local copies, waits for them, and re-layouts, on_device(): chosen = jnp.take(centers, local_ids, axis=0).astype(jnp.float32)  7.59 us
    dot_general x1, matrix products, on_device(): jnp.dot(weights, both_centers, preferred_element_type=jnp.float32)  7.54 us
  transfers between devices with their start and end apart: 7, of which 4 were waited for; matrix products, arithmetic and copies ran while one was open for 9% of the time, Pallas kernels for 0%

profile of v3, /device:TPU:1, one launch (start us, length us, event | category | flops | bytes accessed | tf_op | source)
XLA Modules:
  0.0 207.6 jit_solution(15268252438203017896)
XLA Ops:
  7.2 0.7 all-gather.2.cloned.1.call-update
  7.9 0.7 reduce
  8.6 0.7 fusion.15
  9.3 7.6 %gather_fusion = bf16[1536,512]{1,0:T(8,128)(2,1)S(1)} fusion(bf16[4096,512]{1,0:T(8,128)(2,1)} %param.5, s32[2048]{0:T(1024)S(1)} %pad_clamp_fusion), kind=kCustom, calls=%fused_computation | custom fusion | bytes 3151872 | tf_op jit(solution)/shard_map/jit(_take)/gather | solution.py:37
  17.0 0.8 fusion.8
  17.7 1.1 fusion.9
  18.9 3.3 %collective-permute-start = (bf16[1536,512]{1,0:T(8,128)(2,1)S(1)}, bf16[1536,512]{1,0:T(8,128)(2,1)}, u32[]{:S(2)}, u32[]{:S(2)}) collective-permute-start(bf16[1536,512]{1,0:T(8,128)(2,1)S(1)} %fusion.9), channel_id=1, source_target_pairs={{0,128},{128,0},{1,129},{129,1},{2,130},{130,2},{3,131},{131,3},{4... | collective-permute-start | bytes 4718600 | tf_op jit(solution)/shard_map/ppermute | solution.py:41
  22.2 0.1 collective-permute-start.1
  22.3 0.6 broadcast_in_dim.81
  22.9 9.2 %all-to-all-start = ((s32[16,1,128]{2,1,0:T(1,128)}), s32[16,1,128]{2,1,0:T(1,128)S(1)}, u32[]{:S(2)}, u32[]{:S(2)}) async-start(s32[16,1,128]{2,1,0:T(1,128)} %broadcast_in_dim.81), calls=%async_computation | async-start | bytes 16384 | tf_op jit(solution)/shard_map/all_to_all | solution.py:25
  32.2 0.1 broadcast_in_dim.83
  32.4 8.5 %all-to-all-done = s32[16,1,128]{2,1,0:T(1,128)S(1)} async-done(((s32[16,1,128]{2,1,0:T(1,128)}), s32[16,1,128]{2,1,0:T(1,128)S(1)}, u32[]{:S(2)}, u32[]{:S(2)}) %all-to-all-start) | async-done | bytes 8224 | tf_op jit(solution)/shard_map/all_to_all | solution.py:25
  40.9 5.3 %fusion = f32[1024,512]{1,0:T(8,128)S(1)} fusion(s32[3072]{0:T(1024)S(1)} %pad_add_fusion, s32[1024]{0:T(1024)S(1)} %dynamic_slice.13, bf16[1536,512]{1,0:T(8,128)(2,1)} %collective-permute-done, bf16[1536,512]{1,0:T(8,128)(2,1)} %copy-done), kind=kOutput, calls=%fused_computation.2 | convolution fusion | flops 3230662656 | bytes 5259264 | tf_op jit(solution)/shard_map/dot_general | solution.py:62
  46.3 49.8 %all-gather.2.cloned.1.call-done = bf16[2048,512]{1,0:T(8,128)(2,1)} async-done(((bf16[128,512]{1,0:T(8,128)(2,1)}), bf16[2048,512]{1,0:T(8,128)(2,1)}) %all-gather.2.cloned.1.call-update) | async-done | bytes 2097168 | tf_op jit(solution)/shard_map/all_gather | solution.py:24
  96.1 1.5 multiply_reduce_fusion
  97.6 10.3 %fusion.3 = (f32[1024]{0:T(1024)S(1)}, f32[1024]{0:T(1024)S(1)}, f32[1024,3072]{1,0:T(8,128)}) fusion(s32[3072]{0:T(1024)S(1)} %pad_add_fusion, s32[1024]{0:T(1024)S(1)} %dynamic_slice.13, bf16[1536,512]{1,0:T(8,128)(2,1)} %collective-permute-done, bf16[1536,512]{1,0:T(8,128)(2,1)} %copy-done, f32[1024]{0:T(1024)S(1)} %add_sqrt_fusion.1, ...), kind=kOutput, calls=%fused_computation.6 | convolution fusion | flops 3251107840 | bytes 16805892 | tf_op jit(solution)/shard_map/dot_general | solution.py:52
  107.9 0.1 reshape.122
  108.1 0.1 bitcast_select_fusion.1
  108.1 7.5 %fusion.5 = f32[1024,512]{1,0:T(8,128)S(1)} fusion(f32[1024,3072]{1,0:T(8,128)} %get-tuple-element.8, s32[3072]{0:T(1024)S(1)} %pad_add_fusion, s32[1024]{0:T(1024)S(1)} %dynamic_slice.13, bf16[1536,512]{1,0:T(8,128)(2,1)} %collective-permute-done, bf16[1536,512]{1,0:T(8,128)(2,1)} %copy-done), kind=kOutput, calls=%fused_computation.10 | convolution fusion | flops 3243245568 | bytes 17842176 | tf_op jit(solution)/shard_map/dot_general | solution.py:61
  115.8 0.6 maximum_bitcast_fusion
  116.4 53.9 %all_to_all.16 = f32[8,16,8,1152]{3,2,1,0:T(8,128)} all-to-all(f32[8,16,8,1152]{3,2,1,0:T(8,128)S(1)} %maximum_bitcast_fusion), channel_id=1, replica_groups=mesh['section'=2,'dp'=16,'cls'=8] {'cls'}, dimensions={0} | all-to-all | bytes 9437184 | tf_op jit(solution)/shard_map/all_to_all | solution.py:88
  170.3 3.5 %reduce_sum.67 = f32[16,8,1152]{2,1,0:T(8,128)} reduce(f32[8,16,8,1152]{3,2,1,0:T(8,128)} %all_to_all.16, f32[]{:T(128)} %constant.61.clone.1), dimensions={0}, to_apply=%region_4.5 | reduce | flops 1032192 | bytes 5308420 | tf_op jit(solution)/shard_map/reduce_sum | solution.py:88
  173.8 5.5 %all-to-all-start.2 = ((f32[16,8,1152]{2,1,0:T(8,128)}), f32[16,8,1152]{2,1,0:T(8,128)S(1)}, u32[]{:S(2)}, u32[]{:S(2)}) async-start(f32[16,8,1152]{2,1,0:T(8,128)} %reduce_sum.67), calls=%async_computation.2 | async-start | bytes 1179648 | tf_op jit(solution)/shard_map/all_to_all | solution.py:89
  179.4 0.1 dynamic_slice.15
  179.5 1.5 dynamic-slice_convert_fusion
  181.0 11.0 %all-to-all-done.2 = f32[16,8,1152]{2,1,0:T(8,128)S(1)} async-done(((f32[16,8,1152]{2,1,0:T(8,128)}), f32[16,8,1152]{2,1,0:T(8,128)S(1)}, u32[]{:S(2)}, u32[]{:S(2)}) %all-to-all-start.2) | async-done | bytes 589856 | tf_op jit(solution)/shard_map/all_to_all | solution.py:89
  192.0 7.1 %collective-permute-start.2 = (f32[128]{0:T(128)S(1)}, f32[128]{0:T(128)S(1)}, u32[]{:S(2)}, u32[]{:S(2)}) collective-permute-start(f32[128]{0:T(128)S(1)} %get-tuple-element.5), channel_id=1, source_target_pairs={{0,128},{128,0},{1,129},{129,1},{2,130},{130,2},{3,131},{131,3},{4... | collective-permute-start | bytes 1544 | tf_op jit(solution)/shard_map/ppermute | solution.py:93
  199.1 0.1 collective-permute-start.3
  199.2 0.2 multiply_reduce_fusion.1
  199.3 0.7 subtract_divide_fusion
  200.0 0.2 collective-permute-done.3
  200.2 0.5 fusion.17
  (26 shorter events, 0.4 us)
Async XLA Ops:
  7.2 88.9 %all-gather.2.cloned.1.call-start = ((), (), s32[]{:S(2)}) async-start(), calls=%async_computation.3 | async-start | bytes 2228224 | tf_op jit(solution)/shard_map/all_gather | solution.py:24
  16.9 5.4 %copy-start.1 = (s32[128]{0:T(128)S(1)}, s32[128]{0:T(128)}, u32[]{:S(2)}) copy-start(s32[128]{0:T(128)} %param.7) | copy-start | bytes 1540
  18.9 22.0 %copy-start = (bf16[1536,512]{1,0:T(8,128)(2,1)}, bf16[1536,512]{1,0:T(8,128)(2,1)S(1)}, u32[]{:S(2)}) copy-start(bf16[1536,512]{1,0:T(8,128)(2,1)S(1)} %fusion.9) | copy-start | bytes 4718596
  18.9 22.0 %collective-permute-start = (bf16[1536,512]{1,0:T(8,128)(2,1)S(1)}, bf16[1536,512]{1,0:T(8,128)(2,1)}, u32[]{:S(2)}, u32[]{:S(2)}) collective-permute-start(bf16[1536,512]{1,0:T(8,128)(2,1)S(1)} %fusion.9), channel_id=1, source_target_pairs={{0,128},{128,0},{1,129},{129,1},{2,130},{130,2},{3,131},{131,3},{4... | collective-permute-start | bytes 4718600 | tf_op jit(solution)/shard_map/ppermute | solution.py:41
  22.2 10.2 %collective-permute-start.1 = (s32[1536]{0:T(1024)S(1)}, s32[1536]{0:T(1024)S(1)}, u32[]{:S(2)}, u32[]{:S(2)}) collective-permute-start(s32[1536]{0:T(1024)S(1)} %broadcast_add_fusion), channel_id=1, source_target_pairs={{0,128},{128,0},{1,129},{129,1},{2,130},{130,2},{3,131},{131,3},{4... | collective-permute-start | bytes 18440 | tf_op jit(solution)/shard_map/ppermute | solution.py:42
  22.9 18.0 %all-to-all-start = ((s32[16,1,128]{2,1,0:T(1,128)}), s32[16,1,128]{2,1,0:T(1,128)S(1)}, u32[]{:S(2)}, u32[]{:S(2)}) async-start(s32[16,1,128]{2,1,0:T(1,128)} %broadcast_in_dim.81), calls=%async_computation | async-start | bytes 16384 | tf_op jit(solution)/shard_map/all_to_all | solution.py:25
  173.8 18.1 %all-to-all-start.2 = ((f32[16,8,1152]{2,1,0:T(8,128)}), f32[16,8,1152]{2,1,0:T(8,128)S(1)}, u32[]{:S(2)}, u32[]{:S(2)}) async-start(f32[16,8,1152]{2,1,0:T(8,128)} %reduce_sum.67), calls=%async_computation.2 | async-start | bytes 1179648 | tf_op jit(solution)/shard_map/all_to_all | solution.py:89
  192.0 8.1 %collective-permute-start.2 = (f32[128]{0:T(128)S(1)}, f32[128]{0:T(128)S(1)}, u32[]{:S(2)}, u32[]{:S(2)}) collective-permute-start(f32[128]{0:T(128)S(1)} %get-tuple-element.5), channel_id=1, source_target_pairs={{0,128},{128,0},{1,129},{129,1},{2,130},{130,2},{3,131},{131,3},{4... | collective-permute-start | bytes 1544 | tf_op jit(solution)/shard_map/ppermute | solution.py:93
  199.1 1.2 collective-permute-start.3
Sparse Core Ops, SparseCore 0:
  10.6 85.4 all-gather.1

commit v4 on v3

v4 whole, which is shorter than its diff:
```python
import jax
import jax.numpy as jnp
from jax import lax
from jax.sharding import PartitionSpec as P

LOGIT_SCALE = 64.0
MARGIN = 0.35
EPSILON = 1e-06
EXTRA = 128


def on_device(embeddings, centers, sample_ids, labels):
    section_count = lax.axis_size("section")
    batch_count = lax.axis_size("dp")
    class_count = lax.axis_size("cls")
    assert section_count == 2 and batch_count % 2 == 0
    section = lax.axis_index("section")
    batch = lax.axis_index("dp")
    cls = lax.axis_index("cls")
    shard_index = lax.axis_index(("section", "dp", "cls"))
    swap = [(0, 1), (1, 0)]
    per_shard = centers.shape[0]
    width = embeddings.shape[1]
    rows_per_batch = embeddings.shape[0]
    half = rows_per_batch // section_count
    devices = section_count * batch_count * class_count
    rows_here = rows_per_batch * batch_count // devices
    assert half == class_count * rows_here and rows_here >= 3 and half <= EXTRA and rows_here <= EXTRA

    my_rows = lax.dynamic_slice_in_dim(embeddings, section * half, half, 0)
    my_labels = lax.dynamic_slice_in_dim(labels, section * half, half, 0)
    gathered = lax.all_gather(my_rows, "dp", axis=0, tiled=True)
    label_all = lax.all_to_all(
        jnp.broadcast_to(my_labels[None], (batch_count,) + my_labels.shape), "dp", 0, 0, tiled=False
    ).reshape(-1)

    local_ids = sample_ids[0]
    chosen = jnp.take(centers, local_ids, axis=0).astype(jnp.float32)
    center_norm = jnp.sqrt(jnp.sum(chosen * chosen, axis=1) + EPSILON)
    unit_centers = (chosen / center_norm[:, None]).astype(jnp.bfloat16)
    global_ids = local_ids + shard_index * per_shard
    partner_centers = lax.ppermute(unit_centers, "section", swap)
    partner_ids = lax.ppermute(global_ids, "section", swap)
    both_centers = jnp.concatenate([unit_centers, partner_centers], axis=0)
    both_ids = jnp.concatenate([global_ids, partner_ids], axis=0)

    emb_float = gathered.astype(jnp.float32)
    row_norm = jnp.sqrt(jnp.sum(emb_float * emb_float, axis=1) + EPSILON)
    unit_rows = (emb_float / row_norm[:, None]).astype(jnp.bfloat16)
    cosine = lax.dot_general(
        unit_rows, both_centers, (((1,), (1,)), ((), ())), preferred_element_type=jnp.float32
    )
    matches = both_ids[None, :] == label_all[:, None]
    logits = LOGIT_SCALE * cosine - LOGIT_SCALE * MARGIN * matches.astype(jnp.float32)
    exponent = jnp.exp(logits)
    total_part = jnp.sum(exponent, axis=1)
    target_part = jnp.sum(jnp.where(matches, logits, jnp.float32(0.0)), axis=1)
    weights = exponent.astype(jnp.bfloat16)
    unscaled = jnp.dot(weights, both_centers, preferred_element_type=jnp.float32)
    own_center = jnp.dot(matches.astype(jnp.bfloat16), both_centers, preferred_element_type=jnp.float32)

    h = batch_count // 2

    def to_dest(values):
        tail = values.shape[1:]
        values = values.reshape((2, h, class_count, rows_here) + tail)
        values = jnp.moveaxis(values, 2, 0)
        values = jnp.swapaxes(values, 1, 2)
        return values.reshape((class_count, batch_count, rows_here) + tail)

    def pad(values):
        return jnp.pad(values, [(0, 0)] * (values.ndim - 1) + [(0, EXTRA - values.shape[-1])])

    block_rows = jnp.broadcast_to(
        jnp.stack([pad(total_part.reshape(batch_count, half)), pad(target_part.reshape(batch_count, half))], axis=1)[None],
        (class_count, batch_count, 2, EXTRA),
    )
    own_totals = pad(to_dest(total_part))[:, :, None, :]
    extra = jnp.concatenate(
        [block_rows, own_totals, jnp.zeros((class_count, batch_count, rows_here - 3, EXTRA), jnp.float32)], axis=2
    )
    payload = jnp.concatenate([to_dest(unscaled), to_dest(own_center), extra], axis=3)
    payload = lax.all_to_all(payload, "cls", 0, 0, tiled=False).sum(0)
    summed = lax.all_to_all(payload, "dp", 0, 0, tiled=False).sum(0)

    half_total = summed[0, 2 * width : 2 * width + half]
    half_target = summed[1, 2 * width : 2 * width + half]
    other_total, other_target = lax.ppermute((half_total, half_target), "section", swap)
    first = section == 0
    block_total = jnp.where(first, jnp.concatenate([half_total, other_total]), jnp.concatenate([other_total, half_total]))
    block_target = jnp.where(first, jnp.concatenate([half_target, other_target]), jnp.concatenate([other_target, half_target]))
    row_loss = jnp.log(block_total) - block_target

    unscaled_rows = summed[:, :width]
    own_rows = summed[:, width : 2 * width]
    totals_here = summed[2, 2 * width : 2 * width + rows_here]
    unit_grad = LOGIT_SCALE * (unscaled_rows / totals_here[:, None] - own_rows)
    source_batch = (batch % 2) * h + batch // 2
    offset = source_batch * half + cls * rows_here
    emb_rows = lax.dynamic_slice_in_dim(emb_float, offset, rows_here, 0)
    norm_rows = lax.dynamic_slice_in_dim(row_norm, offset, rows_here, 0)
    unit_float = emb_rows / norm_rows[:, None]
    along = jnp.sum(unit_float * unit_grad, axis=1, keepdims=True)
    computed = (unit_grad - unit_float * along) / norm_rows[:, None]

    pairs = [
        (s * batch_count + e, (1 - s) * batch_count + (e ^ 1))
        for s in range(2)
        for e in range(batch_count)
        if e % 2 != s
    ]
    received = lax.ppermute(computed, ("section", "dp"), pairs)
    feature_grad = jnp.where(batch % 2 == section, computed, received)
    return (feature_grad, row_loss)


def solution(mesh):
    return jax.shard_map(
        on_device,
        mesh=mesh,
        in_specs=(
            P("dp", None),
            P(("section", "dp", "cls"), None),
            P(("section", "dp", "cls"), None),
            P("dp"),
        ),
        out_specs=(P(("section", "dp", "cls"), None), P("dp")),
        check_vma=False,
    )
```

time: 208 us -> 219 us (1.053)
  starting transfers between devices: 25.4 us -> 30.1 us
  other arithmetic: 12 us -> 15.9 us
  local copies, waits for them, and re-layouts: 8.69 us -> 11.7 us
    ppermute x2 -> x3, starting transfers between devices: 7.17 us -> 10.1 us  [the longest x2 6.78 us: on_device(): lax.ppermute((half_total, half_target), 'section', swap)]
  transfers between devices with their start and end apart: 7 -> 8, of which waited for: 4 -> 4; matrix products, arithmetic and copies ran while one was open for 9% -> 5% of each run, Pallas kernels for 0% -> 0%
where the time goes in v4:
time: 219 us
  waiting for transfers between devices  70.9 us (32%)
  blocking collectives  53.1 us (24%)
  starting transfers between devices  30.1 us (14%)
  matrix products  22.7 us (10%)
  other arithmetic  15.9 us (7%)
  between operations  14.3 us (7%)
  local copies, waits for them, and re-layouts  11.7 us (5%)
    all_to_all x1, blocking collectives, on_device(): payload = lax.all_to_all(payload, 'cls', 0, 0, tiled=False).sum(0)  53.1 us
    all_gather x1, waiting for transfers between devices, on_device(): gathered = lax.all_gather(my_rows, 'dp', axis=0, tiled=True)  50 us
    all_to_all x1, waiting for transfers between devices, on_device(): summed = lax.all_to_all(payload, 'dp', 0, 0, tiled=False).sum(0)  11 us
    dot_general x1, matrix products, on_device(): lax.dot_general(unit_rows, both_centers, (((1,), (1,)), ((), ())), prefer...  10.3 us
    all_to_all x1, starting transfers between devices, on_device(): lax.all_to_all(jnp.broadcast_to(my_labels[None], (batch_count,) + my_labe...  9.22 us
    all_to_all x1, waiting for transfers between devices, on_device(): lax.all_to_all(jnp.broadcast_to(my_labels[None], (batch_count,) + my_labe...  8.7 us
    gather x1, local copies, waits for them, and re-layouts, on_device(): chosen = jnp.take(centers, local_ids, axis=0).astype(jnp.float32)  7.59 us
    dot_general x1, matrix products, on_device(): jnp.dot(weights, both_centers, preferred_element_type=jnp.float32)  7.57 us
  transfers between devices with their start and end apart: 8, of which 4 were waited for; matrix products, arithmetic and copies ran while one was open for 5% of the time, Pallas kernels for 0%

profile of v4, /device:TPU:1, one launch (start us, length us, event | category | flops | bytes accessed | tf_op | source)
XLA Modules:
  0.0 218.7 jit_solution(35875459189814517)
XLA Ops:
  7.2 0.7 fusion.14
  8.0 0.7 reduce
  8.7 7.6 %gather_fusion = bf16[1536,512]{1,0:T(8,128)(2,1)S(1)} fusion(bf16[4096,512]{1,0:T(8,128)(2,1)} %param.5, s32[2048]{0:T(1024)S(1)} %pad_clamp_fusion), kind=kCustom, calls=%fused_computation | custom fusion | bytes 3151872 | tf_op jit(solution)/shard_map/jit(_take)/gather | solution.py:38
  16.3 0.8 fusion.8
  17.1 1.1 fusion.9
  18.2 3.3 %collective-permute-start = (bf16[1536,512]{1,0:T(8,128)(2,1)S(1)}, bf16[1536,512]{1,0:T(8,128)(2,1)}, u32[]{:S(2)}, u32[]{:S(2)}) collective-permute-start(bf16[1536,512]{1,0:T(8,128)(2,1)S(1)} %fusion.9), channel_id=1, source_target_pairs={{0,128},{128,0},{1,129},{129,1},{2,130},{130,2},{3,131},{131,3},{4... | collective-permute-start | bytes 4718600 | tf_op jit(solution)/shard_map/ppermute | solution.py:42
  21.5 0.6 constant_dynamic-slice_fusion
  22.2 0.3 collective-permute-start.1
  22.5 0.6 broadcast_in_dim.22
  23.2 9.2 %all-to-all-start = ((s32[16,1,64]{2,1,0:T(1,128)}), s32[16,1,64]{2,1,0:T(1,128)S(1)}, u32[]{:S(2)}, u32[]{:S(2)}) async-start(s32[16,1,64]{2,1,0:T(1,128)} %broadcast_in_dim.22), calls=%async_computation | async-start | bytes 16384 | tf_op jit(solution)/shard_map/all_to_all | solution.py:33
  32.4 8.7 %all-to-all-done = s32[16,1,64]{2,1,0:T(1,128)S(1)} async-done(((s32[16,1,64]{2,1,0:T(1,128)}), s32[16,1,64]{2,1,0:T(1,128)S(1)}, u32[]{:S(2)}, u32[]{:S(2)}) %all-to-all-start) | async-done | bytes 4128 | tf_op jit(solution)/shard_map/all_to_all | solution.py:33
  41.1 0.5 broadcast.66
  41.7 0.7 reduce.6
  42.4 4.9 %fusion = f32[1024,512]{1,0:T(8,128)S(1)} fusion(s32[3072]{0:T(1024)S(1)} %pad_add_fusion, s32[1024]{0:T(1024)S(1)} %eq.26, bf16[1536,512]{1,0:T(8,128)(2,1)} %collective-permute-done, bf16[1536,512]{1,0:T(8,128)(2,1)S(1)} %fusion.9), kind=kOutput, calls=%fused_computation.2 | convolution fusion | flops 3230662656 | bytes 5259264 | tf_op jit(solution)/shard_map/dot_general | solution.py:60
  47.5 50.0 %all-gather.2.cloned.1.call-done = bf16[1024,512]{1,0:T(8,128)(2,1)} async-done(((bf16[64,512]{1,0:T(8,128)(2,1)}), bf16[1024,512]{1,0:T(8,128)(2,1)}) %all-gather.2.cloned.1.call-update) | async-done | bytes 1048592 | tf_op jit(solution)/shard_map/all_gather | solution.py:32
  97.4 1.5 multiply_reduce_fusion
  99.0 10.3 %fusion.3 = (f32[1024]{0:T(1024)S(1)}, f32[1024]{0:T(1024)S(1)}, f32[1024,3072]{1,0:T(8,128)}) fusion(s32[3072]{0:T(1024)S(1)} %pad_add_fusion, s32[1024]{0:T(1024)S(1)} %eq.26, bf16[1536,512]{1,0:T(8,128)(2,1)} %collective-permute-done, bf16[1536,512]{1,0:T(8,128)(2,1)} %copy-done.2, f32[1024]{0:T(1024)S(1)} %add_sqrt_fusion.1, ...), kind=kOutput, calls=%fused_computation.6 | convolution fusion | flops 3251107840 | bytes 16805888 | tf_op jit(solution)/shard_map/dot_general | solution.py:50
  109.4 7.6 %fusion.5 = f32[1024,512]{1,0:T(8,128)S(1)} fusion(f32[1024,3072]{1,0:T(8,128)} %get-tuple-element.6, s32[3072]{0:T(1024)S(1)} %pad_add_fusion, s32[1024]{0:T(1024)S(1)} %eq.26, bf16[1536,512]{1,0:T(8,128)(2,1)} %collective-permute-done, bf16[1536,512]{1,0:T(8,128)(2,1)} %copy-done.2), kind=kOutput, calls=%fused_computation.10 | convolution fusion | flops 3243245568 | bytes 17842176 | tf_op jit(solution)/shard_map/dot_general | solution.py:59
  117.0 1.6 copy.9
  118.8 2.2 maximum_maximum_fusion
  121.0 53.1 %all_to_all.16 = f32[8,16,8,1152]{3,2,1,0:T(8,128)} all-to-all(f32[8,16,8,1152]{3,2,1,0:T(8,128)S(1)} %maximum_maximum_fusion), channel_id=1, replica_groups=mesh['section'=2,'dp'=16,'cls'=8] {'cls'}, dimensions={0} | all-to-all | bytes 9437184 | tf_op jit(solution)/shard_map/all_to_all | solution.py:83
  174.1 3.5 %reduce_sum.67 = f32[16,8,1152]{2,1,0:T(8,128)} reduce(f32[8,16,8,1152]{3,2,1,0:T(8,128)} %all_to_all.16, f32[]{:T(128)} %constant.68.clone.1), dimensions={0}, to_apply=%region_4.5 | reduce | flops 1032192 | bytes 5308420 | tf_op jit(solution)/shard_map/reduce_sum | solution.py:83
  177.6 7.3 %all-to-all-start.2 = ((f32[16,8,1152]{2,1,0:T(8,128)}), f32[16,8,1152]{2,1,0:T(8,128)S(1)}, u32[]{:S(2)}, u32[]{:S(2)}) async-start(f32[16,8,1152]{2,1,0:T(8,128)} %reduce_sum.67), calls=%async_computation.2 | async-start | bytes 1179648 | tf_op jit(solution)/shard_map/all_to_all | solution.py:84
  185.0 1.6 convert_element_type.22
  186.6 11.0 %all-to-all-done.2 = f32[16,8,1152]{2,1,0:T(8,128)S(1)} async-done(((f32[16,8,1152]{2,1,0:T(8,128)}), f32[16,8,1152]{2,1,0:T(8,128)S(1)}, u32[]{:S(2)}, u32[]{:S(2)}) %all-to-all-start.2) | async-done | bytes 589856 | tf_op jit(solution)/shard_map/all_to_all | solution.py:84
  197.7 6.7 %collective-permute-start.3 = (f32[64]{0:T(128)S(1)}, f32[64]{0:T(128)S(1)}, u32[]{:S(2)}, u32[]{:S(2)}) collective-permute-start(f32[64]{0:T(128)S(1)} %get-tuple-element.5), channel_id=1, source_target_pairs={{0,128},{128,0},{1,129},{129,1},{2,130},{130,2},{3,131},{131,3},{4... | collective-permute-start | bytes 776 | tf_op jit(solution)/shard_map/ppermute | solution.py:88
  204.5 0.9 multiply_reduce_fusion.1
  205.4 0.8 subtract_divide_fusion
  206.2 3.3 %collective-permute-start.2 = (f32[8,512]{1,0:T(8,128)S(1)}, f32[8,512]{1,0:T(8,128)S(1)}, u32[]{:S(2)}, u32[]{:S(2)}) collective-permute-start(f32[8,512]{1,0:T(8,128)S(1)} %subtract_divide_fusion), channel_id=1, source_target_pairs={{8,128},{24,144},{40,160},{56,176},{72,192},{88,208},{104,224},{12... | collective-permute-start | bytes 49160 | tf_op jit(solution)/shard_map/ppermute | solution.py:112
  209.5 0.6 fusion.16
  210.1 1.1 collective-permute-done.2
  211.2 0.6 broadcast_select_fusion.1
  (39 shorter events, 1.0 us)
Async XLA Ops:
  7.2 14.4 %copy-start = (bf16[128,512]{1,0:T(8,128)(2,1)S(1)}, bf16[128,512]{1,0:T(8,128)(2,1)}, u32[]{:S(2)}) copy-start(bf16[128,512]{1,0:T(8,128)(2,1)} %param.4) | copy-start | bytes 393220
  7.2 90.3 %all-gather.2.cloned.1.call-start = ((), (), s32[]{:S(2)}) async-start(), calls=%async_computation.3 | async-start | bytes 1114112 | tf_op jit(solution)/shard_map/all_gather | solution.py:32
  16.3 6.2 %copy-start.3 = (s32[128]{0:T(128)S(1)}, s32[128]{0:T(128)}, u32[]{:S(2)}) copy-start(s32[128]{0:T(128)} %param.7) | copy-start | bytes 1540
  18.2 29.0 %copy-start.2 = (bf16[1536,512]{1,0:T(8,128)(2,1)}, bf16[1536,512]{1,0:T(8,128)(2,1)S(1)}, u32[]{:S(2)}) copy-start(bf16[1536,512]{1,0:T(8,128)(2,1)S(1)} %fusion.9) | copy-start | bytes 4718596
  18.2 24.2 %collective-permute-start = (bf16[1536,512]{1,0:T(8,128)(2,1)S(1)}, bf16[1536,512]{1,0:T(8,128)(2,1)}, u32[]{:S(2)}, u32[]{:S(2)}) collective-permute-start(bf16[1536,512]{1,0:T(8,128)(2,1)S(1)} %fusion.9), channel_id=1, source_target_pairs={{0,128},{128,0},{1,129},{129,1},{2,130},{130,2},{3,131},{131,3},{4... | collective-permute-start | bytes 4718600 | tf_op jit(solution)/shard_map/ppermute | solution.py:42
  22.2 10.2 %collective-permute-start.1 = (s32[1536]{0:T(1024)S(1)}, s32[1536]{0:T(1024)S(1)}, u32[]{:S(2)}, u32[]{:S(2)}) collective-permute-start(s32[1536]{0:T(1024)S(1)} %broadcast_add_fusion), channel_id=1, source_target_pairs={{0,128},{128,0},{1,129},{129,1},{2,130},{130,2},{3,131},{131,3},{4... | collective-permute-start | bytes 18440 | tf_op jit(solution)/shard_map/ppermute | solution.py:43
  23.2 18.0 %all-to-all-start = ((s32[16,1,64]{2,1,0:T(1,128)}), s32[16,1,64]{2,1,0:T(1,128)S(1)}, u32[]{:S(2)}, u32[]{:S(2)}) async-start(s32[16,1,64]{2,1,0:T(1,128)} %broadcast_in_dim.22), calls=%async_computation | async-start | bytes 16384 | tf_op jit(solution)/shard_map/all_to_all | solution.py:33
  174.0 10.9 %copy-start.1 = (bf16[1024,512]{1,0:T(8,128)(2,1)S(1)}, bf16[1024,512]{1,0:T(8,128)(2,1)}, u32[]{:S(2)}) copy-start(bf16[1024,512]{1,0:T(8,128)(2,1)} %all-gather.2.cloned.1.call-done) | copy-start | bytes 3145732
  177.6 20.0 %all-to-all-start.2 = ((f32[16,8,1152]{2,1,0:T(8,128)}), f32[16,8,1152]{2,1,0:T(8,128)S(1)}, u32[]{:S(2)}, u32[]{:S(2)}) async-start(f32[16,8,1152]{2,1,0:T(8,128)} %reduce_sum.67), calls=%async_computation.2 | async-start | bytes 1179648 | tf_op jit(solution)/shard_map/all_to_all | solution.py:84
  197.7 11.8 %collective-permute-start.3 = (f32[64]{0:T(128)S(1)}, f32[64]{0:T(128)S(1)}, u32[]{:S(2)}, u32[]{:S(2)}) collective-permute-start(f32[64]{0:T(128)S(1)} %get-tuple-element.5), channel_id=1, source_target_pairs={{0,128},{128,0},{1,129},{129,1},{2,130},{130,2},{3,131},{131,3},{4... | collective-permute-start | bytes 776 | tf_op jit(solution)/shard_map/ppermute | solution.py:88
  204.4 5.1 %collective-permute-start.4 = (f32[64]{0:T(128)S(1)}, f32[64]{0:T(128)S(1)}, u32[]{:S(2)}, u32[]{:S(2)}) collective-permute-start(f32[64]{0:T(128)S(1)} %get-tuple-element.4), channel_id=1, source_target_pairs={{0,128},{128,0},{1,129},{129,1},{2,130},{130,2},{3,131},{131,3},{4... | collective-permute-start | bytes 776 | tf_op jit(solution)/shard_map/ppermute | solution.py:88
  206.2 5.0 %collective-permute-start.2 = (f32[8,512]{1,0:T(8,128)S(1)}, f32[8,512]{1,0:T(8,128)S(1)}, u32[]{:S(2)}, u32[]{:S(2)}) collective-permute-start(f32[8,512]{1,0:T(8,128)S(1)} %subtract_divide_fusion), channel_id=1, source_target_pairs={{8,128},{24,144},{40,160},{56,176},{72,192},{88,208},{104,224},{12... | collective-permute-start | bytes 49160 | tf_op jit(solution)/shard_map/ppermute | solution.py:112
Sparse Core Ops, SparseCore 0:
  22.3 75.0 all-gather.1

commit v5 on v4

--- a/solution.py
+++ b/solution.py
@@ -29,10 +29,16 @@
 
     my_rows = lax.dynamic_slice_in_dim(embeddings, section * half, half, 0)
     my_labels = lax.dynamic_slice_in_dim(labels, section * half, half, 0)
-    gathered = lax.all_gather(my_rows, "dp", axis=0, tiled=True)
-    label_all = lax.all_to_all(
-        jnp.broadcast_to(my_labels[None], (batch_count,) + my_labels.shape), "dp", 0, 0, tiled=False
-    ).reshape(-1)
+    pieces = jnp.stack([my_labels % 256, (my_labels // 256) % 256, my_labels // 65536], axis=1)
+    packed = jnp.concatenate(
+        [my_rows, pieces.astype(jnp.bfloat16), jnp.zeros((half, EXTRA - 3), jnp.bfloat16)], axis=1
+    )
+    packed = lax.all_to_all(
+        jnp.broadcast_to(packed[None], (batch_count,) + packed.shape), "dp", 0, 0, tiled=False
+    ).reshape(batch_count * half, width + EXTRA)
+    gathered = packed[:, :width]
+    received = packed[:, width : width + 3].astype(jnp.int32)
+    label_all = received[:, 0] + 256 * received[:, 1] + 65536 * received[:, 2]
 
     local_ids = sample_ids[0]
     chosen = jnp.take(centers, local_ids, axis=0).astype(jnp.float32)

time: 219 us -> 171 us (0.78)
  waiting for transfers between devices: 70.9 us -> 35.1 us
  between operations: 14.3 us -> 0.95 us
  other arithmetic: 15.9 us -> 13.1 us
  blocking collectives: 53.1 us -> 55.7 us
    all_gather x1 -> x0, waiting for transfers between devices: 50 us -> none  [on_device(): gathered = lax.all_gather(my_rows, 'dp', axis=0, tiled=True)]
    all_to_all x1, waiting for transfers between devices: 8.7 us -> 17.4 us  [on_device(): lax.all_to_all(jnp.broadcast_to(packed[None], (batch_count,) + packed.sha...]
    ppermute x1, waiting for transfers between devices: 0.01 us -> 3.35 us  [on_device(): partner_ids = lax.ppermute(global_ids, 'section', swap)]
    ppermute x2, starting transfers between devices: 6.78 us -> 3.75 us  [on_device(): lax.ppermute((half_total, half_target), 'section', swap)]
    all_to_all x1, blocking collectives: 53.1 us -> 55.7 us  [on_device(): payload = lax.all_to_all(payload, 'cls', 0, 0, tiled=False).sum(0)]
    all_to_all x1, starting transfers between devices: 9.22 us -> 11.7 us  [on_device(): lax.all_to_all(jnp.broadcast_to(packed[None], (batch_count,) + packed.sha...]
    all_to_all x1, waiting for transfers between devices: 11 us -> 13.5 us  [on_device(): summed = lax.all_to_all(payload, 'dp', 0, 0, tiled=False).sum(0)]
    all_to_all x1, starting transfers between devices: 7.28 us -> 9.72 us  [on_device(): summed = lax.all_to_all(payload, 'dp', 0, 0, tiled=False).sum(0)]
  transfers between devices with their start and end apart: 8 -> 7, of which waited for: 4 -> 4; matrix products, arithmetic and copies ran while one was open for 5% -> 9% of each run, Pallas kernels for 0% -> 0%
where the time goes in v5:
time: 171 us
  blocking collectives  55.7 us (33%)
  waiting for transfers between devices  35.1 us (21%)
  starting transfers between devices  30 us (18%)
  matrix products  23 us (13%)
  other arithmetic  13.1 us (8%)
  local copies, waits for them, and re-layouts  12.8 us (7%)
    all_to_all x1, blocking collectives, on_device(): payload = lax.all_to_all(payload, 'cls', 0, 0, tiled=False).sum(0)  55.7 us
    all_to_all x1, waiting for transfers between devices, on_device(): lax.all_to_all(jnp.broadcast_to(packed[None], (batch_count,) + packed.sha...  17.4 us
    all_to_all x1, waiting for transfers between devices, on_device(): summed = lax.all_to_all(payload, 'dp', 0, 0, tiled=False).sum(0)  13.5 us
    all_to_all x1, starting transfers between devices, on_device(): lax.all_to_all(jnp.broadcast_to(packed[None], (batch_count,) + packed.sha...  11.7 us
    dot_general x1, matrix products, on_device(): lax.dot_general(unit_rows, both_centers, (((1,), (1,)), ((), ())), prefer...  10.1 us
    all_to_all x1, starting transfers between devices, on_device(): summed = lax.all_to_all(payload, 'dp', 0, 0, tiled=False).sum(0)  9.72 us
    gather x1, local copies, waits for them, and re-layouts, on_device(): chosen = jnp.take(centers, local_ids, axis=0).astype(jnp.float32)  7.59 us
    dot_general x1, matrix products, on_device(): jnp.dot(weights, both_centers, preferred_element_type=jnp.float32)  7.57 us
  transfers between devices with their start and end apart: 7, of which 4 were waited for; matrix products, arithmetic and copies ran while one was open for 9% of the time, Pallas kernels for 0%

profile of v5, /device:TPU:1, one launch (start us, length us, event | category | flops | bytes accessed | tf_op | source)
XLA Modules:
  0.0 170.7 jit_solution(11153877386887889033)
XLA Ops:
  0.7 0.8 fusion.22
  1.5 0.1 copy.15
  1.6 0.1 copy.16
  2.0 1.2 broadcast_in_dim.23
  3.2 11.7 %all-to-all-start = ((bf16[16,64,640]{2,1,0:T(8,128)(2,1)}), bf16[16,64,640]{2,1,0:T(8,128)(2,1)S(1)}, u32[]{:S(2)}, u32[]{:S(2)}) async-start(bf16[16,64,640]{2,1,0:T(8,128)(2,1)} %broadcast_in_dim.23), calls=%async_computation | async-start | bytes 2621440 | tf_op jit(solution)/shard_map/all_to_all | solution.py:36
  15.0 7.6 %gather_fusion = bf16[1536,512]{1,0:T(8,128)(2,1)S(1)} fusion(bf16[4096,512]{1,0:T(8,128)(2,1)} %param.5, s32[2048]{0:T(1024)S(1)} %pad_clamp_fusion), kind=kCustom, calls=%fused_computation | custom fusion | bytes 3151872 | tf_op jit(solution)/shard_map/jit(_take)/gather | solution.py:44
  22.6 0.8 fusion.8
  23.4 2.0 %fusion.9 = bf16[1536,512]{1,0:T(8,128)(2,1)} fusion(f32[1536]{0:T(1024)S(1)} %add_sqrt_fusion, bf16[1536,512]{1,0:T(8,128)(2,1)S(1)} %gather_fusion, pred[1536]{0:T(1024)(128)(4,1)S(1)} %compare_and_fusion), kind=kLoop, calls=%fused_computation.17 | loop fusion | flops 3145728 | bytes 3153408 | tf_op jit(solution)/shard_map/convert_element_type | solution.py:46
  25.4 1.0 collective-permute-start
  26.4 3.4 %collective-permute-done.1 = s32[1536]{0:T(1024)S(1)} collective-permute-done((s32[1536]{0:T(1024)S(1)}, s32[1536]{0:T(1024)S(1)}, u32[]{:S(2)}, u32[]{:S(2)}) %collective-permute-start.1) | collective-permute-done | bytes 6176 | tf_op jit(solution)/shard_map/ppermute | solution.py:49
  29.7 17.4 %all-to-all-done = bf16[16,64,640]{2,1,0:T(8,128)(2,1)S(1)} async-done(((bf16[16,64,640]{2,1,0:T(8,128)(2,1)}), bf16[16,64,640]{2,1,0:T(8,128)(2,1)S(1)}, u32[]{:S(2)}, u32[]{:S(2)}) %all-to-all-start) | async-done | bytes 1310752 | tf_op jit(solution)/shard_map/all_to_all | solution.py:36
  47.2 0.5 fusion.13
  47.7 0.3 multiply_reduce_fusion
  48.0 10.1 %fusion.3 = (f32[1024]{0:T(1024)S(1)}, f32[1024]{0:T(1024)S(1)}, f32[1024,3072]{1,0:T(8,128)}) fusion(s32[3072]{0:T(1024)S(1)} %pad_add_fusion, s32[1024]{0:T(1024)S(1)} %fusion.13, bf16[1536,512]{1,0:T(8,128)(2,1)} %collective-permute-done, bf16[1536,512]{1,0:T(8,128)(2,1)} %fusion.9, f32[1024]{0:T(1024)S(1)} %add_sqrt_fusion.1, ...), kind=kOutput, calls=%fused_computation.6 | convolution fusion | flops 3251107840 | bytes 16805888 | tf_op jit(solution)/shard_map/dot_general | solution.py:56
  58.3 7.6 %fusion.5 = f32[1024,512]{1,0:T(8,128)S(1)} fusion(f32[1024,3072]{1,0:T(8,128)} %get-tuple-element.9, s32[3072]{0:T(1024)S(1)} %pad_add_fusion, s32[1024]{0:T(1024)S(1)} %fusion.13, bf16[1536,512]{1,0:T(8,128)(2,1)} %collective-permute-done, bf16[1536,512]{1,0:T(8,128)(2,1)} %fusion.9), kind=kOutput, calls=%fused_computation.10 | convolution fusion | flops 3243245568 | bytes 17842176 | tf_op jit(solution)/shard_map/dot_general | solution.py:65
  65.9 1.6 copy.18
  67.6 5.3 %fusion = f32[1024,512]{1,0:T(8,128)S(1)} fusion(s32[3072]{0:T(1024)S(1)} %pad_add_fusion, s32[1024]{0:T(1024)S(1)} %fusion.13, bf16[1536,512]{1,0:T(8,128)(2,1)} %collective-permute-done, bf16[1536,512]{1,0:T(8,128)(2,1)} %fusion.9), kind=kOutput, calls=%fused_computation.2 | convolution fusion | flops 3230662656 | bytes 5259264 | tf_op jit(solution)/shard_map/dot_general | solution.py:66
  73.0 0.2 copy.19
  73.3 1.3 copy-done.1
  74.6 0.6 maximum_maximum_fusion
  75.1 55.7 %all_to_all.15 = f32[8,16,8,1152]{3,2,1,0:T(8,128)} all-to-all(f32[8,16,8,1152]{3,2,1,0:T(8,128)S(1)} %maximum_maximum_fusion), channel_id=1, replica_groups=mesh['section'=2,'dp'=16,'cls'=8] {'cls'}, dimensions={0} | all-to-all | bytes 9437184 | tf_op jit(solution)/shard_map/all_to_all | solution.py:89
  130.8 3.5 %reduce_sum.67 = f32[16,8,1152]{2,1,0:T(8,128)} reduce(f32[8,16,8,1152]{3,2,1,0:T(8,128)} %all_to_all.15, f32[]{:T(128)} %constant.114.clone.1), dimensions={0}, to_apply=%region_4.5 | reduce | flops 1032192 | bytes 5308420 | tf_op jit(solution)/shard_map/reduce_sum | solution.py:89
  134.3 9.7 %all-to-all-start.2 = ((f32[16,8,1152]{2,1,0:T(8,128)}), f32[16,8,1152]{2,1,0:T(8,128)S(1)}, u32[]{:S(2)}, u32[]{:S(2)}) async-start(f32[16,8,1152]{2,1,0:T(8,128)} %reduce_sum.67), calls=%async_computation.2 | async-start | bytes 1179648 | tf_op jit(solution)/shard_map/all_to_all | solution.py:90
  144.1 1.6 slice_convert_fusion
  145.7 13.5 %all-to-all-done.2 = f32[16,8,1152]{2,1,0:T(8,128)S(1)} async-done(((f32[16,8,1152]{2,1,0:T(8,128)}), f32[16,8,1152]{2,1,0:T(8,128)S(1)}, u32[]{:S(2)}, u32[]{:S(2)}) %all-to-all-start.2) | async-done | bytes 589856 | tf_op jit(solution)/shard_map/all_to_all | solution.py:90
  159.3 3.7 %collective-permute-start.3 = (f32[64]{0:T(128)S(1)}, f32[64]{0:T(128)S(1)}, u32[]{:S(2)}, u32[]{:S(2)}) collective-permute-start(f32[64]{0:T(128)S(1)} %get-tuple-element.7), channel_id=1, source_target_pairs={{0,128},{128,0},{1,129},{129,1},{2,130},{130,2},{3,131},{131,3},{4... | collective-permute-start | bytes 776 | tf_op jit(solution)/shard_map/ppermute | solution.py:94
  163.0 0.9 multiply_reduce_fusion.1
  164.0 0.8 subtract_divide_fusion
  164.8 3.9 %collective-permute-start.2 = (f32[8,512]{1,0:T(8,128)S(1)}, f32[8,512]{1,0:T(8,128)S(1)}, u32[]{:S(2)}, u32[]{:S(2)}) collective-permute-start(f32[8,512]{1,0:T(8,128)S(1)} %subtract_divide_fusion), channel_id=1, source_target_pairs={{8,128},{24,144},{40,160},{56,176},{72,192},{88,208},{104,224},{12... | collective-permute-start | bytes 49160 | tf_op jit(solution)/shard_map/ppermute | solution.py:118
  168.7 0.6 fusion.18
  169.3 0.8 collective-permute-done.2
  170.1 0.6 broadcast_select_fusion.1
  (39 shorter events, 1.0 us)
Async XLA Ops:
  0.6 1.2 copy-start
  0.6 14.3 %copy-start.2 = (s32[1,1536]{1,0:T(1,128)S(1)}, s32[1,1536]{1,0:T(1,128)}, u32[]{:S(2)}) copy-start(s32[1,1536]{1,0:T(1,128)} %param.6) | copy-start | bytes 18436
  3.2 44.0 %all-to-all-start = ((bf16[16,64,640]{2,1,0:T(8,128)(2,1)}), bf16[16,64,640]{2,1,0:T(8,128)(2,1)S(1)}, u32[]{:S(2)}, u32[]{:S(2)}) async-start(bf16[16,64,640]{2,1,0:T(8,128)(2,1)} %broadcast_in_dim.23), calls=%async_computation | async-start | bytes 2621440 | tf_op jit(solution)/shard_map/all_to_all | solution.py:36
  25.4 22.6 %collective-permute-start = (bf16[1536,512]{1,0:T(8,128)(2,1)}, bf16[1536,512]{1,0:T(8,128)(2,1)}, u32[]{:S(2)}, u32[]{:S(2)}) collective-permute-start(bf16[1536,512]{1,0:T(8,128)(2,1)} %fusion.9), channel_id=1, source_target_pairs={{0,128},{128,0},{1,129},{129,1},{2,130},{130,2},{3,131},{131,3},{4... | collective-permute-start | bytes 4718600 | tf_op jit(solution)/shard_map/ppermute | solution.py:48
  26.3 3.4 %collective-permute-start.1 = (s32[1536]{0:T(1024)S(1)}, s32[1536]{0:T(1024)S(1)}, u32[]{:S(2)}, u32[]{:S(2)}) collective-permute-start(s32[1536]{0:T(1024)S(1)} %broadcast_add_fusion), channel_id=1, source_target_pairs={{0,128},{128,0},{1,129},{129,1},{2,130},{130,2},{3,131},{131,3},{4... | collective-permute-start | bytes 18440 | tf_op jit(solution)/shard_map/ppermute | solution.py:49
  73.0 1.6 copy-start.1
  134.3 24.9 %all-to-all-start.2 = ((f32[16,8,1152]{2,1,0:T(8,128)}), f32[16,8,1152]{2,1,0:T(8,128)S(1)}, u32[]{:S(2)}, u32[]{:S(2)}) async-start(f32[16,8,1152]{2,1,0:T(8,128)} %reduce_sum.67), calls=%async_computation.2 | async-start | bytes 1179648 | tf_op jit(solution)/shard_map/all_to_all | solution.py:90
  159.3 9.4 %collective-permute-start.3 = (f32[64]{0:T(128)S(1)}, f32[64]{0:T(128)S(1)}, u32[]{:S(2)}, u32[]{:S(2)}) collective-permute-start(f32[64]{0:T(128)S(1)} %get-tuple-element.7), channel_id=1, source_target_pairs={{0,128},{128,0},{1,129},{129,1},{2,130},{130,2},{3,131},{131,3},{4... | collective-permute-start | bytes 776 | tf_op jit(solution)/shard_map/ppermute | solution.py:94
  162.9 5.7 %collective-permute-start.4 = (f32[64]{0:T(128)S(1)}, f32[64]{0:T(128)S(1)}, u32[]{:S(2)}, u32[]{:S(2)}) collective-permute-start(f32[64]{0:T(128)S(1)} %get-tuple-element.6), channel_id=1, source_target_pairs={{0,128},{128,0},{1,129},{129,1},{2,130},{130,2},{3,131},{131,3},{4... | collective-permute-start | bytes 776 | tf_op jit(solution)/shard_map/ppermute | solution.py:94
  164.8 5.3 %collective-permute-start.2 = (f32[8,512]{1,0:T(8,128)S(1)}, f32[8,512]{1,0:T(8,128)S(1)}, u32[]{:S(2)}, u32[]{:S(2)}) collective-permute-start(f32[8,512]{1,0:T(8,128)S(1)} %subtract_divide_fusion), channel_id=1, source_target_pairs={{8,128},{24,144},{40,160},{56,176},{72,192},{88,208},{104,224},{12... | collective-permute-start | bytes 49160 | tf_op jit(solution)/shard_map/ppermute | solution.py:118

commit v6 on v5

--- a/solution.py
+++ b/solution.py
@@ -7,6 +7,26 @@
 MARGIN = 0.35
 EPSILON = 1e-06
 EXTRA = 128
+
+
+def split_pair(values):
+    high = values.astype(jnp.bfloat16)
+    low = (values - high.astype(jnp.float32)).astype(jnp.bfloat16)
+    return high, low
+
+
+def reduce_stage(unscaled, own_center, extra, axis):
+    width, more = unscaled.shape[-1], extra.shape[-1]
+    unscaled_high, unscaled_low = split_pair(unscaled)
+    extra_high, extra_low = split_pair(extra)
+    packed = jnp.concatenate(
+        [unscaled_high, unscaled_low, own_center.astype(jnp.bfloat16), extra_high, extra_low], axis=-1
+    )
+    packed = lax.all_to_all(packed, axis, 0, 0, tiled=False).astype(jnp.float32)
+    unscaled = (packed[..., :width] + packed[..., width : 2 * width]).sum(0)
+    own_center = packed[..., 2 * width : 3 * width].sum(0)
+    extra = (packed[..., 3 * width : 3 * width + more] + packed[..., 3 * width + more :]).sum(0)
+    return unscaled, own_center, extra
 
 
 def on_device(embeddings, centers, sample_ids, labels):
@@ -85,9 +105,10 @@
     extra = jnp.concatenate(
         [block_rows, own_totals, jnp.zeros((class_count, batch_count, rows_here - 3, EXTRA), jnp.float32)], axis=2
     )
-    payload = jnp.concatenate([to_dest(unscaled), to_dest(own_center), extra], axis=3)
-    payload = lax.all_to_all(payload, "cls", 0, 0, tiled=False).sum(0)
-    summed = lax.all_to_all(payload, "dp", 0, 0, tiled=False).sum(0)
+    unscaled, own_center, extra = to_dest(unscaled), to_dest(own_center), extra
+    for axis in ("cls", "dp"):
+        unscaled, own_center, extra = reduce_stage(unscaled, own_center, extra, axis)
+    summed = jnp.concatenate([unscaled, own_center, extra], axis=-1)
 
     half_total = summed[0, 2 * width : 2 * width + half]
     half_target = summed[1, 2 * width : 2 * width + half]

time: 171 us -> 155 us (0.906)
  blocking collectives: 55.7 us -> 44.4 us
  local copies, waits for them, and re-layouts: 12.8 us -> 10.9 us
    all_to_all x1, blocking collectives: 55.7 us -> 44.4 us  [reduce_stage(): packed = lax.all_to_all(packed, axis, 0, 0, tiled=False).astype(jnp.float32)]
    reduce_sum x2 -> x4, other arithmetic: 3.5 us -> 0.52 us  [the longest x1 0.4 us: reduce_stage(): own_center = packed[..., 2 * width:3 * width].sum(0)]
    unnamed x1 -> x7, other arithmetic: 0.02 us -> 2.64 us
    convert_element_type x0 -> x2, other arithmetic: none -> 1.73 us  [reduce_stage(): packed = lax.all_to_all(packed, axis, 0, 0, tiled=False).astype(jnp.float32)]
  transfers between devices with their start and end apart: 7 -> 7, of which waited for: 4 -> 4; matrix products, arithmetic and copies ran while one was open for 9% -> 8% of each run, Pallas kernels for 0% -> 0%
where the time goes in v6:
time: 155 us
  blocking collectives  44.4 us (29%)
  waiting for transfers between devices  34.6 us (22%)
  starting transfers between devices  29.2 us (19%)
  matrix products  23 us (15%)
  other arithmetic  11.9 us (8%)
  local copies, waits for them, and re-layouts  10.9 us (7%)
    all_to_all x1, blocking collectives, reduce_stage(): packed = lax.all_to_all(packed, axis, 0, 0, tiled=False).astype(jnp.float32)  44.4 us
    all_to_all x1, waiting for transfers between devices, on_device(): lax.all_to_all(jnp.broadcast_to(packed[None], (batch_count,) + packed.sha...  17.4 us
    all_to_all x1, waiting for transfers between devices, reduce_stage(): packed = lax.all_to_all(packed, axis, 0, 0, tiled=False).astype(jnp.float32)  12.9 us
    all_to_all x1, starting transfers between devices, on_device(): lax.all_to_all(jnp.broadcast_to(packed[None], (batch_count,) + packed.sha...  11.7 us
    dot_general x1, matrix products, on_device(): lax.dot_general(unit_rows, both_centers, (((1,), (1,)), ((), ())), prefer...  10.1 us
    all_to_all x1, starting transfers between devices, reduce_stage(): packed = lax.all_to_all(packed, axis, 0, 0, tiled=False).astype(jnp.float32)  9.76 us
    gather x1, local copies, waits for them, and re-layouts, on_device(): chosen = jnp.take(centers, local_ids, axis=0).astype(jnp.float32)  7.59 us
    dot_general x1, matrix products, on_device(): jnp.dot(weights, both_centers, preferred_element_type=jnp.float32)  7.57 us
  transfers between devices with their start and end apart: 7, of which 4 were waited for; matrix products, arithmetic and copies ran while one was open for 8% of the time, Pallas kernels for 0%

profile of v6, /device:TPU:1, one launch (start us, length us, event | category | flops | bytes accessed | tf_op | source)
XLA Modules:
  0.0 155.0 jit_solution(12924293637552470216)
XLA Ops:
  0.7 0.8 fusion.36
  2.0 1.2 broadcast_in_dim.23
  3.2 11.7 %all-to-all-start = ((bf16[16,64,640]{2,1,0:T(8,128)(2,1)}), bf16[16,64,640]{2,1,0:T(8,128)(2,1)S(1)}, u32[]{:S(2)}, u32[]{:S(2)}) async-start(bf16[16,64,640]{2,1,0:T(8,128)(2,1)} %broadcast_in_dim.23), calls=%async_computation | async-start | bytes 2621440 | tf_op jit(solution)/shard_map/all_to_all | solution.py:56
  15.0 7.6 %gather_fusion = bf16[1536,512]{1,0:T(8,128)(2,1)S(1)} fusion(bf16[4096,512]{1,0:T(8,128)(2,1)} %param.5, s32[2048]{0:T(1024)S(1)} %pad_clamp_fusion), kind=kCustom, calls=%fused_computation | custom fusion | bytes 3151872 | tf_op jit(solution)/shard_map/jit(_take)/gather | solution.py:64
  22.6 0.8 fusion.8
  23.4 2.0 %fusion.9 = bf16[1536,512]{1,0:T(8,128)(2,1)} fusion(f32[1536]{0:T(1024)S(1)} %add_sqrt_fusion, bf16[1536,512]{1,0:T(8,128)(2,1)S(1)} %gather_fusion, pred[1536]{0:T(1024)(128)(4,1)S(1)} %compare_and_fusion), kind=kLoop, calls=%fused_computation.16 | loop fusion | flops 3145728 | bytes 3153408 | tf_op jit(solution)/shard_map/convert_element_type | solution.py:66
  25.4 1.0 collective-permute-start
  26.4 3.3 %collective-permute-done.1 = s32[1536]{0:T(1024)S(1)} collective-permute-done((s32[1536]{0:T(1024)S(1)}, s32[1536]{0:T(1024)S(1)}, u32[]{:S(2)}, u32[]{:S(2)}) %collective-permute-start.1) | collective-permute-done | bytes 6176 | tf_op jit(solution)/shard_map/ppermute | solution.py:69
  29.7 17.4 %all-to-all-done = bf16[16,64,640]{2,1,0:T(8,128)(2,1)S(1)} async-done(((bf16[16,64,640]{2,1,0:T(8,128)(2,1)}), bf16[16,64,640]{2,1,0:T(8,128)(2,1)S(1)}, u32[]{:S(2)}, u32[]{:S(2)}) %all-to-all-start) | async-done | bytes 1310752 | tf_op jit(solution)/shard_map/all_to_all | solution.py:56
  47.2 0.5 fusion.19
  47.7 0.3 multiply_reduce_fusion
  48.0 10.1 %fusion.3 = (f32[1024]{0:T(1024)S(1)}, f32[1024]{0:T(1024)S(1)}, f32[1024,3072]{1,0:T(8,128)}) fusion(s32[3072]{0:T(1024)S(1)} %pad_add_fusion, s32[1024]{0:T(1024)S(1)} %fusion.19, bf16[1536,512]{1,0:T(8,128)(2,1)} %collective-permute-done, bf16[1536,512]{1,0:T(8,128)(2,1)} %fusion.9, f32[1024]{0:T(1024)S(1)} %add_sqrt_fusion.1, ...), kind=kOutput, calls=%fused_computation.6 | convolution fusion | flops 3251107840 | bytes 16805888 | tf_op jit(solution)/shard_map/dot_general | solution.py:76
  58.4 7.6 %fusion.5 = f32[1024,512]{1,0:T(8,128)S(1)} fusion(f32[1024,3072]{1,0:T(8,128)} %get-tuple-element.13, s32[3072]{0:T(1024)S(1)} %pad_add_fusion, s32[1024]{0:T(1024)S(1)} %fusion.19, bf16[1536,512]{1,0:T(8,128)(2,1)} %collective-permute-done, bf16[1536,512]{1,0:T(8,128)(2,1)} %fusion.9), kind=kOutput, calls=%fused_computation.10 | convolution fusion | flops 3243245568 | bytes 17842176 | tf_op jit(solution)/shard_map/dot_general | solution.py:85
  66.3 0.3 fusion.15
  66.6 5.3 %fusion.11 = bf16[1024,512]{1,0:T(8,128)(2,1)S(1)} fusion(s32[3072]{0:T(1024)S(1)} %pad_add_fusion, s32[1024]{0:T(1024)S(1)} %fusion.19, bf16[1536,512]{1,0:T(8,128)(2,1)} %collective-permute-done, bf16[1536,512]{1,0:T(8,128)(2,1)} %fusion.9), kind=kOutput, calls=%fused_computation.25 | convolution fusion | flops 3231186944 | bytes 4210688 | tf_op jit(solution)/shard_map/dot_general | solution.py:86
  72.7 44.4 %all_to_all.15 = bf16[8,16,8,1792]{3,2,1,0:T(8,128)(2,1)S(1)} all-to-all(bf16[8,16,8,1792]{3,2,1,0:T(8,128)(2,1)S(1)} %fusion.24), channel_id=1, replica_groups=mesh['section'=2,'dp'=16,'cls'=8] {'cls'}, dimensions={0} | all-to-all | bytes 7340032 | tf_op jit(solution)/shard_map/all_to_all | solution.py:25
  117.1 0.6 convert_element_type.99
  117.8 0.4 slice_reduce_fusion
  118.2 0.7 convert_dynamic-update-slice_fusion.2
  118.9 0.7 fusion.27
  119.6 0.7 convert_dynamic-update-slice_fusion.1
  120.3 0.6 constant_dynamic-update-slice_fusion.1
  120.9 0.6 fusion.29
  121.5 9.8 %all-to-all-start.2 = ((bf16[16,8,1792]{2,1,0:T(8,128)(2,1)}), bf16[16,8,1792]{2,1,0:T(8,128)(2,1)}, u32[]{:S(2)}, u32[]{:S(2)}) async-start(bf16[16,8,1792]{2,1,0:T(8,128)(2,1)} %fusion.29), calls=%async_computation.2 | async-start | bytes 917504 | tf_op jit(solution)/shard_map/all_to_all | solution.py:25
  131.4 0.3 slice_convert_fusion
  131.7 12.9 %all-to-all-done.2 = bf16[16,8,1792]{2,1,0:T(8,128)(2,1)} async-done(((bf16[16,8,1792]{2,1,0:T(8,128)(2,1)}), bf16[16,8,1792]{2,1,0:T(8,128)(2,1)}, u32[]{:S(2)}, u32[]{:S(2)}) %all-to-all-start.2) | async-done | bytes 458784 | tf_op jit(solution)/shard_map/all_to_all | solution.py:25
  144.6 1.1 convert_element_type.107
  145.7 3.2 %collective-permute-start.3 = (f32[64]{0:T(128)S(1)}, f32[64]{0:T(128)S(1)}, u32[]{:S(2)}, u32[]{:S(2)}) collective-permute-start(f32[64]{0:T(128)S(1)} %get-tuple-element.11), channel_id=1, source_target_pairs={{0,128},{128,0},{1,129},{129,1},{2,130},{130,2},{3,131},{131,3},{4... | collective-permute-start | bytes 776 | tf_op jit(solution)/shard_map/ppermute | solution.py:115
  149.3 3.4 %collective-permute-start.2 = (f32[8,512]{1,0:T(8,128)S(1)}, f32[8,512]{1,0:T(8,128)S(1)}, u32[]{:S(2)}, u32[]{:S(2)}) collective-permute-start(f32[8,512]{1,0:T(8,128)S(1)} %subtract_divide_fusion), channel_id=1, source_target_pairs={{8,128},{24,144},{40,160},{56,176},{72,192},{88,208},{104,224},{12... | collective-permute-start | bytes 49160 | tf_op jit(solution)/shard_map/ppermute | solution.py:139
  152.8 0.6 fusion.32
  153.4 1.0 collective-permute-done.2
  154.4 0.6 broadcast_select_fusion.1
  (50 shorter events, 2.6 us)
Async XLA Ops:
  0.6 1.2 copy-start
  0.6 14.3 %copy-start.1 = (s32[1,1536]{1,0:T(1,128)S(1)}, s32[1,1536]{1,0:T(1,128)}, u32[]{:S(2)}) copy-start(s32[1,1536]{1,0:T(1,128)} %param.6) | copy-start | bytes 18436
  3.2 44.0 %all-to-all-start = ((bf16[16,64,640]{2,1,0:T(8,128)(2,1)}), bf16[16,64,640]{2,1,0:T(8,128)(2,1)S(1)}, u32[]{:S(2)}, u32[]{:S(2)}) async-start(bf16[16,64,640]{2,1,0:T(8,128)(2,1)} %broadcast_in_dim.23), calls=%async_computation | async-start | bytes 2621440 | tf_op jit(solution)/shard_map/all_to_all | solution.py:56
  25.4 22.6 %collective-permute-start = (bf16[1536,512]{1,0:T(8,128)(2,1)}, bf16[1536,512]{1,0:T(8,128)(2,1)}, u32[]{:S(2)}, u32[]{:S(2)}) collective-permute-start(bf16[1536,512]{1,0:T(8,128)(2,1)} %fusion.9), channel_id=1, source_target_pairs={{0,128},{128,0},{1,129},{129,1},{2,130},{130,2},{3,131},{131,3},{4... | collective-permute-start | bytes 4718600 | tf_op jit(solution)/shard_map/ppermute | solution.py:68
  26.3 3.4 %collective-permute-start.1 = (s32[1536]{0:T(1024)S(1)}, s32[1536]{0:T(1024)S(1)}, u32[]{:S(2)}, u32[]{:S(2)}) collective-permute-start(s32[1536]{0:T(1024)S(1)} %broadcast_add_fusion), channel_id=1, source_target_pairs={{0,128},{128,0},{1,129},{129,1},{2,130},{130,2},{3,131},{131,3},{4... | collective-permute-start | bytes 18440 | tf_op jit(solution)/shard_map/ppermute | solution.py:69
  121.5 23.0 %all-to-all-start.2 = ((bf16[16,8,1792]{2,1,0:T(8,128)(2,1)}), bf16[16,8,1792]{2,1,0:T(8,128)(2,1)}, u32[]{:S(2)}, u32[]{:S(2)}) async-start(bf16[16,8,1792]{2,1,0:T(8,128)(2,1)} %fusion.29), calls=%async_computation.2 | async-start | bytes 917504 | tf_op jit(solution)/shard_map/all_to_all | solution.py:25
  145.7 7.0 %collective-permute-start.3 = (f32[64]{0:T(128)S(1)}, f32[64]{0:T(128)S(1)}, u32[]{:S(2)}, u32[]{:S(2)}) collective-permute-start(f32[64]{0:T(128)S(1)} %get-tuple-element.11), channel_id=1, source_target_pairs={{0,128},{128,0},{1,129},{129,1},{2,130},{130,2},{3,131},{131,3},{4... | collective-permute-start | bytes 776 | tf_op jit(solution)/shard_map/ppermute | solution.py:115
  148.9 3.8 %collective-permute-start.4 = (f32[64]{0:T(128)S(1)}, f32[64]{0:T(128)S(1)}, u32[]{:S(2)}, u32[]{:S(2)}) collective-permute-start(f32[64]{0:T(128)S(1)} %get-tuple-element.10), channel_id=1, source_target_pairs={{0,128},{128,0},{1,129},{129,1},{2,130},{130,2},{3,131},{131,3},{4... | collective-permute-start | bytes 776 | tf_op jit(solution)/shard_map/ppermute | solution.py:115
  149.3 5.1 %collective-permute-start.2 = (f32[8,512]{1,0:T(8,128)S(1)}, f32[8,512]{1,0:T(8,128)S(1)}, u32[]{:S(2)}, u32[]{:S(2)}) collective-permute-start(f32[8,512]{1,0:T(8,128)S(1)} %subtract_divide_fusion), channel_id=1, source_target_pairs={{8,128},{24,144},{40,160},{56,176},{72,192},{88,208},{104,224},{12... | collective-permute-start | bytes 49160 | tf_op jit(solution)/shard_map/ppermute | solution.py:139

commit v7 on v6

--- a/solution.py
+++ b/solution.py
@@ -10,9 +10,9 @@
 
 
 def split_pair(values):
-    high = values.astype(jnp.bfloat16)
-    low = (values - high.astype(jnp.float32)).astype(jnp.bfloat16)
-    return high, low
+    high = lax.reduce_precision(values, exponent_bits=8, mantissa_bits=7)
+    low = (values - high).astype(jnp.bfloat16)
+    return high.astype(jnp.bfloat16), low
 
 
 def reduce_stage(unscaled, own_center, extra, axis):

time: 155 us -> 156 us (level)
  no operation moved by 1% of the time
where the time goes in v7:
time: 156 us; the launch traced here: 155 us
  blocking collectives  44.4 us (28%)
  waiting for transfers between devices  34.6 us (22%)
  starting transfers between devices  29.2 us (19%)
  matrix products  23 us (15%)
  other arithmetic  12 us (8%)
  local copies, waits for them, and re-layouts  10.9 us (7%)
    all_to_all x1, blocking collectives, reduce_stage(): packed = lax.all_to_all(packed, axis, 0, 0, tiled=False).astype(jnp.float32)  44.4 us
    all_to_all x1, waiting for transfers between devices, on_device(): lax.all_to_all(jnp.broadcast_to(packed[None], (batch_count,) + packed.sha...  17.4 us
    all_to_all x1, waiting for transfers between devices, reduce_stage(): packed = lax.all_to_all(packed, axis, 0, 0, tiled=False).astype(jnp.float32)  12.9 us
    all_to_all x1, starting transfers between devices, on_device(): lax.all_to_all(jnp.broadcast_to(packed[None], (batch_count,) + packed.sha...  11.7 us
    dot_general x1, matrix products, on_device(): lax.dot_general(unit_rows, both_centers, (((1,), (1,)), ((), ())), prefer...  10.1 us
    all_to_all x1, starting transfers between devices, reduce_stage(): packed = lax.all_to_all(packed, axis, 0, 0, tiled=False).astype(jnp.float32)  9.77 us
    gather x1, local copies, waits for them, and re-layouts, on_device(): chosen = jnp.take(centers, local_ids, axis=0).astype(jnp.float32)  7.59 us
    dot_general x1, matrix products, on_device(): jnp.dot(weights, both_centers, preferred_element_type=jnp.float32)  7.57 us
  transfers between devices with their start and end apart: 7, of which 4 were waited for; matrix products, arithmetic and copies ran while one was open for 8% of the time, Pallas kernels for 0%

profile of v7, /device:TPU:1, one launch (start us, length us, event | category | flops | bytes accessed | tf_op | source)
XLA Modules:
  0.0 155.1 jit_solution(9567964359326111223)
XLA Ops:
  0.7 0.8 fusion.40
  2.0 1.2 broadcast_in_dim.23
  3.2 11.7 %all-to-all-start = ((bf16[16,64,640]{2,1,0:T(8,128)(2,1)}), bf16[16,64,640]{2,1,0:T(8,128)(2,1)S(1)}, u32[]{:S(2)}, u32[]{:S(2)}) async-start(bf16[16,64,640]{2,1,0:T(8,128)(2,1)} %broadcast_in_dim.23), calls=%async_computation | async-start | bytes 2621440 | tf_op jit(solution)/shard_map/all_to_all | solution.py:56
  15.0 7.6 %gather_fusion = bf16[1536,512]{1,0:T(8,128)(2,1)S(1)} fusion(bf16[4096,512]{1,0:T(8,128)(2,1)} %param.5, s32[2048]{0:T(1024)S(1)} %pad_clamp_fusion), kind=kCustom, calls=%fused_computation | custom fusion | bytes 3151872 | tf_op jit(solution)/shard_map/jit(_take)/gather | solution.py:64
  22.6 0.8 fusion.8
  23.4 2.0 %fusion.9 = bf16[1536,512]{1,0:T(8,128)(2,1)} fusion(f32[1536]{0:T(1024)S(1)} %add_sqrt_fusion, bf16[1536,512]{1,0:T(8,128)(2,1)S(1)} %gather_fusion, pred[1536]{0:T(1024)(128)(4,1)S(1)} %compare_and_fusion), kind=kLoop, calls=%fused_computation.16 | loop fusion | flops 3145728 | bytes 3153408 | tf_op jit(solution)/shard_map/convert_element_type | solution.py:66
  25.4 1.0 collective-permute-start
  26.4 3.3 %collective-permute-done.1 = s32[1536]{0:T(1024)S(1)} collective-permute-done((s32[1536]{0:T(1024)S(1)}, s32[1536]{0:T(1024)S(1)}, u32[]{:S(2)}, u32[]{:S(2)}) %collective-permute-start.1) | collective-permute-done | bytes 6176 | tf_op jit(solution)/shard_map/ppermute | solution.py:69
  29.7 17.4 %all-to-all-done = bf16[16,64,640]{2,1,0:T(8,128)(2,1)S(1)} async-done(((bf16[16,64,640]{2,1,0:T(8,128)(2,1)}), bf16[16,64,640]{2,1,0:T(8,128)(2,1)S(1)}, u32[]{:S(2)}, u32[]{:S(2)}) %all-to-all-start) | async-done | bytes 1310752 | tf_op jit(solution)/shard_map/all_to_all | solution.py:56
  47.2 0.5 fusion.22
  47.7 0.3 multiply_reduce_fusion
  48.0 10.1 %fusion.3 = (f32[1024]{0:T(1024)S(1)}, f32[1024]{0:T(1024)S(1)}, f32[1024,3072]{1,0:T(8,128)}) fusion(s32[3072]{0:T(1024)S(1)} %pad_add_fusion, s32[1024]{0:T(1024)S(1)} %fusion.22, bf16[1536,512]{1,0:T(8,128)(2,1)} %collective-permute-done, bf16[1536,512]{1,0:T(8,128)(2,1)} %fusion.9, f32[1024]{0:T(1024)S(1)} %add_sqrt_fusion.1, ...), kind=kOutput, calls=%fused_computation.6 | convolution fusion | flops 3251107840 | bytes 16805888 | tf_op jit(solution)/shard_map/dot_general | solution.py:76
  58.4 7.6 %fusion.5 = f32[1024,512]{1,0:T(8,128)S(1)} fusion(f32[1024,3072]{1,0:T(8,128)} %get-tuple-element.13, s32[3072]{0:T(1024)S(1)} %pad_add_fusion, s32[1024]{0:T(1024)S(1)} %fusion.22, bf16[1536,512]{1,0:T(8,128)(2,1)} %collective-permute-done, bf16[1536,512]{1,0:T(8,128)(2,1)} %fusion.9), kind=kOutput, calls=%fused_computation.10 | convolution fusion | flops 3243245568 | bytes 17842176 | tf_op jit(solution)/shard_map/dot_general | solution.py:85
  66.3 0.4 fusion.16
  66.7 5.3 %fusion.12 = bf16[1024,512]{1,0:T(8,128)(2,1)S(1)} fusion(s32[3072]{0:T(1024)S(1)} %pad_add_fusion, s32[1024]{0:T(1024)S(1)} %fusion.22, bf16[1536,512]{1,0:T(8,128)(2,1)} %collective-permute-done, bf16[1536,512]{1,0:T(8,128)(2,1)} %fusion.9), kind=kOutput, calls=%fused_computation.27 | convolution fusion | flops 3231186944 | bytes 4210688 | tf_op jit(solution)/shard_map/dot_general | solution.py:86
  72.9 44.4 %all_to_all.15 = bf16[8,16,8,1792]{3,2,1,0:T(8,128)(2,1)S(1)} all-to-all(bf16[8,16,8,1792]{3,2,1,0:T(8,128)(2,1)S(1)} %fusion.24), channel_id=1, replica_groups=mesh['section'=2,'dp'=16,'cls'=8] {'cls'}, dimensions={0} | all-to-all | bytes 7340032 | tf_op jit(solution)/shard_map/all_to_all | solution.py:25
  117.2 0.6 convert_element_type.85
  117.9 0.4 slice_reduce_fusion
  118.3 0.7 fusion.29
  119.0 0.7 fusion.28
  119.7 0.7 convert_dynamic-update-slice_fusion
  120.4 0.6 fusion.33
  121.0 0.6 fusion.32
  121.6 9.8 %all-to-all-start.2 = ((bf16[16,8,1792]{2,1,0:T(8,128)(2,1)}), bf16[16,8,1792]{2,1,0:T(8,128)(2,1)}, u32[]{:S(2)}, u32[]{:S(2)}) async-start(bf16[16,8,1792]{2,1,0:T(8,128)(2,1)} %fusion.32), calls=%async_computation.2 | async-start | bytes 917504 | tf_op jit(solution)/shard_map/all_to_all | solution.py:25
  131.5 0.3 slice_convert_fusion
  131.8 12.9 %all-to-all-done.2 = bf16[16,8,1792]{2,1,0:T(8,128)(2,1)} async-done(((bf16[16,8,1792]{2,1,0:T(8,128)(2,1)}), bf16[16,8,1792]{2,1,0:T(8,128)(2,1)}, u32[]{:S(2)}, u32[]{:S(2)}) %all-to-all-start.2) | async-done | bytes 458784 | tf_op jit(solution)/shard_map/all_to_all | solution.py:25
  144.7 1.1 convert_element_type.91
  145.8 3.2 %collective-permute-start.3 = (f32[64]{0:T(128)S(1)}, f32[64]{0:T(128)S(1)}, u32[]{:S(2)}, u32[]{:S(2)}) collective-permute-start(f32[64]{0:T(128)S(1)} %get-tuple-element.11), channel_id=1, source_target_pairs={{0,128},{128,0},{1,129},{129,1},{2,130},{130,2},{3,131},{131,3},{4... | collective-permute-start | bytes 776 | tf_op jit(solution)/shard_map/ppermute | solution.py:115
  149.4 3.4 %collective-permute-start.2 = (f32[8,512]{1,0:T(8,128)S(1)}, f32[8,512]{1,0:T(8,128)S(1)}, u32[]{:S(2)}, u32[]{:S(2)}) collective-permute-start(f32[8,512]{1,0:T(8,128)S(1)} %subtract_divide_fusion), channel_id=1, source_target_pairs={{8,128},{24,144},{40,160},{56,176},{72,192},{88,208},{104,224},{12... | collective-permute-start | bytes 49160 | tf_op jit(solution)/shard_map/ppermute | solution.py:139
  152.9 0.6 fusion.36
  153.5 1.0 collective-permute-done.2
  154.5 0.6 broadcast_select_fusion.1
  (50 shorter events, 2.6 us)
Async XLA Ops:
  0.6 1.2 copy-start
  0.6 14.3 %copy-start.1 = (s32[1,1536]{1,0:T(1,128)S(1)}, s32[1,1536]{1,0:T(1,128)}, u32[]{:S(2)}) copy-start(s32[1,1536]{1,0:T(1,128)} %param.6) | copy-start | bytes 18436
  3.2 44.0 %all-to-all-start = ((bf16[16,64,640]{2,1,0:T(8,128)(2,1)}), bf16[16,64,640]{2,1,0:T(8,128)(2,1)S(1)}, u32[]{:S(2)}, u32[]{:S(2)}) async-start(bf16[16,64,640]{2,1,0:T(8,128)(2,1)} %broadcast_in_dim.23), calls=%async_computation | async-start | bytes 2621440 | tf_op jit(solution)/shard_map/all_to_all | solution.py:56
  25.4 22.6 %collective-permute-start = (bf16[1536,512]{1,0:T(8,128)(2,1)}, bf16[1536,512]{1,0:T(8,128)(2,1)}, u32[]{:S(2)}, u32[]{:S(2)}) collective-permute-start(bf16[1536,512]{1,0:T(8,128)(2,1)} %fusion.9), channel_id=1, source_target_pairs={{0,128},{128,0},{1,129},{129,1},{2,130},{130,2},{3,131},{131,3},{4... | collective-permute-start | bytes 4718600 | tf_op jit(solution)/shard_map/ppermute | solution.py:68
  26.3 3.4 %collective-permute-start.1 = (s32[1536]{0:T(1024)S(1)}, s32[1536]{0:T(1024)S(1)}, u32[]{:S(2)}, u32[]{:S(2)}) collective-permute-start(s32[1536]{0:T(1024)S(1)} %broadcast_add_fusion), channel_id=1, source_target_pairs={{0,128},{128,0},{1,129},{129,1},{2,130},{130,2},{3,131},{131,3},{4... | collective-permute-start | bytes 18440 | tf_op jit(solution)/shard_map/ppermute | solution.py:69
  121.6 23.0 %all-to-all-start.2 = ((bf16[16,8,1792]{2,1,0:T(8,128)(2,1)}), bf16[16,8,1792]{2,1,0:T(8,128)(2,1)}, u32[]{:S(2)}, u32[]{:S(2)}) async-start(bf16[16,8,1792]{2,1,0:T(8,128)(2,1)} %fusion.32), calls=%async_computation.2 | async-start | bytes 917504 | tf_op jit(solution)/shard_map/all_to_all | solution.py:25
  145.8 7.0 %collective-permute-start.3 = (f32[64]{0:T(128)S(1)}, f32[64]{0:T(128)S(1)}, u32[]{:S(2)}, u32[]{:S(2)}) collective-permute-start(f32[64]{0:T(128)S(1)} %get-tuple-element.11), channel_id=1, source_target_pairs={{0,128},{128,0},{1,129},{129,1},{2,130},{130,2},{3,131},{131,3},{4... | collective-permute-start | bytes 776 | tf_op jit(solution)/shard_map/ppermute | solution.py:115
  149.1 3.8 %collective-permute-start.4 = (f32[64]{0:T(128)S(1)}, f32[64]{0:T(128)S(1)}, u32[]{:S(2)}, u32[]{:S(2)}) collective-permute-start(f32[64]{0:T(128)S(1)} %get-tuple-element.10), channel_id=1, source_target_pairs={{0,128},{128,0},{1,129},{129,1},{2,130},{130,2},{3,131},{131,3},{4... | collective-permute-start | bytes 776 | tf_op jit(solution)/shard_map/ppermute | solution.py:115
  149.4 5.1 %collective-permute-start.2 = (f32[8,512]{1,0:T(8,128)S(1)}, f32[8,512]{1,0:T(8,128)S(1)}, u32[]{:S(2)}, u32[]{:S(2)}) collective-permute-start(f32[8,512]{1,0:T(8,128)S(1)} %subtract_divide_fusion), channel_id=1, source_target_pairs={{8,128},{24,144},{40,160},{56,176},{72,192},{88,208},{104,224},{12... | collective-permute-start | bytes 49160 | tf_op jit(solution)/shard_map/ppermute | solution.py:139

commit v8 on v7

--- a/solution.py
+++ b/solution.py
@@ -7,6 +7,7 @@
 MARGIN = 0.35
 EPSILON = 1e-06
 EXTRA = 128
+CHUNKS = 2
 
 
 def split_pair(values):
@@ -45,7 +46,9 @@
     half = rows_per_batch // section_count
     devices = section_count * batch_count * class_count
     rows_here = rows_per_batch * batch_count // devices
-    assert half == class_count * rows_here and rows_here >= 3 and half <= EXTRA and rows_here <= EXTRA
+    piece = rows_here // CHUNKS
+    assert half == class_count * rows_here and rows_here % CHUNKS == 0 and piece >= 3
+    assert half <= EXTRA and rows_here <= EXTRA
 
     my_rows = lax.dynamic_slice_in_dim(embeddings, section * half, half, 0)
     my_labels = lax.dynamic_slice_in_dim(labels, section * half, half, 0)
@@ -73,54 +76,66 @@
     emb_float = gathered.astype(jnp.float32)
     row_norm = jnp.sqrt(jnp.sum(emb_float * emb_float, axis=1) + EPSILON)
     unit_rows = (emb_float / row_norm[:, None]).astype(jnp.bfloat16)
-    cosine = lax.dot_general(
-        unit_rows, both_centers, (((1,), (1,)), ((), ())), preferred_element_type=jnp.float32
-    )
-    matches = both_ids[None, :] == label_all[:, None]
-    logits = LOGIT_SCALE * cosine - LOGIT_SCALE * MARGIN * matches.astype(jnp.float32)
-    exponent = jnp.exp(logits)
-    total_part = jnp.sum(exponent, axis=1)
-    target_part = jnp.sum(jnp.where(matches, logits, jnp.float32(0.0)), axis=1)
-    weights = exponent.astype(jnp.bfloat16)
-    unscaled = jnp.dot(weights, both_centers, preferred_element_type=jnp.float32)
-    own_center = jnp.dot(matches.astype(jnp.bfloat16), both_centers, preferred_element_type=jnp.float32)
-
     h = batch_count // 2
-
-    def to_dest(values):
-        tail = values.shape[1:]
-        values = values.reshape((2, h, class_count, rows_here) + tail)
-        values = jnp.moveaxis(values, 2, 0)
-        values = jnp.swapaxes(values, 1, 2)
-        return values.reshape((class_count, batch_count, rows_here) + tail)
 
     def pad(values):
         return jnp.pad(values, [(0, 0)] * (values.ndim - 1) + [(0, EXTRA - values.shape[-1])])
 
-    block_rows = jnp.broadcast_to(
-        jnp.stack([pad(total_part.reshape(batch_count, half)), pad(target_part.reshape(batch_count, half))], axis=1)[None],
-        (class_count, batch_count, 2, EXTRA),
-    )
-    own_totals = pad(to_dest(total_part))[:, :, None, :]
-    extra = jnp.concatenate(
-        [block_rows, own_totals, jnp.zeros((class_count, batch_count, rows_here - 3, EXTRA), jnp.float32)], axis=2
-    )
-    unscaled, own_center, extra = to_dest(unscaled), to_dest(own_center), extra
-    for axis in ("cls", "dp"):
-        unscaled, own_center, extra = reduce_stage(unscaled, own_center, extra, axis)
-    summed = jnp.concatenate([unscaled, own_center, extra], axis=-1)
+    def to_dest(values):
+        tail = values.shape[3:]
+        values = values.reshape((2, h, class_count, piece) + tail)
+        values = jnp.moveaxis(values, 2, 0)
+        values = jnp.swapaxes(values, 1, 2)
+        return values.reshape((class_count, batch_count, piece) + tail)
 
-    half_total = summed[0, 2 * width : 2 * width + half]
-    half_target = summed[1, 2 * width : 2 * width + half]
+    row_view = unit_rows.reshape(batch_count, class_count, rows_here, width)
+    label_view = label_all.reshape(batch_count, class_count, rows_here)
+    results = []
+    for k in range(CHUNKS):
+        chunk_rows = row_view[:, :, k * piece : (k + 1) * piece].reshape(-1, width)
+        chunk_labels = label_view[:, :, k * piece : (k + 1) * piece].reshape(-1)
+        cosine = lax.dot_general(
+            chunk_rows, both_centers, (((1,), (1,)), ((), ())), preferred_element_type=jnp.float32
+        )
+        matches = both_ids[None, :] == chunk_labels[:, None]
+        logits = LOGIT_SCALE * cosine - LOGIT_SCALE * MARGIN * matches.astype(jnp.float32)
+        exponent = jnp.exp(logits)
+        total_part = jnp.sum(exponent, axis=1)
+        target_part = jnp.sum(jnp.where(matches, logits, jnp.float32(0.0)), axis=1)
+        weights = exponent.astype(jnp.bfloat16)
+        unscaled = jnp.dot(weights, both_centers, preferred_element_type=jnp.float32)
+        own_center = jnp.dot(matches.astype(jnp.bfloat16), both_centers, preferred_element_type=jnp.float32)
+        shape4 = (batch_count, class_count, piece)
+        block_rows = jnp.broadcast_to(
+            jnp.stack(
+                [pad(total_part.reshape(batch_count, -1)), pad(target_part.reshape(batch_count, -1))], axis=1
+            )[None],
+            (class_count, batch_count, 2, EXTRA),
+        )
+        own_totals = pad(to_dest(total_part.reshape(shape4)))[:, :, None, :]
+        extra = jnp.concatenate(
+            [block_rows, own_totals, jnp.zeros((class_count, batch_count, piece - 3, EXTRA), jnp.float32)], axis=2
+        )
+        parts = (to_dest(unscaled.reshape(shape4 + (width,))), to_dest(own_center.reshape(shape4 + (width,))), extra)
+        for axis in ("cls", "dp"):
+            parts = reduce_stage(*parts, axis)
+        results.append(parts)
+
+    def block_values(row):
+        per_chunk = [r[2][row, : class_count * piece].reshape(class_count, piece) for r in results]
+        return jnp.concatenate(per_chunk, axis=1).reshape(-1)
+
+    half_total = block_values(0)
+    half_target = block_values(1)
     other_total, other_target = lax.ppermute((half_total, half_target), "section", swap)
     first = section == 0
     block_total = jnp.where(first, jnp.concatenate([half_total, other_total]), jnp.concatenate([other_total, half_total]))
     block_target = jnp.where(first, jnp.concatenate([half_target, other_target]), jnp.concatenate([other_target, half_target]))
     row_loss = jnp.log(block_total) - block_target
 
-    unscaled_rows = summed[:, :width]
-    own_rows = summed[:, width : 2 * width]
-    totals_here = summed[2, 2 * width : 2 * width + rows_here]
+    unscaled_rows = jnp.concatenate([r[0] for r in results], axis=0)
+    own_rows = jnp.concatenate([r[1] for r in results], axis=0)
+    totals_here = jnp.concatenate([r[2][2, :piece] for r in results], axis=0)
     unit_grad = LOGIT_SCALE * (unscaled_rows / totals_here[:, None] - own_rows)
     source_batch = (batch % 2) * h + batch // 2
     offset = source_batch * half + cls * rows_here
@@ -136,8 +151,8 @@
         for e in range(batch_count)
         if e % 2 != s
     ]
-    received = lax.ppermute(computed, ("section", "dp"), pairs)
-    feature_grad = jnp.where(batch % 2 == section, computed, received)
+    received_grad = lax.ppermute(computed, ("section", "dp"), pairs)
+    feature_grad = jnp.where(batch % 2 == section, computed, received_grad)
     return (feature_grad, row_loss)
 
 

time: 156 us -> 216 us (1.38)
  blocking collectives: 44.4 us -> 0 us
  waiting for transfers between devices: 34.6 us -> 78.4 us
  local copies, waits for them, and re-layouts: 10.9 us -> 35.6 us
  starting transfers between devices: 29.2 us -> 44.8 us
  matrix products: 23 us -> 33.1 us
  other arithmetic: 12 us -> 21.4 us
    all_to_all x1 -> x4, waiting for transfers between devices: 12.9 us -> 57.5 us  [reduce_stage(): packed = lax.all_to_all(packed, axis, 0, 0, tiled=False).astype(jnp.float32)]
    all_to_all x1 -> x0, blocking collectives: 44.4 us -> none  [reduce_stage(): packed = lax.all_to_all(packed, axis, 0, 0, tiled=False).astype(jnp.float32)]
    all_to_all x1 -> x4, starting transfers between devices: 9.77 us -> 23.5 us  [reduce_stage(): packed = lax.all_to_all(packed, axis, 0, 0, tiled=False).astype(jnp.float32)]
    concatenate x0 -> x2, local copies, waits for them, and re-layouts: none -> 5.41 us  [reduce_stage(): jnp.concatenate([unscaled_high, unscaled_low, own_center.astype(jnp.bfloa...]
    unnamed x6 -> x26, local copies, waits for them, and re-layouts: 0.76 us -> 5.19 us
    dot_general x1 -> x2, matrix products: 7.57 us -> 11.9 us  [on_device(): jnp.dot(weights, both_centers, preferred_element_type=jnp.float32)]
    another operation x0 -> x10, local copies, waits for them, and re-layouts: none -> 4.27 us  [the longest x6 3.97 us: to_dest(): values = values.reshape((2, h, class_count, piece) + tail)]
    dot_general x1 -> x2, matrix products: 10.1 us -> 13.8 us  [on_device(): lax.dot_general(chunk_rows, both_centers, (((1,), (1,)), ((), ())), prefe...]
  transfers between devices with their start and end apart: 7 -> 10, of which waited for: 4 -> 6; matrix products, arithmetic and copies ran while one was open for 8% -> 12% of each run, Pallas kernels for 0% -> 0%
where the time goes in v8:
time: 216 us; the launch traced here: 214 us
  waiting for transfers between devices  78.4 us (36%)
  starting transfers between devices  44.8 us (21%)
  local copies, waits for them, and re-layouts  35.6 us (16%)
  matrix products  33.1 us (15%)
  other arithmetic  21.4 us (10%)
    all_to_all x4, waiting for transfers between devices, reduce_stage(): packed = lax.all_to_all(packed, axis, 0, 0, tiled=False).astype(jnp.float32)  57.5 us
    all_to_all x4, starting transfers between devices, reduce_stage(): packed = lax.all_to_all(packed, axis, 0, 0, tiled=False).astype(jnp.float32)  23.5 us
    all_to_all x1, waiting for transfers between devices, on_device(): lax.all_to_all(jnp.broadcast_to(packed[None], (batch_count,) + packed.sha...  20.1 us
    dot_general x2, matrix products, on_device(): lax.dot_general(chunk_rows, both_centers, (((1,), (1,)), ((), ())), prefe...  13.8 us
    dot_general x2, matrix products, on_device(): jnp.dot(weights, both_centers, preferred_element_type=jnp.float32)  11.9 us
    all_to_all x1, starting transfers between devices, on_device(): lax.all_to_all(jnp.broadcast_to(packed[None], (batch_count,) + packed.sha...  11.7 us
    gather x1, local copies, waits for them, and re-layouts, on_device(): chosen = jnp.take(centers, local_ids, axis=0).astype(jnp.float32)  7.59 us
    dot_general x2, matrix products, on_device(): jnp.dot(matches.astype(jnp.bfloat16), both_centers, preferred_element_typ...  7.42 us
  transfers between devices with their start and end apart: 10, of which 6 were waited for; matrix products, arithmetic and copies ran while one was open for 12% of the time, Pallas kernels for 0%

profile of v8, /device:TPU:1, one launch (start us, length us, event | category | flops | bytes accessed | tf_op | source)
XLA Modules:
  0.0 214.5 jit_solution(18047957451786108256)
XLA Ops:
  2.0 1.2 broadcast_in_dim.26
  3.2 11.7 %all-to-all-start = ((bf16[16,64,640]{2,1,0:T(8,128)(2,1)}), bf16[16,64,640]{2,1,0:T(8,128)(2,1)S(1)}, u32[]{:S(2)}, u32[]{:S(2)}) async-start(bf16[16,64,640]{2,1,0:T(8,128)(2,1)} %broadcast_in_dim.26), calls=%async_computation | async-start | bytes 2621440 | tf_op jit(solution)/shard_map/all_to_all | solution.py:59
  16.1 7.6 %gather_fusion = bf16[1536,512]{1,0:T(8,128)(2,1)S(1)} fusion(bf16[4096,512]{1,0:T(8,128)(2,1)} %param.5, s32[2048]{0:T(1024)S(1)} %pad_clamp_fusion), kind=kCustom, calls=%fused_computation | custom fusion | bytes 3151872 | tf_op jit(solution)/shard_map/jit(_take)/gather | solution.py:67
  24.5 2.0 fusion.9
  27.1 20.1 %all-to-all-done = bf16[16,64,640]{2,1,0:T(8,128)(2,1)S(1)} async-done(((bf16[16,64,640]{2,1,0:T(8,128)(2,1)}), bf16[16,64,640]{2,1,0:T(8,128)(2,1)S(1)}, u32[]{:S(2)}, u32[]{:S(2)}) %all-to-all-start) | async-done | bytes 1310752 | tf_op jit(solution)/shard_map/all_to_all | solution.py:59
  49.8 3.7 %fusion.6 = f32[512,3072]{1,0:T(8,128)S(1)} fusion(bf16[512,512]{1,0:T(8,128)(2,1)S(1)} %reshape.120, s32[3072]{0:T(1024)S(1)} %pad_add_fusion, s32[512]{0:T(512)S(1)} %eq.45, bf16[1536,512]{1,0:T(8,128)(2,1)} %collective-permute-done, bf16[1536,512]{1,0:T(8,128)(2,1)} %fusion.9), kind=kOutput, calls=%fused_computation.11 | convolution fusion | flops 1623195648 | bytes 9975808 | tf_op jit(solution)/shard_map/dot_general | solution.py:97
  53.6 10.0 %fusion.5 = (f32[512]{0:T(512)}, f32[512]{0:T(512)S(1)}, f32[512]{0:T(512)S(1)}, f32[512]{0:T(512)}, f32[512,3072]{1,0:T(8,128)}) fusion(s32[3072]{0:T(1024)S(1)} %pad_add_fusion, s32[512]{0:T(512)S(1)} %eq.42, f32[512,3072]{1,0:T(8,128)S(1)} %fusion.6, s32[512]{0:T(512)S(1)} %eq.45, bf16[512,512]{1,0:T(8,128)(2,1)S(1)} %reshape.115, ...), kind=kOutput, calls=%fused_computation.10 | convolution fusion | flops 1634203648 | bytes 16277504 | tf_op jit(solution)/shard_map/dot_general | solution.py:97
  65.2 3.7 %fusion.16 = bf16[512,512]{1,0:T(8,128)(2,1)S(1)} fusion(s32[3072]{0:T(1024)S(1)} %pad_add_fusion, s32[512]{0:T(512)S(1)} %eq.42, bf16[1536,512]{1,0:T(8,128)(2,1)} %collective-permute-done, bf16[1536,512]{1,0:T(8,128)(2,1)} %fusion.9), kind=kOutput, calls=%fused_computation.35 | convolution fusion | flops 1618739200 | bytes 3684352 | tf_op jit(solution)/shard_map/dot_general | solution.py:107
  69.9 3.7 %fusion.19 = bf16[512,512]{1,0:T(8,128)(2,1)S(1)} fusion(s32[3072]{0:T(1024)S(1)} %pad_add_fusion, s32[512]{0:T(512)S(1)} %eq.45, bf16[1536,512]{1,0:T(8,128)(2,1)} %collective-permute-done, bf16[1536,512]{1,0:T(8,128)(2,1)} %fusion.9), kind=kOutput, calls=%fused_computation.36 | convolution fusion | flops 1618739200 | bytes 3684352 | tf_op jit(solution)/shard_map/dot_general | solution.py:107
  74.7 5.5 %fusion.10 = f32[512,512]{1,0:T(8,128)S(1)} fusion(f32[512,3072]{1,0:T(8,128)} %get-tuple-element.33, bf16[1536,512]{1,0:T(8,128)(2,1)} %collective-permute-done, bf16[1536,512]{1,0:T(8,128)(2,1)} %fusion.9), kind=kOutput, calls=%fused_computation.21 | convolution fusion | flops 1618477056 | bytes 10485760 | tf_op jit(solution)/shard_map/dot_general | solution.py:106
  80.8 6.5 %fusion.11 = f32[512,512]{1,0:T(8,128)} fusion(f32[512,3072]{1,0:T(8,128)} %copy-done.8, bf16[1536,512]{1,0:T(8,128)(2,1)} %collective-permute-done, bf16[1536,512]{1,0:T(8,128)(2,1)} %fusion.9), kind=kOutput, calls=%fused_computation.22 | convolution fusion | flops 1618477056 | bytes 10485760 | tf_op jit(solution)/shard_map/dot_general | solution.py:106
  87.3 1.5 reshape_reshape.16
  90.1 1.1 fusion.22
  91.3 1.4 reshape.118
  92.7 1.3 pad.21
  94.0 1.3 reshape.123
  97.7 1.1 constant_dynamic-update-slice_fusion.2
  101.2 1.2 copy-done.1
  102.6 2.0 copy.51
  104.6 4.1 %all-to-all-start.3 = ((bf16[8,16,4,1792]{3,2,1,0:T(4,128)(2,1)}), bf16[8,16,4,1792]{3,2,1,0:T(4,128)(2,1)S(1)}, u32[]{:S(2)}, u32[]{:S(2)}) async-start(bf16[8,16,4,1792]{3,2,1,0:T(4,128)(2,1)} %copy.51), calls=%async_computation.3 | async-start | bytes 3670016 | tf_op jit(solution)/shard_map/all_to_all | solution.py:26
  108.7 3.4 %copy.46 = bf16[8,16,4,1792]{3,2,1,0:T(4,128)(2,1)} copy(bf16[8,16,4,1792]{3,0,2,1:T(8,128)(2,1)} %copy-done.1) | data formatting | bytes 3670016 | tf_op jit(solution)/shard_map/concatenate | solution.py:23
  112.2 21.1 %all-to-all-done.3 = bf16[8,16,4,1792]{3,2,1,0:T(4,128)(2,1)S(1)} async-done(((bf16[8,16,4,1792]{3,2,1,0:T(4,128)(2,1)}), bf16[8,16,4,1792]{3,2,1,0:T(4,128)(2,1)S(1)}, u32[]{:S(2)}, u32[]{:S(2)}) %all-to-all-start.3) | async-done | bytes 1835040 | tf_op jit(solution)/shard_map/all_to_all | solution.py:26
  133.2 4.5 %all-to-all-start.1 = ((bf16[8,16,4,1792]{3,2,1,0:T(4,128)(2,1)}), bf16[8,16,4,1792]{3,2,1,0:T(4,128)(2,1)}, u32[]{:S(2)}, u32[]{:S(2)}) async-start(bf16[8,16,4,1792]{3,2,1,0:T(4,128)(2,1)} %copy.46), calls=%async_computation.1 | async-start | bytes 3670016 | tf_op jit(solution)/shard_map/all_to_all | solution.py:26
  138.6 1.6 slice_convert_fusion
  141.2 21.6 %all-to-all-done.1 = bf16[8,16,4,1792]{3,2,1,0:T(4,128)(2,1)} async-done(((bf16[8,16,4,1792]{3,2,1,0:T(4,128)(2,1)}), bf16[8,16,4,1792]{3,2,1,0:T(4,128)(2,1)}, u32[]{:S(2)}, u32[]{:S(2)}) %all-to-all-start.1) | async-done | bytes 1835040 | tf_op jit(solution)/shard_map/all_to_all | solution.py:26
  162.8 2.0 convert_element_type.138
  168.4 10.7 %all-to-all-start.4 = ((bf16[16,4,1792]{2,1,0:T(4,128)(2,1)}), bf16[16,4,1792]{2,1,0:T(4,128)(2,1)S(1)}, u32[]{:S(2)}, u32[]{:S(2)}) async-start(bf16[16,4,1792]{2,1,0:T(4,128)(2,1)} %constant_dynamic-update-slice_fusion.8), calls=%async_computation.4 | async-start | bytes 458752 | tf_op jit(solution)/shard_map/all_to_all | solution.py:26
  182.3 5.9 %all-to-all-done.4 = bf16[16,4,1792]{2,1,0:T(4,128)(2,1)S(1)} async-done(((bf16[16,4,1792]{2,1,0:T(4,128)(2,1)}), bf16[16,4,1792]{2,1,0:T(4,128)(2,1)S(1)}, u32[]{:S(2)}, u32[]{:S(2)}) %all-to-all-start.4) | async-done | bytes 229408 | tf_op jit(solution)/shard_map/all_to_all | solution.py:26
  188.2 4.1 %all-to-all-start.2 = ((bf16[16,4,1792]{2,1,0:T(4,128)(2,1)}), bf16[16,4,1792]{2,1,0:T(4,128)(2,1)S(1)}, u32[]{:S(2)}, u32[]{:S(2)}) async-start(bf16[16,4,1792]{2,1,0:T(4,128)(2,1)} %constant_dynamic-update-slice_fusion.3), calls=%async_computation.2 | async-start | bytes 458752 | tf_op jit(solution)/shard_map/all_to_all | solution.py:26
  192.5 8.9 %all-to-all-done.2 = bf16[16,4,1792]{2,1,0:T(4,128)(2,1)S(1)} async-done(((bf16[16,4,1792]{2,1,0:T(4,128)(2,1)}), bf16[16,4,1792]{2,1,0:T(4,128)(2,1)S(1)}, u32[]{:S(2)}, u32[]{:S(2)}) %all-to-all-start.2) | async-done | bytes 229408 | tf_op jit(solution)/shard_map/all_to_all | solution.py:26
  202.2 4.6 %collective-permute-start.3 = (f32[64]{0:T(128)S(1)}, f32[64]{0:T(128)S(1)}, u32[]{:S(2)}, u32[]{:S(2)}) collective-permute-start(f32[64]{0:T(128)S(1)} %reshape.125), channel_id=1, source_target_pairs={{0,128},{128,0},{1,129},{129,1},{2,130},{130,2},{3,131},{131,3},{4... | collective-permute-start | bytes 776 | tf_op jit(solution)/shard_map/ppermute | solution.py:130
  208.7 3.8 %collective-permute-start.2 = (f32[8,512]{1,0:T(8,128)S(1)}, f32[8,512]{1,0:T(8,128)S(1)}, u32[]{:S(2)}, u32[]{:S(2)}) collective-permute-start(f32[8,512]{1,0:T(8,128)S(1)} %subtract_divide_fusion), channel_id=1, source_target_pairs={{8,128},{24,144},{40,160},{56,176},{72,192},{88,208},{104,224},{12... | collective-permute-start | bytes 49160 | tf_op jit(solution)/shard_map/ppermute | solution.py:154
  (123 shorter events, 30.1 us)
Async XLA Ops:
  0.6 1.2 copy-start
  0.6 14.3 %copy-start.5 = (s32[1,1536]{1,0:T(1,128)S(1)}, s32[1,1536]{1,0:T(1,128)}, u32[]{:S(2)}) copy-start(s32[1,1536]{1,0:T(1,128)} %param.6) | copy-start | bytes 18436
  3.2 44.0 %all-to-all-start = ((bf16[16,64,640]{2,1,0:T(8,128)(2,1)}), bf16[16,64,640]{2,1,0:T(8,128)(2,1)S(1)}, u32[]{:S(2)}, u32[]{:S(2)}) async-start(bf16[16,64,640]{2,1,0:T(8,128)(2,1)} %broadcast_in_dim.26), calls=%async_computation | async-start | bytes 2621440 | tf_op jit(solution)/shard_map/all_to_all | solution.py:59
  15.0 12.1 %collective-permute-start.1 = (s32[1536]{0:T(1024)S(1)}, s32[1536]{0:T(1024)S(1)}, u32[]{:S(2)}, u32[]{:S(2)}) collective-permute-start(s32[1536]{0:T(1024)S(1)} %broadcast_add_fusion), channel_id=1, source_target_pairs={{0,128},{128,0},{1,129},{129,1},{2,130},{130,2},{3,131},{131,3},{4... | collective-permute-start | bytes 18440 | tf_op jit(solution)/shard_map/ppermute | solution.py:72
  26.5 23.3 %collective-permute-start = (bf16[1536,512]{1,0:T(8,128)(2,1)}, bf16[1536,512]{1,0:T(8,128)(2,1)}, u32[]{:S(2)}, u32[]{:S(2)}) collective-permute-start(bf16[1536,512]{1,0:T(8,128)(2,1)} %fusion.9), channel_id=1, source_target_pairs={{0,128},{128,0},{1,129},{129,1},{2,130},{130,2},{3,131},{131,3},{4... | collective-permute-start | bytes 4718600 | tf_op jit(solution)/shard_map/ppermute | solution.py:71
  48.4 0.6 copy-start.6
  53.6 10.0 %copy-start.8 = (f32[512,3072]{1,0:T(8,128)}, f32[512,3072]{1,0:T(8,128)S(1)}, u32[]{:S(2)}) copy-start(f32[512,3072]{1,0:T(8,128)S(1)} %fusion.6) | copy-start | bytes 18874372
  90.1 10.6 %copy-start.2 = (bf16[2,8,8,4,512]{4,2,3,0,1:T(8,128)(2,1)S(1)}, bf16[2,8,8,4,512]{4,2,3,0,1:T(8,128)(2,1)}, u32[]{:S(2)}) copy-start(bf16[2,8,8,4,512]{4,2,3,0,1:T(8,128)(2,1)} %copy.44) | copy-start | bytes 1572868
  91.3 9.4 %copy-start.4 = (bf16[8,16,4,512]{3,0,2,1:T(8,128)(2,1)S(1)}, bf16[8,16,4,512]{3,0,2,1:T(8,128)(2,1)}, u32[]{:S(2)}) copy-start(bf16[8,16,4,512]{3,0,2,1:T(8,128)(2,1)} %get-tuple-element.22) | copy-start | bytes 1572868
  91.3 9.6 %copy-start.3 = (bf16[2,8,8,4,512]{4,2,3,0,1:T(8,128)(2,1)S(1)}, bf16[2,8,8,4,512]{4,2,3,0,1:T(8,128)(2,1)}, u32[]{:S(2)}) copy-start(bf16[2,8,8,4,512]{4,2,3,0,1:T(8,128)(2,1)} %copy.49) | copy-start | bytes 1572868
  97.7 3.2 %copy-start.7 = (f32[4]{0:T(128)S(1)}, f32[4]{0:T(128)}, u32[]{:S(2)}) copy-start(f32[4]{0:T(128)} %pad.51.clone) | copy-start | bytes 52
  101.2 1.3 copy-start.1
  104.6 28.7 %all-to-all-start.3 = ((bf16[8,16,4,1792]{3,2,1,0:T(4,128)(2,1)}), bf16[8,16,4,1792]{3,2,1,0:T(4,128)(2,1)S(1)}, u32[]{:S(2)}, u32[]{:S(2)}) async-start(bf16[8,16,4,1792]{3,2,1,0:T(4,128)(2,1)} %copy.51), calls=%async_computation.3 | async-start | bytes 3670016 | tf_op jit(solution)/shard_map/all_to_all | solution.py:26
  133.2 29.6 %all-to-all-start.1 = ((bf16[8,16,4,1792]{3,2,1,0:T(4,128)(2,1)}), bf16[8,16,4,1792]{3,2,1,0:T(4,128)(2,1)}, u32[]{:S(2)}, u32[]{:S(2)}) async-start(bf16[8,16,4,1792]{3,2,1,0:T(4,128)(2,1)} %copy.46), calls=%async_computation.1 | async-start | bytes 3670016 | tf_op jit(solution)/shard_map/all_to_all | solution.py:26
  168.4 19.8 %all-to-all-start.4 = ((bf16[16,4,1792]{2,1,0:T(4,128)(2,1)}), bf16[16,4,1792]{2,1,0:T(4,128)(2,1)S(1)}, u32[]{:S(2)}, u32[]{:S(2)}) async-start(bf16[16,4,1792]{2,1,0:T(4,128)(2,1)} %constant_dynamic-update-slice_fusion.8), calls=%async_computation.4 | async-start | bytes 458752 | tf_op jit(solution)/shard_map/all_to_all | solution.py:26
  188.2 13.2 %all-to-all-start.2 = ((bf16[16,4,1792]{2,1,0:T(4,128)(2,1)}), bf16[16,4,1792]{2,1,0:T(4,128)(2,1)S(1)}, u32[]{:S(2)}, u32[]{:S(2)}) async-start(bf16[16,4,1792]{2,1,0:T(4,128)(2,1)} %constant_dynamic-update-slice_fusion.3), calls=%async_computation.2 | async-start | bytes 458752 | tf_op jit(solution)/shard_map/all_to_all | solution.py:26
  202.2 10.3 %collective-permute-start.3 = (f32[64]{0:T(128)S(1)}, f32[64]{0:T(128)S(1)}, u32[]{:S(2)}, u32[]{:S(2)}) collective-permute-start(f32[64]{0:T(128)S(1)} %reshape.125), channel_id=1, source_target_pairs={{0,128},{128,0},{1,129},{129,1},{2,130},{130,2},{3,131},{131,3},{4... | collective-permute-start | bytes 776 | tf_op jit(solution)/shard_map/ppermute | solution.py:130
  206.8 5.7 %collective-permute-start.4 = (f32[64]{0:T(128)S(1)}, f32[64]{0:T(128)S(1)}, u32[]{:S(2)}, u32[]{:S(2)}) collective-permute-start(f32[64]{0:T(128)S(1)} %reshape.126), channel_id=1, source_target_pairs={{0,128},{128,0},{1,129},{129,1},{2,130},{130,2},{3,131},{131,3},{4... | collective-permute-start | bytes 776 | tf_op jit(solution)/shard_map/ppermute | solution.py:130
  208.7 5.2 %collective-permute-start.2 = (f32[8,512]{1,0:T(8,128)S(1)}, f32[8,512]{1,0:T(8,128)S(1)}, u32[]{:S(2)}, u32[]{:S(2)}) collective-permute-start(f32[8,512]{1,0:T(8,128)S(1)} %subtract_divide_fusion), channel_id=1, source_target_pairs={{8,128},{24,144},{40,160},{56,176},{72,192},{88,208},{104,224},{12... | collective-permute-start | bytes 49160 | tf_op jit(solution)/shard_map/ppermute | solution.py:154

commit v9 on v7

--- a/solution.py
+++ b/solution.py
@@ -16,16 +16,19 @@
 
 
 def reduce_stage(unscaled, own_center, extra, axis):
-    width, more = unscaled.shape[-1], extra.shape[-1]
+    width, rows = unscaled.shape[-1], extra.shape[-2]
     unscaled_high, unscaled_low = split_pair(unscaled)
-    extra_high, extra_low = split_pair(extra)
+    extra_high, extra_low = split_pair(extra[..., :3, :])
+    spare = jnp.zeros(extra.shape[:-2] + (rows - 6, extra.shape[-1]), jnp.bfloat16)
+    extra_packed = jnp.concatenate([extra_high, extra_low, spare], axis=-2)
     packed = jnp.concatenate(
-        [unscaled_high, unscaled_low, own_center.astype(jnp.bfloat16), extra_high, extra_low], axis=-1
+        [unscaled_high, unscaled_low, own_center.astype(jnp.bfloat16), extra_packed], axis=-1
     )
     packed = lax.all_to_all(packed, axis, 0, 0, tiled=False).astype(jnp.float32)
     unscaled = (packed[..., :width] + packed[..., width : 2 * width]).sum(0)
     own_center = packed[..., 2 * width : 3 * width].sum(0)
-    extra = (packed[..., 3 * width : 3 * width + more] + packed[..., 3 * width + more :]).sum(0)
+    extra_sum = (packed[..., 3 * width :][..., :3, :] + packed[..., 3 * width :][..., 3:6, :]).sum(0)
+    extra = jnp.concatenate([extra_sum, jnp.zeros(extra_sum.shape[:-2] + (rows - 3, extra_sum.shape[-1]), jnp.float32)], axis=-2)
     return unscaled, own_center, extra
 
 
@@ -45,7 +48,7 @@
     half = rows_per_batch // section_count
     devices = section_count * batch_count * class_count
     rows_here = rows_per_batch * batch_count // devices
-    assert half == class_count * rows_here and rows_here >= 3 and half <= EXTRA and rows_here <= EXTRA
+    assert half == class_count * rows_here and rows_here >= 6 and half <= EXTRA and rows_here <= EXTRA
 
     my_rows = lax.dynamic_slice_in_dim(embeddings, section * half, half, 0)
     my_labels = lax.dynamic_slice_in_dim(labels, section * half, half, 0)

time: 156 us -> 151 us (0.968)
  blocking collectives: 44.4 us -> 41.6 us
    all_to_all x1, blocking collectives: 44.4 us -> 41.6 us  [reduce_stage(): packed = lax.all_to_all(packed, axis, 0, 0, tiled=False).astype(jnp.float32)]
    unnamed x7 -> x1, other arithmetic: 2.72 us -> 0.02 us
    convert_element_type x0 -> x4, other arithmetic: none -> 1.57 us  [split_pair(): return (high.astype(jnp.bfloat16), low)]
where the time goes in v9:
time: 151 us
  blocking collectives  41.6 us (28%)
  waiting for transfers between devices  34 us (23%)
  starting transfers between devices  29 us (19%)
  matrix products  23 us (15%)
  other arithmetic  11.4 us (8%)
  local copies, waits for them, and re-layouts  10.8 us (7%)
    all_to_all x1, blocking collectives, reduce_stage(): packed = lax.all_to_all(packed, axis, 0, 0, tiled=False).astype(jnp.float32)  41.6 us
    all_to_all x1, waiting for transfers between devices, on_device(): lax.all_to_all(jnp.broadcast_to(packed[None], (batch_count,) + packed.sha...  17.4 us
    all_to_all x1, waiting for transfers between devices, reduce_stage(): packed = lax.all_to_all(packed, axis, 0, 0, tiled=False).astype(jnp.float32)  11.8 us
    all_to_all x1, starting transfers between devices, on_device(): lax.all_to_all(jnp.broadcast_to(packed[None], (batch_count,) + packed.sha...  11.7 us
    dot_general x1, matrix products, on_device(): lax.dot_general(unit_rows, both_centers, (((1,), (1,)), ((), ())), prefer...  10.1 us
    all_to_all x1, starting transfers between devices, reduce_stage(): packed = lax.all_to_all(packed, axis, 0, 0, tiled=False).astype(jnp.float32)  9.49 us
    gather x1, local copies, waits for them, and re-layouts, on_device(): chosen = jnp.take(centers, local_ids, axis=0).astype(jnp.float32)  7.59 us
    dot_general x1, matrix products, on_device(): jnp.dot(weights, both_centers, preferred_element_type=jnp.float32)  7.56 us
  transfers between devices with their start and end apart: 7, of which 4 were waited for; matrix products, arithmetic and copies ran while one was open for 8% of the time, Pallas kernels for 0%

profile of v9, /device:TPU:1, one launch (start us, length us, event | category | flops | bytes accessed | tf_op | source)
XLA Modules:
  0.0 150.8 jit_solution(2677301049621806855)
XLA Ops:
  0.7 0.8 fusion.32
  2.0 1.2 broadcast_in_dim.25
  3.2 11.7 %all-to-all-start = ((bf16[16,64,640]{2,1,0:T(8,128)(2,1)}), bf16[16,64,640]{2,1,0:T(8,128)(2,1)S(1)}, u32[]{:S(2)}, u32[]{:S(2)}) async-start(bf16[16,64,640]{2,1,0:T(8,128)(2,1)} %broadcast_in_dim.25), calls=%async_computation | async-start | bytes 2621440 | tf_op jit(solution)/shard_map/all_to_all | solution.py:59
  15.0 7.6 %gather_fusion = bf16[1536,512]{1,0:T(8,128)(2,1)S(1)} fusion(bf16[4096,512]{1,0:T(8,128)(2,1)} %param.5, s32[2048]{0:T(1024)S(1)} %pad_clamp_fusion), kind=kCustom, calls=%fused_computation | custom fusion | bytes 3151872 | tf_op jit(solution)/shard_map/jit(_take)/gather | solution.py:67
  22.6 0.8 fusion.8
  23.4 2.0 %fusion.9 = bf16[1536,512]{1,0:T(8,128)(2,1)} fusion(f32[1536]{0:T(1024)S(1)} %add_sqrt_fusion, bf16[1536,512]{1,0:T(8,128)(2,1)S(1)} %gather_fusion, pred[1536]{0:T(1024)(128)(4,1)S(1)} %compare_and_fusion), kind=kLoop, calls=%fused_computation.17 | loop fusion | flops 3145728 | bytes 3153408 | tf_op jit(solution)/shard_map/convert_element_type | solution.py:69
  25.4 1.0 collective-permute-start
  26.4 3.4 %collective-permute-done.1 = s32[1536]{0:T(1024)S(1)} collective-permute-done((s32[1536]{0:T(1024)S(1)}, s32[1536]{0:T(1024)S(1)}, u32[]{:S(2)}, u32[]{:S(2)}) %collective-permute-start.1) | collective-permute-done | bytes 6176 | tf_op jit(solution)/shard_map/ppermute | solution.py:72
  29.7 17.4 %all-to-all-done = bf16[16,64,640]{2,1,0:T(8,128)(2,1)S(1)} async-done(((bf16[16,64,640]{2,1,0:T(8,128)(2,1)}), bf16[16,64,640]{2,1,0:T(8,128)(2,1)S(1)}, u32[]{:S(2)}, u32[]{:S(2)}) %all-to-all-start) | async-done | bytes 1310752 | tf_op jit(solution)/shard_map/all_to_all | solution.py:59
  47.2 0.5 fusion.18
  47.7 0.3 multiply_reduce_fusion
  48.0 10.1 %fusion.3 = (f32[1024]{0:T(1024)S(1)}, f32[1024]{0:T(1024)S(1)}, f32[1024,3072]{1,0:T(8,128)}) fusion(s32[3072]{0:T(1024)S(1)} %pad_add_fusion, s32[1024]{0:T(1024)S(1)} %fusion.18, bf16[1536,512]{1,0:T(8,128)(2,1)} %collective-permute-done, bf16[1536,512]{1,0:T(8,128)(2,1)} %fusion.9, f32[1024]{0:T(1024)S(1)} %add_sqrt_fusion.1, ...), kind=kOutput, calls=%fused_computation.6 | convolution fusion | flops 3251107840 | bytes 16805888 | tf_op jit(solution)/shard_map/dot_general | solution.py:79
  58.3 7.6 %fusion.5 = f32[1024,512]{1,0:T(8,128)S(1)} fusion(f32[1024,3072]{1,0:T(8,128)} %get-tuple-element.21, s32[3072]{0:T(1024)S(1)} %pad_add_fusion, s32[1024]{0:T(1024)S(1)} %fusion.18, bf16[1536,512]{1,0:T(8,128)(2,1)} %collective-permute-done, bf16[1536,512]{1,0:T(8,128)(2,1)} %fusion.9), kind=kOutput, calls=%fused_computation.10 | convolution fusion | flops 3243245568 | bytes 17842176 | tf_op jit(solution)/shard_map/dot_general | solution.py:88
  65.8 0.2 copy.18
  66.0 1.4 reduce-precision_convert_fusion
  67.5 5.3 %fusion.12 = bf16[1024,512]{1,0:T(8,128)(2,1)S(1)} fusion(s32[3072]{0:T(1024)S(1)} %pad_add_fusion, s32[1024]{0:T(1024)S(1)} %fusion.18, bf16[1536,512]{1,0:T(8,128)(2,1)} %collective-permute-done, bf16[1536,512]{1,0:T(8,128)(2,1)} %fusion.9), kind=kOutput, calls=%fused_computation.28 | convolution fusion | flops 3231186944 | bytes 4210688 | tf_op jit(solution)/shard_map/dot_general | solution.py:89
  73.2 0.9 copy-done.1
  74.1 0.8 maximum_maximum_fusion
  74.9 41.6 %all_to_all.15 = bf16[8,16,8,1664]{3,2,1,0:T(8,128)(2,1)S(1)} all-to-all(bf16[8,16,8,1664]{3,2,1,0:T(8,128)(2,1)S(1)} %maximum_maximum_fusion), channel_id=1, replica_groups=mesh['section'=2,'dp'=16,'cls'=8] {'cls'}, dimensions={0} | all-to-all | bytes 6815744 | tf_op jit(solution)/shard_map/all_to_all | solution.py:27
  116.4 0.5 convert_element_type.85
  116.9 0.3 fusion.11
  117.3 0.8 maximum_maximum_fusion.1
  118.2 9.5 %all-to-all-start.2 = ((bf16[16,8,1664]{2,1,0:T(8,128)(2,1)}), bf16[16,8,1664]{2,1,0:T(8,128)(2,1)}, u32[]{:S(2)}, u32[]{:S(2)}) async-start(bf16[16,8,1664]{2,1,0:T(8,128)(2,1)} %maximum_maximum_fusion.1), calls=%async_computation.2 | async-start | bytes 851968 | tf_op jit(solution)/shard_map/all_to_all | solution.py:27
  127.8 0.3 slice_convert_fusion
  128.1 11.8 %all-to-all-done.2 = bf16[16,8,1664]{2,1,0:T(8,128)(2,1)} async-done(((bf16[16,8,1664]{2,1,0:T(8,128)(2,1)}), bf16[16,8,1664]{2,1,0:T(8,128)(2,1)}, u32[]{:S(2)}, u32[]{:S(2)}) %all-to-all-start.2) | async-done | bytes 426016 | tf_op jit(solution)/shard_map/all_to_all | solution.py:27
  139.9 1.1 convert_element_type.91
  141.0 3.7 %collective-permute-start.3 = (f32[64]{0:T(128)S(1)}, f32[64]{0:T(128)S(1)}, u32[]{:S(2)}, u32[]{:S(2)}) collective-permute-start(f32[64]{0:T(128)S(1)} %get-tuple-element.19), channel_id=1, source_target_pairs={{0,128},{128,0},{1,129},{129,1},{2,130},{130,2},{3,131},{131,3},{4... | collective-permute-start | bytes 776 | tf_op jit(solution)/shard_map/ppermute | solution.py:118
  144.8 0.2 multiply_reduce_fusion.1
  145.1 3.0 %collective-permute-start.2 = (f32[8,512]{1,0:T(8,128)S(1)}, f32[8,512]{1,0:T(8,128)S(1)}, u32[]{:S(2)}, u32[]{:S(2)}) collective-permute-start(f32[8,512]{1,0:T(8,128)S(1)} %subtract_divide_fusion), channel_id=1, source_target_pairs={{8,128},{24,144},{40,160},{56,176},{72,192},{88,208},{104,224},{12... | collective-permute-start | bytes 49160 | tf_op jit(solution)/shard_map/ppermute | solution.py:142
  148.2 0.6 fusion.28
  148.8 1.4 collective-permute-done.2
  150.2 0.6 broadcast_select_fusion.1
  (48 shorter events, 1.8 us)
Async XLA Ops:
  0.6 1.2 copy-start
  0.6 14.3 %copy-start.2 = (s32[1,1536]{1,0:T(1,128)S(1)}, s32[1,1536]{1,0:T(1,128)}, u32[]{:S(2)}) copy-start(s32[1,1536]{1,0:T(1,128)} %param.6) | copy-start | bytes 18436
  3.2 44.0 %all-to-all-start = ((bf16[16,64,640]{2,1,0:T(8,128)(2,1)}), bf16[16,64,640]{2,1,0:T(8,128)(2,1)S(1)}, u32[]{:S(2)}, u32[]{:S(2)}) async-start(bf16[16,64,640]{2,1,0:T(8,128)(2,1)} %broadcast_in_dim.25), calls=%async_computation | async-start | bytes 2621440 | tf_op jit(solution)/shard_map/all_to_all | solution.py:59
  25.4 22.6 %collective-permute-start = (bf16[1536,512]{1,0:T(8,128)(2,1)}, bf16[1536,512]{1,0:T(8,128)(2,1)}, u32[]{:S(2)}, u32[]{:S(2)}) collective-permute-start(bf16[1536,512]{1,0:T(8,128)(2,1)} %fusion.9), channel_id=1, source_target_pairs={{0,128},{128,0},{1,129},{129,1},{2,130},{130,2},{3,131},{131,3},{4... | collective-permute-start | bytes 4718600 | tf_op jit(solution)/shard_map/ppermute | solution.py:71
  26.3 3.4 %collective-permute-start.1 = (s32[1536]{0:T(1024)S(1)}, s32[1536]{0:T(1024)S(1)}, u32[]{:S(2)}, u32[]{:S(2)}) collective-permute-start(s32[1536]{0:T(1024)S(1)} %broadcast_add_fusion), channel_id=1, source_target_pairs={{0,128},{128,0},{1,129},{129,1},{2,130},{130,2},{3,131},{131,3},{4... | collective-permute-start | bytes 18440 | tf_op jit(solution)/shard_map/ppermute | solution.py:72
  72.8 1.2 copy-start.1
  118.2 21.7 %all-to-all-start.2 = ((bf16[16,8,1664]{2,1,0:T(8,128)(2,1)}), bf16[16,8,1664]{2,1,0:T(8,128)(2,1)}, u32[]{:S(2)}, u32[]{:S(2)}) async-start(bf16[16,8,1664]{2,1,0:T(8,128)(2,1)} %maximum_maximum_fusion.1), calls=%async_computation.2 | async-start | bytes 851968 | tf_op jit(solution)/shard_map/all_to_all | solution.py:27
  141.0 7.1 %collective-permute-start.3 = (f32[64]{0:T(128)S(1)}, f32[64]{0:T(128)S(1)}, u32[]{:S(2)}, u32[]{:S(2)}) collective-permute-start(f32[64]{0:T(128)S(1)} %get-tuple-element.19), channel_id=1, source_target_pairs={{0,128},{128,0},{1,129},{129,1},{2,130},{130,2},{3,131},{131,3},{4... | collective-permute-start | bytes 776 | tf_op jit(solution)/shard_map/ppermute | solution.py:118
  144.7 3.4 %collective-permute-start.4 = (f32[64]{0:T(128)S(1)}, f32[64]{0:T(128)S(1)}, u32[]{:S(2)}, u32[]{:S(2)}) collective-permute-start(f32[64]{0:T(128)S(1)} %get-tuple-element.18), channel_id=1, source_target_pairs={{0,128},{128,0},{1,129},{129,1},{2,130},{130,2},{3,131},{131,3},{4... | collective-permute-start | bytes 776 | tf_op jit(solution)/shard_map/ppermute | solution.py:118
  145.1 5.1 %collective-permute-start.2 = (f32[8,512]{1,0:T(8,128)S(1)}, f32[8,512]{1,0:T(8,128)S(1)}, u32[]{:S(2)}, u32[]{:S(2)}) collective-permute-start(f32[8,512]{1,0:T(8,128)S(1)} %subtract_divide_fusion), channel_id=1, source_target_pairs={{8,128},{24,144},{40,160},{56,176},{72,192},{88,208},{104,224},{12... | collective-permute-start | bytes 49160 | tf_op jit(solution)/shard_map/ppermute | solution.py:142

commit v10 on v9

--- a/solution.py
+++ b/solution.py
@@ -85,8 +85,9 @@
     total_part = jnp.sum(exponent, axis=1)
     target_part = jnp.sum(jnp.where(matches, logits, jnp.float32(0.0)), axis=1)
     weights = exponent.astype(jnp.bfloat16)
-    unscaled = jnp.dot(weights, both_centers, preferred_element_type=jnp.float32)
-    own_center = jnp.dot(matches.astype(jnp.bfloat16), both_centers, preferred_element_type=jnp.float32)
+    stacked = jnp.concatenate([weights, matches.astype(jnp.bfloat16)], axis=0)
+    products = jnp.dot(stacked, both_centers, preferred_element_type=jnp.float32)
+    unscaled, own_center = products[: weights.shape[0]], products[weights.shape[0] :]
 
     h = batch_count // 2
 

time: 151 us -> 159 us (1.053)
  local copies, waits for them, and re-layouts: 10.8 us -> 18.2 us
  other arithmetic: 11.4 us -> 14.2 us
    slice x0 -> x2, local copies, waits for them, and re-layouts: none -> 4.48 us  [the longest x1 2.71 us: on_device(): products[weights.shape[0]:]]
    ppermute x1, waiting for transfers between devices: 3.35 us -> 0.01 us  [on_device(): partner_ids = lax.ppermute(global_ids, 'section', swap)]
    all_to_all x1, waiting for transfers between devices: 17.4 us -> 20.1 us  [on_device(): lax.all_to_all(jnp.broadcast_to(packed[None], (batch_count,) + packed.sha...]
    convert_element_type x0 -> x1, other arithmetic: none -> 1.66 us  [on_device(): stacked = jnp.concatenate([weights, matches.astype(jnp.bfloat16)], axis=0)]
    dot_general x2 -> x1, matrix products: 12.9 us -> 12 us  [on_device(): jnp.dot(stacked, both_centers, preferred_element_type=jnp.float32)]
  transfers between devices with their start and end apart: 7 -> 7, of which waited for: 4 -> 3; matrix products, arithmetic and copies ran while one was open for 8% -> 10% of each run, Pallas kernels for 0% -> 0%
where the time goes in v10:
time: 159 us; the launch traced here: 158 us
  blocking collectives  41.7 us (26%)
  waiting for transfers between devices  32.6 us (21%)
  starting transfers between devices  29 us (18%)
  matrix products  21.6 us (14%)
  local copies, waits for them, and re-layouts  18.2 us (11%)
  other arithmetic  14.2 us (9%)
    all_to_all x1, blocking collectives, reduce_stage(): packed = lax.all_to_all(packed, axis, 0, 0, tiled=False).astype(jnp.float32)  41.7 us
    all_to_all x1, waiting for transfers between devices, on_device(): lax.all_to_all(jnp.broadcast_to(packed[None], (batch_count,) + packed.sha...  20.1 us
    dot_general x1, matrix products, on_device(): jnp.dot(stacked, both_centers, preferred_element_type=jnp.float32)  12 us
    all_to_all x1, starting transfers between devices, on_device(): lax.all_to_all(jnp.broadcast_to(packed[None], (batch_count,) + packed.sha...  11.7 us
    all_to_all x1, waiting for transfers between devices, reduce_stage(): packed = lax.all_to_all(packed, axis, 0, 0, tiled=False).astype(jnp.float32)  11.1 us
    dot_general x1, matrix products, on_device(): lax.dot_general(unit_rows, both_centers, (((1,), (1,)), ((), ())), prefer...  9.63 us
    all_to_all x1, starting transfers between devices, reduce_stage(): packed = lax.all_to_all(packed, axis, 0, 0, tiled=False).astype(jnp.float32)  9.36 us
    gather x1, local copies, waits for them, and re-layouts, on_device(): chosen = jnp.take(centers, local_ids, axis=0).astype(jnp.float32)  7.59 us
  transfers between devices with their start and end apart: 7, of which 3 were waited for; matrix products, arithmetic and copies ran while one was open for 10% of the time, Pallas kernels for 0%

profile of v10, /device:TPU:1, one launch (start us, length us, event | category | flops | bytes accessed | tf_op | source)
XLA Modules:
  0.0 158.2 jit_solution(2736359404093148790)
XLA Ops:
  0.7 0.8 fusion.27
  2.0 1.2 broadcast_in_dim.25
  3.2 11.7 %all-to-all-start = ((bf16[16,64,640]{2,1,0:T(8,128)(2,1)}), bf16[16,64,640]{2,1,0:T(8,128)(2,1)S(1)}, u32[]{:S(2)}, u32[]{:S(2)}) async-start(bf16[16,64,640]{2,1,0:T(8,128)(2,1)} %broadcast_in_dim.25), calls=%async_computation | async-start | bytes 2621440 | tf_op jit(solution)/shard_map/all_to_all | solution.py:59
  15.0 1.0 collective-permute-start.1
  16.1 7.6 %gather_fusion = bf16[1536,512]{1,0:T(8,128)(2,1)S(1)} fusion(bf16[4096,512]{1,0:T(8,128)(2,1)} %param.5, s32[2048]{0:T(1024)S(1)} %pad_clamp_fusion), kind=kCustom, calls=%fused_computation | custom fusion | bytes 3151872 | tf_op jit(solution)/shard_map/jit(_take)/gather | solution.py:67
  23.7 0.8 fusion.6
  24.5 2.0 %fusion.7 = bf16[1536,512]{1,0:T(8,128)(2,1)} fusion(f32[1536]{0:T(1024)S(1)} %add_sqrt_fusion, bf16[1536,512]{1,0:T(8,128)(2,1)S(1)} %gather_fusion, pred[1536]{0:T(1024)(128)(4,1)S(1)} %compare_and_fusion), kind=kLoop, calls=%fused_computation.16 | loop fusion | flops 3145728 | bytes 3153408 | tf_op jit(solution)/shard_map/convert_element_type | solution.py:69
  26.5 0.6 pad.33.clone
  27.1 20.1 %all-to-all-done = bf16[16,64,640]{2,1,0:T(8,128)(2,1)S(1)} async-done(((bf16[16,64,640]{2,1,0:T(8,128)(2,1)}), bf16[16,64,640]{2,1,0:T(8,128)(2,1)S(1)}, u32[]{:S(2)}, u32[]{:S(2)}) %all-to-all-start) | async-done | bytes 1310752 | tf_op jit(solution)/shard_map/all_to_all | solution.py:59
  47.2 0.5 fusion.13
  48.0 1.7 %compare_convert_fusion = bf16[1024,3072]{1,0:T(8,128)(2,1)S(1)} fusion(s32[3072]{0:T(1024)S(1)} %pad_add_fusion, s32[1024]{0:T(1024)S(1)} %fusion.13), kind=kLoop, calls=%fused_computation.2 | loop fusion | flops 6291456 | bytes 6307840 | tf_op jit(solution)/shard_map/convert_element_type | solution.py:88
  49.7 9.6 %fusion.1 = (f32[1024]{0:T(1024)}, f32[1024]{0:T(1024)S(1)}, bf16[1024,3072]{1,0:T(8,128)(2,1)}) fusion(s32[3072]{0:T(1024)S(1)} %pad_add_fusion, s32[1024]{0:T(1024)S(1)} %fusion.13, bf16[1536,512]{1,0:T(8,128)(2,1)S(1)} %collective-permute-done, bf16[1536,512]{1,0:T(8,128)(2,1)} %fusion.7, f32[1024]{0:T(1024)S(1)} %add_sqrt_fusion.1, ...), kind=kOutput, calls=%fused_computation.5 | convolution fusion | flops 3254253568 | bytes 10514432 | tf_op jit(solution)/shard_map/dot_general | solution.py:79
  59.3 12.0 %fusion.2 = f32[2048,512]{1,0:T(8,128)} fusion(bf16[1024,3072]{1,0:T(8,128)(2,1)S(1)} %compare_convert_fusion, bf16[1024,3072]{1,0:T(8,128)(2,1)} %get-tuple-element.10, bf16[1536,512]{1,0:T(8,128)(2,1)S(1)} %collective-permute-done, bf16[1536,512]{1,0:T(8,128)(2,1)} %fusion.7), kind=kOutput, calls=%fused_computation.6 | convolution fusion | flops 6473908224 | bytes 19922944 | tf_op jit(solution)/shard_map/dot_general | solution.py:89
  71.3 1.8 %slice.96 = f32[1024,512]{1,0:T(8,128)S(1)} slice(f32[2048,512]{1,0:T(8,128)} %fusion.2), slice={[0:1024], [0:512]} | slice | bytes 4194304 | tf_op jit(solution)/shard_map/slice | solution.py:90
  73.0 2.7 %slice.148 = bf16[1024,512]{1,0:T(8,128)(2,1)} slice(f32[2048,512]{1,0:T(8,128)} %fusion.2), slice={[1024:2048], [0:512]} | slice | bytes 2097152 | tf_op jit(solution)/shard_map/slice | solution.py:90
  75.8 0.7 reshape.82
  76.7 1.4 reduce-precision_convert_fusion
  78.3 0.8 reshape.81
  79.1 0.9 copy.20
  80.2 1.9 %maximum_maximum_fusion = bf16[8,16,8,1664]{3,2,1,0:T(8,128)(2,1)S(1)} fusion(bf16[8,16,3,128]{3,2,1,0:T(4,128)(2,1)S(1)} %get-tuple-element.16, bf16[8,16,3,128]{3,2,1,0:T(4,128)(2,1)S(1)} %get-tuple-element.15, bf16[8,16,8,512]{3,2,1,0:T(8,128)(2,1)S(1)} %bitcast.34, bf16[8,16,8,512]{3,2,1,0:T(8,128)(2,1)} %get-tuple-element.12, ...), kind=kLoop, calls=%fused_computation.14 | loop fusion | flops 20447232 | bytes 6776832 | tf_op jit(solution)/shard_map/concatenate | solution.py:24
  82.1 41.7 %all_to_all.15 = bf16[8,16,8,1664]{3,2,1,0:T(8,128)(2,1)S(1)} all-to-all(bf16[8,16,8,1664]{3,2,1,0:T(8,128)(2,1)S(1)} %maximum_maximum_fusion), channel_id=1, replica_groups=mesh['section'=2,'dp'=16,'cls'=8] {'cls'}, dimensions={0} | all-to-all | bytes 6815744 | tf_op jit(solution)/shard_map/all_to_all | solution.py:27
  123.8 0.5 convert_element_type.85
  125.0 0.8 maximum_maximum_fusion.1
  125.8 9.4 %all-to-all-start.2 = ((bf16[16,8,1664]{2,1,0:T(8,128)(2,1)}), bf16[16,8,1664]{2,1,0:T(8,128)(2,1)}, u32[]{:S(2)}, u32[]{:S(2)}) async-start(bf16[16,8,1664]{2,1,0:T(8,128)(2,1)} %maximum_maximum_fusion.1), calls=%async_computation.2 | async-start | bytes 851968 | tf_op jit(solution)/shard_map/all_to_all | solution.py:27
  135.2 0.8 dynamic_slice.15
  136.3 11.1 %all-to-all-done.2 = bf16[16,8,1664]{2,1,0:T(8,128)(2,1)} async-done(((bf16[16,8,1664]{2,1,0:T(8,128)(2,1)}), bf16[16,8,1664]{2,1,0:T(8,128)(2,1)}, u32[]{:S(2)}, u32[]{:S(2)}) %all-to-all-start.2) | async-done | bytes 426016 | tf_op jit(solution)/shard_map/all_to_all | solution.py:27
  147.3 1.1 convert_element_type.91
  148.5 3.7 %collective-permute-start.3 = (f32[64]{0:T(128)S(1)}, f32[64]{0:T(128)S(1)}, u32[]{:S(2)}, u32[]{:S(2)}) collective-permute-start(f32[64]{0:T(128)S(1)} %get-tuple-element.20), channel_id=1, source_target_pairs={{0,128},{128,0},{1,129},{129,1},{2,130},{130,2},{3,131},{131,3},{4... | collective-permute-start | bytes 776 | tf_op jit(solution)/shard_map/ppermute | solution.py:119
  152.6 3.0 %collective-permute-start.2 = (f32[8,512]{1,0:T(8,128)S(1)}, f32[8,512]{1,0:T(8,128)S(1)}, u32[]{:S(2)}, u32[]{:S(2)}) collective-permute-start(f32[8,512]{1,0:T(8,128)S(1)} %subtract_divide_fusion), channel_id=1, source_target_pairs={{8,128},{24,144},{40,160},{56,176},{72,192},{88,208},{104,224},{12... | collective-permute-start | bytes 49160 | tf_op jit(solution)/shard_map/ppermute | solution.py:143
  155.6 0.6 fusion.23
  156.2 1.4 collective-permute-done.2
  157.6 0.6 broadcast_select_fusion.1
  (54 shorter events, 3.0 us)
Async XLA Ops:
  0.6 1.2 copy-start
  0.6 14.3 %copy-start.3 = (s32[1,1536]{1,0:T(1,128)S(1)}, s32[1,1536]{1,0:T(1,128)}, u32[]{:S(2)}) copy-start(s32[1,1536]{1,0:T(1,128)} %param.6) | copy-start | bytes 18436
  3.2 44.0 %all-to-all-start = ((bf16[16,64,640]{2,1,0:T(8,128)(2,1)}), bf16[16,64,640]{2,1,0:T(8,128)(2,1)S(1)}, u32[]{:S(2)}, u32[]{:S(2)}) async-start(bf16[16,64,640]{2,1,0:T(8,128)(2,1)} %broadcast_in_dim.25), calls=%async_computation | async-start | bytes 2621440 | tf_op jit(solution)/shard_map/all_to_all | solution.py:59
  15.0 12.1 %collective-permute-start.1 = (s32[1536]{0:T(1024)S(1)}, s32[1536]{0:T(1024)S(1)}, u32[]{:S(2)}, u32[]{:S(2)}) collective-permute-start(s32[1536]{0:T(1024)S(1)} %broadcast_add_fusion), channel_id=1, source_target_pairs={{0,128},{128,0},{1,129},{129,1},{2,130},{130,2},{3,131},{131,3},{4... | collective-permute-start | bytes 18440 | tf_op jit(solution)/shard_map/ppermute | solution.py:72
  26.4 23.2 %collective-permute-start = (bf16[1536,512]{1,0:T(8,128)(2,1)}, bf16[1536,512]{1,0:T(8,128)(2,1)S(1)}, u32[]{:S(2)}, u32[]{:S(2)}) collective-permute-start(bf16[1536,512]{1,0:T(8,128)(2,1)} %fusion.7), channel_id=1, source_target_pairs={{0,128},{128,0},{1,129},{129,1},{2,130},{130,2},{3,131},{131,3},{4... | collective-permute-start | bytes 4718600 | tf_op jit(solution)/shard_map/ppermute | solution.py:71
  48.0 11.3 %copy-start.4 = (f32[1024]{0:T(1024)}, f32[1024]{0:T(1024)S(1)}, u32[]{:S(2)}) copy-start(f32[1024]{0:T(1024)S(1)} %add_sqrt_fusion.1) | copy-start | bytes 12292
  76.5 1.6 %copy-start.1 = (bf16[1024,512]{1,0:T(8,128)(2,1)S(1)}, bf16[1024,512]{1,0:T(8,128)(2,1)}, u32[]{:S(2)}) copy-start(bf16[1024,512]{1,0:T(8,128)(2,1)} %slice.148) | copy-start | bytes 3145732
  124.2 0.7 copy-start.2
  125.8 21.5 %all-to-all-start.2 = ((bf16[16,8,1664]{2,1,0:T(8,128)(2,1)}), bf16[16,8,1664]{2,1,0:T(8,128)(2,1)}, u32[]{:S(2)}, u32[]{:S(2)}) async-start(bf16[16,8,1664]{2,1,0:T(8,128)(2,1)} %maximum_maximum_fusion.1), calls=%async_computation.2 | async-start | bytes 851968 | tf_op jit(solution)/shard_map/all_to_all | solution.py:27
  148.5 7.1 %collective-permute-start.3 = (f32[64]{0:T(128)S(1)}, f32[64]{0:T(128)S(1)}, u32[]{:S(2)}, u32[]{:S(2)}) collective-permute-start(f32[64]{0:T(128)S(1)} %get-tuple-element.20), channel_id=1, source_target_pairs={{0,128},{128,0},{1,129},{129,1},{2,130},{130,2},{3,131},{131,3},{4... | collective-permute-start | bytes 776 | tf_op jit(solution)/shard_map/ppermute | solution.py:119
  152.2 3.4 %collective-permute-start.4 = (f32[64]{0:T(128)S(1)}, f32[64]{0:T(128)S(1)}, u32[]{:S(2)}, u32[]{:S(2)}) collective-permute-start(f32[64]{0:T(128)S(1)} %get-tuple-element.19), channel_id=1, source_target_pairs={{0,128},{128,0},{1,129},{129,1},{2,130},{130,2},{3,131},{131,3},{4... | collective-permute-start | bytes 776 | tf_op jit(solution)/shard_map/ppermute | solution.py:119
  152.6 5.1 %collective-permute-start.2 = (f32[8,512]{1,0:T(8,128)S(1)}, f32[8,512]{1,0:T(8,128)S(1)}, u32[]{:S(2)}, u32[]{:S(2)}) collective-permute-start(f32[8,512]{1,0:T(8,128)S(1)} %subtract_divide_fusion), channel_id=1, source_target_pairs={{8,128},{24,144},{40,160},{56,176},{72,192},{88,208},{104,224},{12... | collective-permute-start | bytes 49160 | tf_op jit(solution)/shard_map/ppermute | solution.py:143

commit v11 on v9

--- a/solution.py
+++ b/solution.py
@@ -84,7 +84,7 @@
     exponent = jnp.exp(logits)
     total_part = jnp.sum(exponent, axis=1)
     target_part = jnp.sum(jnp.where(matches, logits, jnp.float32(0.0)), axis=1)
-    weights = exponent.astype(jnp.bfloat16)
+    weights = lax.optimization_barrier(exponent.astype(jnp.bfloat16))
     unscaled = jnp.dot(weights, both_centers, preferred_element_type=jnp.float32)
     own_center = jnp.dot(matches.astype(jnp.bfloat16), both_centers, preferred_element_type=jnp.float32)
 

time: 151 us -> 149 us (0.987)
  matrix products: 23 us -> 21.1 us
where the time goes in v11:
time: 149 us
  blocking collectives  41.5 us (28%)
  waiting for transfers between devices  34 us (23%)
  starting transfers between devices  29 us (19%)
  matrix products  21.1 us (14%)
  other arithmetic  11.4 us (8%)
  local copies, waits for them, and re-layouts  10.8 us (7%)
    all_to_all x1, blocking collectives, reduce_stage(): packed = lax.all_to_all(packed, axis, 0, 0, tiled=False).astype(jnp.float32)  41.5 us
    all_to_all x1, waiting for transfers between devices, on_device(): lax.all_to_all(jnp.broadcast_to(packed[None], (batch_count,) + packed.sha...  17.4 us
    all_to_all x1, waiting for transfers between devices, reduce_stage(): packed = lax.all_to_all(packed, axis, 0, 0, tiled=False).astype(jnp.float32)  11.8 us
    all_to_all x1, starting transfers between devices, on_device(): lax.all_to_all(jnp.broadcast_to(packed[None], (batch_count,) + packed.sha...  11.7 us
    all_to_all x1, starting transfers between devices, reduce_stage(): packed = lax.all_to_all(packed, axis, 0, 0, tiled=False).astype(jnp.float32)  9.49 us
    dot_general x1, matrix products, on_device(): lax.dot_general(unit_rows, both_centers, (((1,), (1,)), ((), ())), prefer...  9.33 us
    gather x1, local copies, waits for them, and re-layouts, on_device(): chosen = jnp.take(centers, local_ids, axis=0).astype(jnp.float32)  7.59 us
    dot_general x1, matrix products, on_device(): jnp.dot(weights, both_centers, preferred_element_type=jnp.float32)  6.45 us
  transfers between devices with their start and end apart: 7, of which 4 were waited for; matrix products, arithmetic and copies ran while one was open for 8% of the time, Pallas kernels for 0%

profile of v11, /device:TPU:1, one launch (start us, length us, event | category | flops | bytes accessed | tf_op | source)
XLA Modules:
  0.0 148.9 jit_solution(8638081948083724214)
XLA Ops:
  0.7 0.8 fusion.31
  2.0 1.2 broadcast_in_dim.25
  3.2 11.7 %all-to-all-start = ((bf16[16,64,640]{2,1,0:T(8,128)(2,1)}), bf16[16,64,640]{2,1,0:T(8,128)(2,1)S(1)}, u32[]{:S(2)}, u32[]{:S(2)}) async-start(bf16[16,64,640]{2,1,0:T(8,128)(2,1)} %broadcast_in_dim.25), calls=%async_computation | async-start | bytes 2621440 | tf_op jit(solution)/shard_map/all_to_all | solution.py:59
  15.0 7.6 %gather_fusion = bf16[1536,512]{1,0:T(8,128)(2,1)S(1)} fusion(bf16[4096,512]{1,0:T(8,128)(2,1)} %param.5, s32[2048]{0:T(1024)S(1)} %pad_clamp_fusion), kind=kCustom, calls=%fused_computation | custom fusion | bytes 3151872 | tf_op jit(solution)/shard_map/jit(_take)/gather | solution.py:67
  22.6 0.8 fusion.6
  23.4 2.0 %fusion.7 = bf16[1536,512]{1,0:T(8,128)(2,1)} fusion(f32[1536]{0:T(1024)S(1)} %add_sqrt_fusion, bf16[1536,512]{1,0:T(8,128)(2,1)S(1)} %gather_fusion, pred[1536]{0:T(1024)(128)(4,1)S(1)} %compare_and_fusion), kind=kLoop, calls=%fused_computation.15 | loop fusion | flops 3145728 | bytes 3153408 | tf_op jit(solution)/shard_map/convert_element_type | solution.py:69
  25.4 1.0 collective-permute-start
  26.4 3.4 %collective-permute-done.1 = s32[1536]{0:T(1024)S(1)} collective-permute-done((s32[1536]{0:T(1024)S(1)}, s32[1536]{0:T(1024)S(1)}, u32[]{:S(2)}, u32[]{:S(2)}) %collective-permute-start.1) | collective-permute-done | bytes 6176 | tf_op jit(solution)/shard_map/ppermute | solution.py:72
  29.7 17.4 %all-to-all-done = bf16[16,64,640]{2,1,0:T(8,128)(2,1)S(1)} async-done(((bf16[16,64,640]{2,1,0:T(8,128)(2,1)}), bf16[16,64,640]{2,1,0:T(8,128)(2,1)S(1)}, u32[]{:S(2)}, u32[]{:S(2)}) %all-to-all-start) | async-done | bytes 1310752 | tf_op jit(solution)/shard_map/all_to_all | solution.py:59
  47.2 0.5 fusion.17
  47.7 0.3 multiply_reduce_fusion
  48.0 9.3 %fusion.3 = (f32[1024]{0:T(1024)S(1)}, f32[1024]{0:T(1024)S(1)}, bf16[1024,3072]{1,0:T(8,128)(2,1)}) fusion(s32[3072]{0:T(1024)S(1)} %pad_add_fusion, s32[1024]{0:T(1024)S(1)} %fusion.17, bf16[1536,512]{1,0:T(8,128)(2,1)} %collective-permute-done, bf16[1536,512]{1,0:T(8,128)(2,1)} %fusion.7, f32[1024]{0:T(1024)S(1)} %add_sqrt_fusion.1, ...), kind=kOutput, calls=%fused_computation.6 | convolution fusion | flops 3254253568 | bytes 10514432 | tf_op jit(solution)/shard_map/dot_general | solution.py:79
  57.5 6.5 %fusion.15 = f32[1024,512]{1,0:T(8,128)S(1)} fusion(bf16[1024,3072]{1,0:T(8,128)(2,1)} %get-tuple-element.10, bf16[1536,512]{1,0:T(8,128)(2,1)} %collective-permute-done, bf16[1536,512]{1,0:T(8,128)(2,1)} %fusion.7), kind=kOutput, calls=%fused_computation.30 | convolution fusion | flops 3227516928 | bytes 11534336 | tf_op jit(solution)/shard_map/dot_general | solution.py:88
  64.0 0.2 copy.18
  64.1 1.4 reduce-precision_convert_fusion
  65.7 5.3 %fusion.10 = bf16[1024,512]{1,0:T(8,128)(2,1)S(1)} fusion(s32[3072]{0:T(1024)S(1)} %pad_add_fusion, s32[1024]{0:T(1024)S(1)} %fusion.17, bf16[1536,512]{1,0:T(8,128)(2,1)} %collective-permute-done, bf16[1536,512]{1,0:T(8,128)(2,1)} %fusion.7), kind=kOutput, calls=%fused_computation.26 | convolution fusion | flops 3231186944 | bytes 4210688 | tf_op jit(solution)/shard_map/dot_general | solution.py:89
  71.4 0.9 copy-done.1
  72.2 0.8 maximum_maximum_fusion
  73.0 41.5 %all_to_all.15 = bf16[8,16,8,1664]{3,2,1,0:T(8,128)(2,1)S(1)} all-to-all(bf16[8,16,8,1664]{3,2,1,0:T(8,128)(2,1)S(1)} %maximum_maximum_fusion), channel_id=1, replica_groups=mesh['section'=2,'dp'=16,'cls'=8] {'cls'}, dimensions={0} | all-to-all | bytes 6815744 | tf_op jit(solution)/shard_map/all_to_all | solution.py:27
  114.5 0.5 convert_element_type.85
  115.0 0.3 fusion.9
  115.5 0.8 maximum_maximum_fusion.1
  116.3 9.5 %all-to-all-start.2 = ((bf16[16,8,1664]{2,1,0:T(8,128)(2,1)}), bf16[16,8,1664]{2,1,0:T(8,128)(2,1)}, u32[]{:S(2)}, u32[]{:S(2)}) async-start(bf16[16,8,1664]{2,1,0:T(8,128)(2,1)} %maximum_maximum_fusion.1), calls=%async_computation.2 | async-start | bytes 851968 | tf_op jit(solution)/shard_map/all_to_all | solution.py:27
  125.9 0.3 slice_convert_fusion
  126.2 11.8 %all-to-all-done.2 = bf16[16,8,1664]{2,1,0:T(8,128)(2,1)} async-done(((bf16[16,8,1664]{2,1,0:T(8,128)(2,1)}), bf16[16,8,1664]{2,1,0:T(8,128)(2,1)}, u32[]{:S(2)}, u32[]{:S(2)}) %all-to-all-start.2) | async-done | bytes 426016 | tf_op jit(solution)/shard_map/all_to_all | solution.py:27
  138.0 1.1 convert_element_type.91
  139.2 3.7 %collective-permute-start.3 = (f32[64]{0:T(128)S(1)}, f32[64]{0:T(128)S(1)}, u32[]{:S(2)}, u32[]{:S(2)}) collective-permute-start(f32[64]{0:T(128)S(1)} %get-tuple-element.20), channel_id=1, source_target_pairs={{0,128},{128,0},{1,129},{129,1},{2,130},{130,2},{3,131},{131,3},{4... | collective-permute-start | bytes 776 | tf_op jit(solution)/shard_map/ppermute | solution.py:118
  143.0 0.2 multiply_reduce_fusion.1
  143.2 3.0 %collective-permute-start.2 = (f32[8,512]{1,0:T(8,128)S(1)}, f32[8,512]{1,0:T(8,128)S(1)}, u32[]{:S(2)}, u32[]{:S(2)}) collective-permute-start(f32[8,512]{1,0:T(8,128)S(1)} %subtract_divide_fusion), channel_id=1, source_target_pairs={{8,128},{24,144},{40,160},{56,176},{72,192},{88,208},{104,224},{12... | collective-permute-start | bytes 49160 | tf_op jit(solution)/shard_map/ppermute | solution.py:142
  146.3 0.6 fusion.27
  146.9 1.4 collective-permute-done.2
  148.3 0.6 broadcast_select_fusion.1
  (48 shorter events, 1.8 us)
Async XLA Ops:
  0.6 1.2 copy-start
  0.6 14.3 %copy-start.2 = (s32[1,1536]{1,0:T(1,128)S(1)}, s32[1,1536]{1,0:T(1,128)}, u32[]{:S(2)}) copy-start(s32[1,1536]{1,0:T(1,128)} %param.6) | copy-start | bytes 18436
  3.2 44.0 %all-to-all-start = ((bf16[16,64,640]{2,1,0:T(8,128)(2,1)}), bf16[16,64,640]{2,1,0:T(8,128)(2,1)S(1)}, u32[]{:S(2)}, u32[]{:S(2)}) async-start(bf16[16,64,640]{2,1,0:T(8,128)(2,1)} %broadcast_in_dim.25), calls=%async_computation | async-start | bytes 2621440 | tf_op jit(solution)/shard_map/all_to_all | solution.py:59
  25.4 22.6 %collective-permute-start = (bf16[1536,512]{1,0:T(8,128)(2,1)}, bf16[1536,512]{1,0:T(8,128)(2,1)}, u32[]{:S(2)}, u32[]{:S(2)}) collective-permute-start(bf16[1536,512]{1,0:T(8,128)(2,1)} %fusion.7), channel_id=1, source_target_pairs={{0,128},{128,0},{1,129},{129,1},{2,130},{130,2},{3,131},{131,3},{4... | collective-permute-start | bytes 4718600 | tf_op jit(solution)/shard_map/ppermute | solution.py:71
  26.3 3.4 %collective-permute-start.1 = (s32[1536]{0:T(1024)S(1)}, s32[1536]{0:T(1024)S(1)}, u32[]{:S(2)}, u32[]{:S(2)}) collective-permute-start(s32[1536]{0:T(1024)S(1)} %broadcast_add_fusion), channel_id=1, source_target_pairs={{0,128},{128,0},{1,129},{129,1},{2,130},{130,2},{3,131},{131,3},{4... | collective-permute-start | bytes 18440 | tf_op jit(solution)/shard_map/ppermute | solution.py:72
  71.0 1.2 copy-start.1
  116.3 21.7 %all-to-all-start.2 = ((bf16[16,8,1664]{2,1,0:T(8,128)(2,1)}), bf16[16,8,1664]{2,1,0:T(8,128)(2,1)}, u32[]{:S(2)}, u32[]{:S(2)}) async-start(bf16[16,8,1664]{2,1,0:T(8,128)(2,1)} %maximum_maximum_fusion.1), calls=%async_computation.2 | async-start | bytes 851968 | tf_op jit(solution)/shard_map/all_to_all | solution.py:27
  139.2 7.1 %collective-permute-start.3 = (f32[64]{0:T(128)S(1)}, f32[64]{0:T(128)S(1)}, u32[]{:S(2)}, u32[]{:S(2)}) collective-permute-start(f32[64]{0:T(128)S(1)} %get-tuple-element.20), channel_id=1, source_target_pairs={{0,128},{128,0},{1,129},{129,1},{2,130},{130,2},{3,131},{131,3},{4... | collective-permute-start | bytes 776 | tf_op jit(solution)/shard_map/ppermute | solution.py:118
  142.9 3.4 %collective-permute-start.4 = (f32[64]{0:T(128)S(1)}, f32[64]{0:T(128)S(1)}, u32[]{:S(2)}, u32[]{:S(2)}) collective-permute-start(f32[64]{0:T(128)S(1)} %get-tuple-element.19), channel_id=1, source_target_pairs={{0,128},{128,0},{1,129},{129,1},{2,130},{130,2},{3,131},{131,3},{4... | collective-permute-start | bytes 776 | tf_op jit(solution)/shard_map/ppermute | solution.py:118
  143.2 5.1 %collective-permute-start.2 = (f32[8,512]{1,0:T(8,128)S(1)}, f32[8,512]{1,0:T(8,128)S(1)}, u32[]{:S(2)}, u32[]{:S(2)}) collective-permute-start(f32[8,512]{1,0:T(8,128)S(1)} %subtract_divide_fusion), channel_id=1, source_target_pairs={{8,128},{24,144},{40,160},{56,176},{72,192},{88,208},{104,224},{12... | collective-permute-start | bytes 49160 | tf_op jit(solution)/shard_map/ppermute | solution.py:142

commit v12 on v11

--- a/solution.py
+++ b/solution.py
@@ -86,7 +86,10 @@
     target_part = jnp.sum(jnp.where(matches, logits, jnp.float32(0.0)), axis=1)
     weights = lax.optimization_barrier(exponent.astype(jnp.bfloat16))
     unscaled = jnp.dot(weights, both_centers, preferred_element_type=jnp.float32)
-    own_center = jnp.dot(matches.astype(jnp.bfloat16), both_centers, preferred_element_type=jnp.float32)
+    column_ids = jnp.arange(both_ids.shape[0], dtype=jnp.int32)
+    position = jnp.sum(jnp.where(matches, column_ids[None, :], 0), axis=1)
+    owned = jnp.any(matches, axis=1)
+    own_center = jnp.where(owned[:, None], jnp.take(both_centers, position, axis=0), jnp.bfloat16(0)).astype(jnp.float32)
 
     h = batch_count // 2
 

time: 149 us -> 155 us (1.040)
  other arithmetic: 11.4 us -> 20.7 us
  matrix products: 21.1 us -> 15.5 us
  local copies, waits for them, and re-layouts: 10.8 us -> 15.2 us
  waiting for transfers between devices: 34 us -> 31.9 us
    dot_general x1 -> x0, matrix products: 5.33 us -> none  [on_device(): jnp.dot(matches.astype(jnp.bfloat16), both_centers, preferred_element_typ...]
    gather x0 -> x1, local copies, waits for them, and re-layouts: none -> 5.07 us  [on_device(): jnp.take(both_centers, position, axis=0)]
    concatenate x0 -> x1, other arithmetic: none -> 2.09 us  [on_device(): both_centers = jnp.concatenate([unit_centers, partner_centers], axis=0)]
    reduce_sum x0 -> x1, other arithmetic: none -> 1.76 us  [on_device(): position = jnp.sum(jnp.where(matches, column_ids[None, :], 0), axis=1)]
    reduce_or x0 -> x1, other arithmetic: none -> 1.71 us  [on_device(): owned = jnp.any(matches, axis=1)]
    select_n x0 -> x2, other arithmetic: none -> 1.64 us  [the longest x1 1.63 us: on_device(): jnp.where(owned[:, None], jnp.take(both_centers, position, axis=0), jnp.b...]
  transfers between devices with their start and end apart: 7 -> 7, of which waited for: 4 -> 4; matrix products, arithmetic and copies ran while one was open for 8% -> 9% of each run, Pallas kernels for 0% -> 0%
where the time goes in v12:
time: 155 us
  blocking collectives  41.5 us (27%)
  waiting for transfers between devices  31.9 us (21%)
  starting transfers between devices  28.8 us (19%)
  other arithmetic  20.7 us (13%)
  matrix products  15.5 us (10%)
  local copies, waits for them, and re-layouts  15.2 us (10%)
    all_to_all x1, blocking collectives, reduce_stage(): packed = lax.all_to_all(packed, axis, 0, 0, tiled=False).astype(jnp.float32)  41.5 us
    all_to_all x1, waiting for transfers between devices, on_device(): lax.all_to_all(jnp.broadcast_to(packed[None], (batch_count,) + packed.sha...  16.4 us
    all_to_all x1, starting transfers between devices, on_device(): lax.all_to_all(jnp.broadcast_to(packed[None], (batch_count,) + packed.sha...  11.8 us
    all_to_all x1, waiting for transfers between devices, reduce_stage(): packed = lax.all_to_all(packed, axis, 0, 0, tiled=False).astype(jnp.float32)  11 us
    all_to_all x1, starting transfers between devices, reduce_stage(): packed = lax.all_to_all(packed, axis, 0, 0, tiled=False).astype(jnp.float32)  9.72 us
    dot_general x1, matrix products, on_device(): lax.dot_general(unit_rows, both_centers, (((1,), (1,)), ((), ())), prefer...  9.03 us
    gather x1, local copies, waits for them, and re-layouts, on_device(): chosen = jnp.take(centers, local_ids, axis=0).astype(jnp.float32)  7.59 us
    dot_general x1, matrix products, on_device(): jnp.dot(weights, both_centers, preferred_element_type=jnp.float32)  6.45 us
  transfers between devices with their start and end apart: 7, of which 4 were waited for; matrix products, arithmetic and copies ran while one was open for 9% of the time, Pallas kernels for 0%

profile of v12, /device:TPU:1, one launch (start us, length us, event | category | flops | bytes accessed | tf_op | source)
XLA Modules:
  0.0 154.8 jit_solution(15796519393976756279)
XLA Ops:
  0.7 0.8 fusion.25
  2.0 1.2 broadcast_in_dim.82
  3.2 11.8 %all-to-all-start = ((bf16[16,64,640]{2,1,0:T(8,128)(2,1)}), bf16[16,64,640]{2,1,0:T(8,128)(2,1)}, u32[]{:S(2)}, u32[]{:S(2)}) async-start(bf16[16,64,640]{2,1,0:T(8,128)(2,1)} %broadcast_in_dim.82), calls=%async_computation | async-start | bytes 2621440 | tf_op jit(solution)/shard_map/all_to_all | solution.py:59
  15.1 7.6 %gather_fusion = bf16[1536,512]{1,0:T(8,128)(2,1)S(1)} fusion(bf16[4096,512]{1,0:T(8,128)(2,1)} %param.5, s32[2048]{0:T(1024)S(1)} %pad_clamp_fusion), kind=kCustom, calls=%fused_computation | custom fusion | bytes 3151872 | tf_op jit(solution)/shard_map/jit(_take)/gather | solution.py:67
  22.7 0.8 fusion.3
  23.4 1.1 fusion.4
  24.6 1.0 collective-permute-start
  25.9 2.9 %collective-permute-done.1 = s32[1536]{0:T(1024)S(1)} collective-permute-done((s32[1536]{0:T(1024)S(1)}, s32[1536]{0:T(1024)S(1)}, u32[]{:S(2)}, u32[]{:S(2)}) %collective-permute-start.1) | collective-permute-done | bytes 6176 | tf_op jit(solution)/shard_map/ppermute | solution.py:72
  28.8 2.1 %pad_maximum_fusion = bf16[3072,512]{1,0:T(8,128)(2,1)S(1)} fusion(bf16[1536,512]{1,0:T(8,128)(2,1)} %collective-permute-done, bf16[1536,512]{1,0:T(8,128)(2,1)} %copy-done.1), kind=kLoop, calls=%fused_computation.16 | loop fusion | flops 6291456 | bytes 6291456 | tf_op jit(solution)/shard_map/concatenate | solution.py:73
  30.9 16.4 %all-to-all-done = bf16[16,64,640]{2,1,0:T(8,128)(2,1)} async-done(((bf16[16,64,640]{2,1,0:T(8,128)(2,1)}), bf16[16,64,640]{2,1,0:T(8,128)(2,1)}, u32[]{:S(2)}, u32[]{:S(2)}) %all-to-all-start) | async-done | bytes 1310752 | tf_op jit(solution)/shard_map/all_to_all | solution.py:59
  47.3 1.1 slice_convert_fusion.2
  48.4 1.5 multiply_reduce_fusion
  49.9 0.5 fusion.11
  50.4 1.8 %fusion.1 = s32[1024]{0:T(1024)S(1)} fusion(s32[3072]{0:T(1024)S(1)} %pad_add_fusion, s32[1024]{0:T(1024)S(1)} %fusion.11), kind=kLoop, calls=%fused_computation.7 | loop fusion | flops 9436160 | bytes 20480 | tf_op jit(solution)/shard_map/reduce_sum | solution.py:90
  52.2 1.7 %compare_reduce_fusion = pred[1024]{0:T(1024)(128)(4,1)S(1)} fusion(s32[3072]{0:T(1024)S(1)} %pad_add_fusion, s32[1024]{0:T(1024)S(1)} %fusion.11), kind=kLoop, calls=%fused_computation.4 | loop fusion | flops 6290432 | bytes 17408 | tf_op jit(solution)/shard_map/reduce_or | solution.py:91
  53.9 9.0 %fusion.2 = (f32[1024]{0:T(1024)S(1)}, f32[1024]{0:T(1024)S(1)}, bf16[1024,3072]{1,0:T(8,128)(2,1)}) fusion(s32[3072]{0:T(1024)S(1)} %pad_add_fusion, s32[1024]{0:T(1024)S(1)} %fusion.11, bf16[1536,512]{1,0:T(8,128)(2,1)} %collective-permute-done, bf16[1536,512]{1,0:T(8,128)(2,1)S(1)} %copy-done.2, f32[1024]{0:T(1024)S(1)} %add_sqrt_fusion.1, ...), kind=kOutput, calls=%fused_computation.8 | convolution fusion | flops 3254253568 | bytes 10514432 | tf_op jit(solution)/shard_map/dot_general | solution.py:79
  63.1 6.5 %fusion.27 = f32[1024,512]{1,0:T(8,128)S(1)} fusion(bf16[1024,3072]{1,0:T(8,128)(2,1)} %get-tuple-element.10, bf16[1536,512]{1,0:T(8,128)(2,1)} %collective-permute-done, bf16[1536,512]{1,0:T(8,128)(2,1)} %copy-done.1), kind=kOutput, calls=%fused_computation.100 | convolution fusion | flops 3227516928 | bytes 11534336 | tf_op jit(solution)/shard_map/dot_general | solution.py:88
  69.7 1.8 %reduce-precision_convert_fusion = (bf16[8,16,8,512]{3,2,1,0:T(8,128)(2,1)}, bf16[8,16,8,512]{3,2,1,0:T(8,128)(2,1)}) fusion(f32[8,16,8,512]{3,2,1,0:T(8,128)S(1)} %bitcast.31), kind=kLoop, calls=%fused_computation.18 | loop fusion | flops 2097152 | bytes 4194304 | tf_op jit(solution)/shard_map/convert_element_type | solution.py:15
  72.0 5.1 %gather_fusion.1 = bf16[1024,512]{1,0:T(8,128)(2,1)} fusion(bf16[3072,512]{1,0:T(8,128)(2,1)S(1)} %pad_maximum_fusion, s32[1024]{0:T(1024)S(1)} %broadcast_clamp_fusion), kind=kCustom, calls=%fused_computation.1 | custom fusion | bytes 2101248 | tf_op jit(solution)/shard_map/jit(_take)/gather | solution.py:92
  77.3 1.6 %fusion.8 = bf16[2,8,8,8,512]{4,3,0,1,2:T(8,128)(2,1)S(1)} fusion(bf16[2,8,8,8,512]{4,3,2,1,0:T(8,128)(2,1)} %bitcast.32, pred[2,8,8,8]{3,0,1,2:T(4,128)(4,1)S(1)} %copy.28, pred[2,8,8,8]{3,0,1,2:T(4,128)(4,1)S(1)} %copy.27), kind=kLoop, calls=%fused_computation.29 | loop fusion | flops 1048576 | bytes 2099200 | tf_op jit(solution)/shard_map/jit(_where)/select_n | solution.py:92
  78.9 0.8 maximum_maximum_fusion
  79.7 41.5 %all_to_all.15 = bf16[8,16,8,1664]{3,2,1,0:T(8,128)(2,1)S(1)} all-to-all(bf16[8,16,8,1664]{3,2,1,0:T(8,128)(2,1)S(1)} %maximum_maximum_fusion), channel_id=1, replica_groups=mesh['section'=2,'dp'=16,'cls'=8] {'cls'}, dimensions={0} | all-to-all | bytes 6815744 | tf_op jit(solution)/shard_map/all_to_all | solution.py:27
  121.3 0.5 convert_element_type.79
  122.2 0.8 maximum_maximum_fusion.1
  123.1 9.7 %all-to-all-start.2 = ((bf16[16,8,1664]{2,1,0:T(8,128)(2,1)}), bf16[16,8,1664]{2,1,0:T(8,128)(2,1)S(1)}, u32[]{:S(2)}, u32[]{:S(2)}) async-start(bf16[16,8,1664]{2,1,0:T(8,128)(2,1)} %maximum_maximum_fusion.1), calls=%async_computation.2 | async-start | bytes 851968 | tf_op jit(solution)/shard_map/all_to_all | solution.py:27
  132.9 1.5 slice_convert_fusion
  134.4 11.0 %all-to-all-done.2 = bf16[16,8,1664]{2,1,0:T(8,128)(2,1)S(1)} async-done(((bf16[16,8,1664]{2,1,0:T(8,128)(2,1)}), bf16[16,8,1664]{2,1,0:T(8,128)(2,1)S(1)}, u32[]{:S(2)}, u32[]{:S(2)}) %all-to-all-start.2) | async-done | bytes 426016 | tf_op jit(solution)/shard_map/all_to_all | solution.py:27
  145.6 3.1 %collective-permute-start.3 = (f32[64]{0:T(128)S(1)}, f32[64]{0:T(128)S(1)}, u32[]{:S(2)}, u32[]{:S(2)}) collective-permute-start(f32[64]{0:T(128)S(1)} %get-tuple-element.20), channel_id=1, source_target_pairs={{0,128},{128,0},{1,129},{129,1},{2,130},{130,2},{3,131},{131,3},{4... | collective-permute-start | bytes 776 | tf_op jit(solution)/shard_map/ppermute | solution.py:121
  149.1 2.8 %collective-permute-start.2 = (f32[8,512]{1,0:T(8,128)S(1)}, f32[8,512]{1,0:T(8,128)S(1)}, u32[]{:S(2)}, u32[]{:S(2)}) collective-permute-start(f32[8,512]{1,0:T(8,128)S(1)} %subtract_divide_fusion), channel_id=1, source_target_pairs={{8,128},{24,144},{40,160},{56,176},{72,192},{88,208},{104,224},{12... | collective-permute-start | bytes 49160 | tf_op jit(solution)/shard_map/ppermute | solution.py:145
  151.9 0.6 fusion.21
  152.5 1.6 %collective-permute-done.2 = f32[8,512]{1,0:T(8,128)S(1)} collective-permute-done((f32[8,512]{1,0:T(8,128)S(1)}, f32[8,512]{1,0:T(8,128)S(1)}, u32[]{:S(2)}, u32[]{:S(2)}) %collective-permute-start.2) | collective-permute-done | bytes 16416 | tf_op jit(solution)/shard_map/ppermute | solution.py:145
  154.2 0.6 broadcast_select_fusion.1
  (64 shorter events, 2.9 us)
Async XLA Ops:
  0.6 1.2 copy-start
  0.6 14.3 %copy-start.5 = (s32[1,1536]{1,0:T(1,128)S(1)}, s32[1,1536]{1,0:T(1,128)}, u32[]{:S(2)}) copy-start(s32[1,1536]{1,0:T(1,128)} %param.6) | copy-start | bytes 18436
  3.2 44.1 %all-to-all-start = ((bf16[16,64,640]{2,1,0:T(8,128)(2,1)}), bf16[16,64,640]{2,1,0:T(8,128)(2,1)}, u32[]{:S(2)}, u32[]{:S(2)}) async-start(bf16[16,64,640]{2,1,0:T(8,128)(2,1)} %broadcast_in_dim.82), calls=%async_computation | async-start | bytes 2621440 | tf_op jit(solution)/shard_map/all_to_all | solution.py:59
  24.6 4.2 %copy-start.1 = (bf16[1536,512]{1,0:T(8,128)(2,1)}, bf16[1536,512]{1,0:T(8,128)(2,1)S(1)}, u32[]{:S(2)}) copy-start(bf16[1536,512]{1,0:T(8,128)(2,1)S(1)} %fusion.4) | copy-start | bytes 4718596
  24.6 4.2 %collective-permute-start = (bf16[1536,512]{1,0:T(8,128)(2,1)S(1)}, bf16[1536,512]{1,0:T(8,128)(2,1)}, u32[]{:S(2)}, u32[]{:S(2)}) collective-permute-start(bf16[1536,512]{1,0:T(8,128)(2,1)S(1)} %fusion.4), channel_id=1, source_target_pairs={{0,128},{128,0},{1,129},{129,1},{2,130},{130,2},{3,131},{131,3},{4... | collective-permute-start | bytes 4718600 | tf_op jit(solution)/shard_map/ppermute | solution.py:71
  25.6 3.2 %collective-permute-start.1 = (s32[1536]{0:T(1024)S(1)}, s32[1536]{0:T(1024)S(1)}, u32[]{:S(2)}, u32[]{:S(2)}) collective-permute-start(s32[1536]{0:T(1024)S(1)} %broadcast_add_fusion), channel_id=1, source_target_pairs={{0,128},{128,0},{1,129},{129,1},{2,130},{130,2},{3,131},{131,3},{4... | collective-permute-start | bytes 18440 | tf_op jit(solution)/shard_map/ppermute | solution.py:72
  47.3 6.6 %copy-start.2 = (bf16[1536,512]{1,0:T(8,128)(2,1)S(1)}, bf16[1536,512]{1,0:T(8,128)(2,1)}, u32[]{:S(2)}) copy-start(bf16[1536,512]{1,0:T(8,128)(2,1)} %copy-done.1) | copy-start | bytes 4718596
  77.0 1.9 %copy-start.3 = (bf16[8,16,8,512]{3,2,1,0:T(8,128)(2,1)S(1)}, bf16[8,16,8,512]{3,2,1,0:T(8,128)(2,1)}, u32[]{:S(2)}) copy-start(bf16[8,16,8,512]{3,2,1,0:T(8,128)(2,1)} %get-tuple-element.11) | copy-start | bytes 3145732
  77.0 1.9 %copy-start.4 = (bf16[8,16,8,512]{3,2,1,0:T(8,128)(2,1)S(1)}, bf16[8,16,8,512]{3,2,1,0:T(8,128)(2,1)}, u32[]{:S(2)}) copy-start(bf16[8,16,8,512]{3,2,1,0:T(8,128)(2,1)} %get-tuple-element.12) | copy-start | bytes 3145732
  123.1 22.4 %all-to-all-start.2 = ((bf16[16,8,1664]{2,1,0:T(8,128)(2,1)}), bf16[16,8,1664]{2,1,0:T(8,128)(2,1)S(1)}, u32[]{:S(2)}, u32[]{:S(2)}) async-start(bf16[16,8,1664]{2,1,0:T(8,128)(2,1)} %maximum_maximum_fusion.1), calls=%async_computation.2 | async-start | bytes 851968 | tf_op jit(solution)/shard_map/all_to_all | solution.py:27
  145.6 6.3 %collective-permute-start.3 = (f32[64]{0:T(128)S(1)}, f32[64]{0:T(128)S(1)}, u32[]{:S(2)}, u32[]{:S(2)}) collective-permute-start(f32[64]{0:T(128)S(1)} %get-tuple-element.20), channel_id=1, source_target_pairs={{0,128},{128,0},{1,129},{129,1},{2,130},{130,2},{3,131},{131,3},{4... | collective-permute-start | bytes 776 | tf_op jit(solution)/shard_map/ppermute | solution.py:121
  148.7 3.2 %collective-permute-start.4 = (f32[64]{0:T(128)S(1)}, f32[64]{0:T(128)S(1)}, u32[]{:S(2)}, u32[]{:S(2)}) collective-permute-start(f32[64]{0:T(128)S(1)} %get-tuple-element.19), channel_id=1, source_target_pairs={{0,128},{128,0},{1,129},{129,1},{2,130},{130,2},{3,131},{131,3},{4... | collective-permute-start | bytes 776 | tf_op jit(solution)/shard_map/ppermute | solution.py:121
  149.1 5.1 %collective-permute-start.2 = (f32[8,512]{1,0:T(8,128)S(1)}, f32[8,512]{1,0:T(8,128)S(1)}, u32[]{:S(2)}, u32[]{:S(2)}) collective-permute-start(f32[8,512]{1,0:T(8,128)S(1)} %subtract_divide_fusion), channel_id=1, source_target_pairs={{8,128},{24,144},{40,160},{56,176},{72,192},{88,208},{104,224},{12... | collective-permute-start | bytes 49160 | tf_op jit(solution)/shard_map/ppermute | solution.py:145

commit v13 on v11

--- a/solution.py
+++ b/solution.py
@@ -24,10 +24,14 @@
     packed = jnp.concatenate(
         [unscaled_high, unscaled_low, own_center.astype(jnp.bfloat16), extra_packed], axis=-1
     )
-    packed = lax.all_to_all(packed, axis, 0, 0, tiled=False).astype(jnp.float32)
-    unscaled = (packed[..., :width] + packed[..., width : 2 * width]).sum(0)
-    own_center = packed[..., 2 * width : 3 * width].sum(0)
-    extra_sum = (packed[..., 3 * width :][..., :3, :] + packed[..., 3 * width :][..., 3:6, :]).sum(0)
+    packed = lax.all_to_all(packed, axis, 0, 0, tiled=False)
+
+    def total(part):
+        return jnp.sum(part, axis=0, dtype=jnp.float32)
+
+    unscaled = total(packed[..., :width]) + total(packed[..., width : 2 * width])
+    own_center = total(packed[..., 2 * width : 3 * width])
+    extra_sum = total(packed[..., 3 * width :][..., :3, :]) + total(packed[..., 3 * width :][..., 3:6, :])
     extra = jnp.concatenate([extra_sum, jnp.zeros(extra_sum.shape[:-2] + (rows - 3, extra_sum.shape[-1]), jnp.float32)], axis=-2)
     return unscaled, own_center, extra
 

time: 149 us -> 150 us (level)
    convert_element_type x2 -> x0, other arithmetic: 1.52 us -> none  [reduce_stage(): packed = lax.all_to_all(packed, axis, 0, 0, tiled=False).astype(jnp.float32)]
  transfers between devices with their start and end apart: 7 -> 7, of which waited for: 4 -> 4; matrix products, arithmetic and copies ran while one was open for 8% -> 9% of each run, Pallas kernels for 0% -> 0%
where the time goes in v13:
time: 150 us; the launch traced here: 149 us
  blocking collectives  41.5 us (28%)
  waiting for transfers between devices  34 us (23%)
  starting transfers between devices  29 us (19%)
  matrix products  21.1 us (14%)
  local copies, waits for them, and re-layouts  11.7 us (8%)
  other arithmetic  11.1 us (7%)
    all_to_all x1, blocking collectives, reduce_stage(): packed = lax.all_to_all(packed, axis, 0, 0, tiled=False)  41.5 us
    all_to_all x1, waiting for transfers between devices, on_device(): lax.all_to_all(jnp.broadcast_to(packed[None], (batch_count,) + packed.sha...  17.4 us
    all_to_all x1, waiting for transfers between devices, reduce_stage(): packed = lax.all_to_all(packed, axis, 0, 0, tiled=False)  11.8 us
    all_to_all x1, starting transfers between devices, on_device(): lax.all_to_all(jnp.broadcast_to(packed[None], (batch_count,) + packed.sha...  11.7 us
    all_to_all x1, starting transfers between devices, reduce_stage(): packed = lax.all_to_all(packed, axis, 0, 0, tiled=False)  9.49 us
    dot_general x1, matrix products, on_device(): lax.dot_general(unit_rows, both_centers, (((1,), (1,)), ((), ())), prefer...  9.33 us
    gather x1, local copies, waits for them, and re-layouts, on_device(): chosen = jnp.take(centers, local_ids, axis=0).astype(jnp.float32)  7.59 us
    dot_general x1, matrix products, on_device(): jnp.dot(weights, both_centers, preferred_element_type=jnp.float32)  6.45 us
  transfers between devices with their start and end apart: 7, of which 4 were waited for; matrix products, arithmetic and copies ran while one was open for 9% of the time, Pallas kernels for 0%

profile of v13, /device:TPU:1, one launch (start us, length us, event | category | flops | bytes accessed | tf_op | source)
XLA Modules:
  0.0 149.5 jit_solution(16460912645541594554)
XLA Ops:
  0.7 0.8 fusion.27
  2.0 1.2 broadcast_in_dim.25
  3.2 11.7 %all-to-all-start = ((bf16[16,64,640]{2,1,0:T(8,128)(2,1)}), bf16[16,64,640]{2,1,0:T(8,128)(2,1)S(1)}, u32[]{:S(2)}, u32[]{:S(2)}) async-start(bf16[16,64,640]{2,1,0:T(8,128)(2,1)} %broadcast_in_dim.25), calls=%async_computation | async-start | bytes 2621440 | tf_op jit(solution)/shard_map/all_to_all | solution.py:63
  15.0 7.6 %gather_fusion = bf16[1536,512]{1,0:T(8,128)(2,1)S(1)} fusion(bf16[4096,512]{1,0:T(8,128)(2,1)} %param.5, s32[2048]{0:T(1024)S(1)} %pad_clamp_fusion), kind=kCustom, calls=%fused_computation | custom fusion | bytes 3151872 | tf_op jit(solution)/shard_map/jit(_take)/gather | solution.py:71
  22.6 0.8 fusion.6
  23.4 2.0 %fusion.7 = bf16[1536,512]{1,0:T(8,128)(2,1)} fusion(f32[1536]{0:T(1024)S(1)} %add_sqrt_fusion, bf16[1536,512]{1,0:T(8,128)(2,1)S(1)} %gather_fusion, pred[1536]{0:T(1024)(128)(4,1)S(1)} %compare_and_fusion), kind=kLoop, calls=%fused_computation.15 | loop fusion | flops 3145728 | bytes 3153408 | tf_op jit(solution)/shard_map/convert_element_type | solution.py:73
  25.4 1.0 collective-permute-start
  26.4 3.4 %collective-permute-done.1 = s32[1536]{0:T(1024)S(1)} collective-permute-done((s32[1536]{0:T(1024)S(1)}, s32[1536]{0:T(1024)S(1)}, u32[]{:S(2)}, u32[]{:S(2)}) %collective-permute-start.1) | collective-permute-done | bytes 6176 | tf_op jit(solution)/shard_map/ppermute | solution.py:76
  29.7 17.4 %all-to-all-done = bf16[16,64,640]{2,1,0:T(8,128)(2,1)S(1)} async-done(((bf16[16,64,640]{2,1,0:T(8,128)(2,1)}), bf16[16,64,640]{2,1,0:T(8,128)(2,1)S(1)}, u32[]{:S(2)}, u32[]{:S(2)}) %all-to-all-start) | async-done | bytes 1310752 | tf_op jit(solution)/shard_map/all_to_all | solution.py:63
  47.2 0.5 fusion.16
  47.7 0.3 multiply_reduce_fusion
  48.0 9.3 %fusion.3 = (f32[1024]{0:T(1024)S(1)}, f32[1024]{0:T(1024)S(1)}, bf16[1024,3072]{1,0:T(8,128)(2,1)}) fusion(s32[3072]{0:T(1024)S(1)} %pad_add_fusion, s32[1024]{0:T(1024)S(1)} %fusion.16, bf16[1536,512]{1,0:T(8,128)(2,1)} %collective-permute-done, bf16[1536,512]{1,0:T(8,128)(2,1)} %fusion.7, f32[1024]{0:T(1024)S(1)} %add_sqrt_fusion.1, ...), kind=kOutput, calls=%fused_computation.6 | convolution fusion | flops 3254253568 | bytes 10514432 | tf_op jit(solution)/shard_map/dot_general | solution.py:83
  57.5 6.5 %fusion.14 = f32[1024,512]{1,0:T(8,128)S(1)} fusion(bf16[1024,3072]{1,0:T(8,128)(2,1)} %get-tuple-element.15, bf16[1536,512]{1,0:T(8,128)(2,1)} %collective-permute-done, bf16[1536,512]{1,0:T(8,128)(2,1)} %fusion.7), kind=kOutput, calls=%fused_computation.30 | convolution fusion | flops 3227516928 | bytes 11534336 | tf_op jit(solution)/shard_map/dot_general | solution.py:92
  64.0 0.2 copy.35
  64.1 1.4 reduce-precision_convert_fusion
  65.7 5.3 %fusion.9 = bf16[1024,512]{1,0:T(8,128)(2,1)S(1)} fusion(s32[3072]{0:T(1024)S(1)} %pad_add_fusion, s32[1024]{0:T(1024)S(1)} %fusion.16, bf16[1536,512]{1,0:T(8,128)(2,1)} %collective-permute-done, bf16[1536,512]{1,0:T(8,128)(2,1)} %fusion.7), kind=kOutput, calls=%fused_computation.25 | convolution fusion | flops 3231186944 | bytes 4210688 | tf_op jit(solution)/shard_map/dot_general | solution.py:93
  71.4 0.9 copy-done.1
  72.2 0.8 maximum_maximum_fusion
  73.0 41.5 %all_to_all.15 = bf16[8,16,8,1664]{3,2,1,0:T(8,128)(2,1)S(1)} all-to-all(bf16[8,16,8,1664]{3,2,1,0:T(8,128)(2,1)S(1)} %maximum_maximum_fusion), channel_id=1, replica_groups=mesh['section'=2,'dp'=16,'cls'=8] {'cls'}, dimensions={0} | all-to-all | bytes 6815744 | tf_op jit(solution)/shard_map/all_to_all | solution.py:27
  114.5 0.3 convert_reduce_fusion
  115.2 0.8 maximum_maximum_fusion.1
  116.1 9.5 %all-to-all-start.2 = ((bf16[16,8,1664]{2,1,0:T(8,128)(2,1)}), bf16[16,8,1664]{2,1,0:T(8,128)(2,1)}, u32[]{:S(2)}, u32[]{:S(2)}) async-start(bf16[16,8,1664]{2,1,0:T(8,128)(2,1)} %maximum_maximum_fusion.1), calls=%async_computation.2 | async-start | bytes 851968 | tf_op jit(solution)/shard_map/all_to_all | solution.py:27
  125.7 0.3 slice_convert_fusion
  126.0 11.8 %all-to-all-done.2 = bf16[16,8,1664]{2,1,0:T(8,128)(2,1)} async-done(((bf16[16,8,1664]{2,1,0:T(8,128)(2,1)}), bf16[16,8,1664]{2,1,0:T(8,128)(2,1)}, u32[]{:S(2)}, u32[]{:S(2)}) %all-to-all-start.2) | async-done | bytes 426016 | tf_op jit(solution)/shard_map/all_to_all | solution.py:27
  137.7 0.8 fusion.32
  138.6 3.7 %collective-permute-start.3 = (f32[64]{0:T(128)S(1)}, f32[64]{0:T(128)S(1)}, u32[]{:S(2)}, u32[]{:S(2)}) collective-permute-start(f32[64]{0:T(128)S(1)} %get-tuple-element.27), channel_id=1, source_target_pairs={{0,128},{128,0},{1,129},{129,1},{2,130},{130,2},{3,131},{131,3},{4... | collective-permute-start | bytes 776 | tf_op jit(solution)/shard_map/ppermute | solution.py:122
  142.4 1.1 convert_reduce_fusion.3
  143.5 0.2 multiply_reduce_fusion.1
  143.8 3.0 %collective-permute-start.2 = (f32[8,512]{1,0:T(8,128)S(1)}, f32[8,512]{1,0:T(8,128)S(1)}, u32[]{:S(2)}, u32[]{:S(2)}) collective-permute-start(f32[8,512]{1,0:T(8,128)S(1)} %subtract_divide_fusion), channel_id=1, source_target_pairs={{8,128},{24,144},{40,160},{56,176},{72,192},{88,208},{104,224},{12... | collective-permute-start | bytes 49160 | tf_op jit(solution)/shard_map/ppermute | solution.py:146
  146.9 0.6 fusion.23
  147.5 1.4 collective-permute-done.2
  148.9 0.6 broadcast_select_fusion.1
  (49 shorter events, 1.9 us)
Async XLA Ops:
  0.6 1.2 copy-start
  0.6 14.3 %copy-start.2 = (s32[1,1536]{1,0:T(1,128)S(1)}, s32[1,1536]{1,0:T(1,128)}, u32[]{:S(2)}) copy-start(s32[1,1536]{1,0:T(1,128)} %param.6) | copy-start | bytes 18436
  3.2 44.0 %all-to-all-start = ((bf16[16,64,640]{2,1,0:T(8,128)(2,1)}), bf16[16,64,640]{2,1,0:T(8,128)(2,1)S(1)}, u32[]{:S(2)}, u32[]{:S(2)}) async-start(bf16[16,64,640]{2,1,0:T(8,128)(2,1)} %broadcast_in_dim.25), calls=%async_computation | async-start | bytes 2621440 | tf_op jit(solution)/shard_map/all_to_all | solution.py:63
  25.4 22.6 %collective-permute-start = (bf16[1536,512]{1,0:T(8,128)(2,1)}, bf16[1536,512]{1,0:T(8,128)(2,1)}, u32[]{:S(2)}, u32[]{:S(2)}) collective-permute-start(bf16[1536,512]{1,0:T(8,128)(2,1)} %fusion.7), channel_id=1, source_target_pairs={{0,128},{128,0},{1,129},{129,1},{2,130},{130,2},{3,131},{131,3},{4... | collective-permute-start | bytes 4718600 | tf_op jit(solution)/shard_map/ppermute | solution.py:75
  26.3 3.4 %collective-permute-start.1 = (s32[1536]{0:T(1024)S(1)}, s32[1536]{0:T(1024)S(1)}, u32[]{:S(2)}, u32[]{:S(2)}) collective-permute-start(s32[1536]{0:T(1024)S(1)} %broadcast_add_fusion), channel_id=1, source_target_pairs={{0,128},{128,0},{1,129},{129,1},{2,130},{130,2},{3,131},{131,3},{4... | collective-permute-start | bytes 18440 | tf_op jit(solution)/shard_map/ppermute | solution.py:76
  71.0 1.2 copy-start.1
  116.1 21.7 %all-to-all-start.2 = ((bf16[16,8,1664]{2,1,0:T(8,128)(2,1)}), bf16[16,8,1664]{2,1,0:T(8,128)(2,1)}, u32[]{:S(2)}, u32[]{:S(2)}) async-start(bf16[16,8,1664]{2,1,0:T(8,128)(2,1)} %maximum_maximum_fusion.1), calls=%async_computation.2 | async-start | bytes 851968 | tf_op jit(solution)/shard_map/all_to_all | solution.py:27
  138.6 8.2 %collective-permute-start.3 = (f32[64]{0:T(128)S(1)}, f32[64]{0:T(128)S(1)}, u32[]{:S(2)}, u32[]{:S(2)}) collective-permute-start(f32[64]{0:T(128)S(1)} %get-tuple-element.27), channel_id=1, source_target_pairs={{0,128},{128,0},{1,129},{129,1},{2,130},{130,2},{3,131},{131,3},{4... | collective-permute-start | bytes 776 | tf_op jit(solution)/shard_map/ppermute | solution.py:122
  142.3 4.5 %collective-permute-start.4 = (f32[64]{0:T(128)S(1)}, f32[64]{0:T(128)S(1)}, u32[]{:S(2)}, u32[]{:S(2)}) collective-permute-start(f32[64]{0:T(128)S(1)} %get-tuple-element.26), channel_id=1, source_target_pairs={{0,128},{128,0},{1,129},{129,1},{2,130},{130,2},{3,131},{131,3},{4... | collective-permute-start | bytes 776 | tf_op jit(solution)/shard_map/ppermute | solution.py:122
  143.8 5.1 %collective-permute-start.2 = (f32[8,512]{1,0:T(8,128)S(1)}, f32[8,512]{1,0:T(8,128)S(1)}, u32[]{:S(2)}, u32[]{:S(2)}) collective-permute-start(f32[8,512]{1,0:T(8,128)S(1)} %subtract_divide_fusion), channel_id=1, source_target_pairs={{8,128},{24,144},{40,160},{56,176},{72,192},{88,208},{104,224},{12... | collective-permute-start | bytes 49160 | tf_op jit(solution)/shard_map/ppermute | solution.py:146

commit v14 on v11

--- a/solution.py
+++ b/solution.py
@@ -115,7 +115,7 @@
 
     half_total = summed[0, 2 * width : 2 * width + half]
     half_target = summed[1, 2 * width : 2 * width + half]
-    other_total, other_target = lax.ppermute((half_total, half_target), "section", swap)
+    other_total, other_target = lax.ppermute(jnp.stack([half_total, half_target]), "section", swap)
     first = section == 0
     block_total = jnp.where(first, jnp.concatenate([half_total, other_total]), jnp.concatenate([other_total, half_total]))
     block_target = jnp.where(first, jnp.concatenate([half_target, other_target]), jnp.concatenate([other_target, half_target]))

time: 149 us -> 150 us (level)
    ppermute x2 -> x1, starting transfers between devices: 3.8 us -> 3.13 us  [on_device(): lax.ppermute(jnp.stack([half_total, half_target]), 'section', swap)]
  transfers between devices with their start and end apart: 7 -> 6, of which waited for: 4 -> 4; matrix products, arithmetic and copies ran while one was open for 8% -> 8% of each run, Pallas kernels for 0% -> 0%
where the time goes in v14:
time: 150 us; the launch traced here: 149 us
  blocking collectives  41.6 us (28%)
  waiting for transfers between devices  35.2 us (23%)
  starting transfers between devices  28 us (19%)
  matrix products  21.1 us (14%)
  other arithmetic  11.4 us (8%)
  local copies, waits for them, and re-layouts  10.9 us (7%)
    all_to_all x1, blocking collectives, reduce_stage(): packed = lax.all_to_all(packed, axis, 0, 0, tiled=False).astype(jnp.float32)  41.6 us
    all_to_all x1, waiting for transfers between devices, on_device(): lax.all_to_all(jnp.broadcast_to(packed[None], (batch_count,) + packed.sha...  17.4 us
    all_to_all x1, waiting for transfers between devices, reduce_stage(): packed = lax.all_to_all(packed, axis, 0, 0, tiled=False).astype(jnp.float32)  12.3 us
    all_to_all x1, starting transfers between devices, on_device(): lax.all_to_all(jnp.broadcast_to(packed[None], (batch_count,) + packed.sha...  11.7 us
    all_to_all x1, starting transfers between devices, reduce_stage(): packed = lax.all_to_all(packed, axis, 0, 0, tiled=False).astype(jnp.float32)  9.74 us
    dot_general x1, matrix products, on_device(): lax.dot_general(unit_rows, both_centers, (((1,), (1,)), ((), ())), prefer...  9.32 us
    gather x1, local copies, waits for them, and re-layouts, on_device(): chosen = jnp.take(centers, local_ids, axis=0).astype(jnp.float32)  7.59 us
    dot_general x1, matrix products, on_device(): jnp.dot(weights, both_centers, preferred_element_type=jnp.float32)  6.45 us
  transfers between devices with their start and end apart: 6, of which 4 were waited for; matrix products, arithmetic and copies ran while one was open for 8% of the time, Pallas kernels for 0%

profile of v14, /device:TPU:1, one launch (start us, length us, event | category | flops | bytes accessed | tf_op | source)
XLA Modules:
  0.0 149.1 jit_solution(1164197765271873271)
XLA Ops:
  0.7 0.8 fusion.31
  2.0 1.2 broadcast_in_dim.25
  3.2 11.7 %all-to-all-start = ((bf16[16,64,640]{2,1,0:T(8,128)(2,1)}), bf16[16,64,640]{2,1,0:T(8,128)(2,1)S(1)}, u32[]{:S(2)}, u32[]{:S(2)}) async-start(bf16[16,64,640]{2,1,0:T(8,128)(2,1)} %broadcast_in_dim.25), calls=%async_computation | async-start | bytes 2621440 | tf_op jit(solution)/shard_map/all_to_all | solution.py:59
  15.0 7.6 %gather_fusion = bf16[1536,512]{1,0:T(8,128)(2,1)S(1)} fusion(bf16[4096,512]{1,0:T(8,128)(2,1)} %param.5, s32[2048]{0:T(1024)S(1)} %pad_clamp_fusion), kind=kCustom, calls=%fused_computation | custom fusion | bytes 3151872 | tf_op jit(solution)/shard_map/jit(_take)/gather | solution.py:67
  22.6 0.8 fusion.6
  23.4 2.0 %fusion.7 = bf16[1536,512]{1,0:T(8,128)(2,1)} fusion(f32[1536]{0:T(1024)S(1)} %add_sqrt_fusion, bf16[1536,512]{1,0:T(8,128)(2,1)S(1)} %gather_fusion, pred[1536]{0:T(1024)(128)(4,1)S(1)} %compare_and_fusion), kind=kLoop, calls=%fused_computation.15 | loop fusion | flops 3145728 | bytes 3153408 | tf_op jit(solution)/shard_map/convert_element_type | solution.py:69
  25.4 1.0 collective-permute-start
  26.4 3.4 %collective-permute-done.1 = s32[1536]{0:T(1024)S(1)} collective-permute-done((s32[1536]{0:T(1024)S(1)}, s32[1536]{0:T(1024)S(1)}, u32[]{:S(2)}, u32[]{:S(2)}) %collective-permute-start.1) | collective-permute-done | bytes 6176 | tf_op jit(solution)/shard_map/ppermute | solution.py:72
  29.7 17.4 %all-to-all-done = bf16[16,64,640]{2,1,0:T(8,128)(2,1)S(1)} async-done(((bf16[16,64,640]{2,1,0:T(8,128)(2,1)}), bf16[16,64,640]{2,1,0:T(8,128)(2,1)S(1)}, u32[]{:S(2)}, u32[]{:S(2)}) %all-to-all-start) | async-done | bytes 1310752 | tf_op jit(solution)/shard_map/all_to_all | solution.py:59
  47.2 0.5 fusion.17
  47.7 0.3 multiply_reduce_fusion
  48.0 9.3 %fusion.3 = (f32[1024]{0:T(1024)S(1)}, f32[1024]{0:T(1024)S(1)}, bf16[1024,3072]{1,0:T(8,128)(2,1)}) fusion(s32[3072]{0:T(1024)S(1)} %pad_add_fusion, s32[1024]{0:T(1024)S(1)} %fusion.17, bf16[1536,512]{1,0:T(8,128)(2,1)} %collective-permute-done, bf16[1536,512]{1,0:T(8,128)(2,1)} %fusion.7, f32[1024]{0:T(1024)S(1)} %add_sqrt_fusion.1, ...), kind=kOutput, calls=%fused_computation.6 | convolution fusion | flops 3254253568 | bytes 10514432 | tf_op jit(solution)/shard_map/dot_general | solution.py:79
  57.5 6.5 %fusion.15 = f32[1024,512]{1,0:T(8,128)S(1)} fusion(bf16[1024,3072]{1,0:T(8,128)(2,1)} %get-tuple-element.10, bf16[1536,512]{1,0:T(8,128)(2,1)} %collective-permute-done, bf16[1536,512]{1,0:T(8,128)(2,1)} %fusion.7), kind=kOutput, calls=%fused_computation.30 | convolution fusion | flops 3227516928 | bytes 11534336 | tf_op jit(solution)/shard_map/dot_general | solution.py:88
  64.0 0.2 copy.18
  64.1 1.4 reduce-precision_convert_fusion
  65.6 5.3 %fusion.10 = bf16[1024,512]{1,0:T(8,128)(2,1)S(1)} fusion(s32[3072]{0:T(1024)S(1)} %pad_add_fusion, s32[1024]{0:T(1024)S(1)} %fusion.17, bf16[1536,512]{1,0:T(8,128)(2,1)} %collective-permute-done, bf16[1536,512]{1,0:T(8,128)(2,1)} %fusion.7), kind=kOutput, calls=%fused_computation.26 | convolution fusion | flops 3231186944 | bytes 4210688 | tf_op jit(solution)/shard_map/dot_general | solution.py:89
  71.4 0.9 copy-done.1
  72.2 0.8 maximum_maximum_fusion
  73.0 41.6 %all_to_all.15 = bf16[8,16,8,1664]{3,2,1,0:T(8,128)(2,1)S(1)} all-to-all(bf16[8,16,8,1664]{3,2,1,0:T(8,128)(2,1)S(1)} %maximum_maximum_fusion), channel_id=1, replica_groups=mesh['section'=2,'dp'=16,'cls'=8] {'cls'}, dimensions={0} | all-to-all | bytes 6815744 | tf_op jit(solution)/shard_map/all_to_all | solution.py:27
  114.5 0.5 convert_element_type.85
  115.0 0.3 fusion.9
  115.5 0.8 maximum_maximum_fusion.1
  116.3 9.7 %all-to-all-start.2 = ((bf16[16,8,1664]{2,1,0:T(8,128)(2,1)}), bf16[16,8,1664]{2,1,0:T(8,128)(2,1)}, u32[]{:S(2)}, u32[]{:S(2)}) async-start(bf16[16,8,1664]{2,1,0:T(8,128)(2,1)} %maximum_maximum_fusion.1), calls=%async_computation.2 | async-start | bytes 851968 | tf_op jit(solution)/shard_map/all_to_all | solution.py:27
  126.2 0.3 slice_convert_fusion
  126.5 12.3 %all-to-all-done.2 = bf16[16,8,1664]{2,1,0:T(8,128)(2,1)} async-done(((bf16[16,8,1664]{2,1,0:T(8,128)(2,1)}), bf16[16,8,1664]{2,1,0:T(8,128)(2,1)}, u32[]{:S(2)}, u32[]{:S(2)}) %all-to-all-start.2) | async-done | bytes 426016 | tf_op jit(solution)/shard_map/all_to_all | solution.py:27
  138.8 1.1 convert_element_type.91
  140.0 3.1 %collective-permute-start.3 = (f32[2,64]{1,0:T(2,128)S(1)}, f32[2,64]{1,0:T(2,128)S(1)}, u32[]{:S(2)}, u32[]{:S(2)}) collective-permute-start(f32[2,64]{1,0:T(2,128)S(1)} %stack.32), channel_id=1, source_target_pairs={{0,128},{128,0},{1,129},{129,1},{2,130},{130,2},{3,131},{131,3},{4... | collective-permute-start | bytes 1544 | tf_op jit(solution)/shard_map/ppermute | solution.py:118
  143.1 0.2 multiply_reduce_fusion.1
  143.4 2.4 %collective-permute-start.2 = (f32[8,512]{1,0:T(8,128)S(1)}, f32[8,512]{1,0:T(8,128)S(1)}, u32[]{:S(2)}, u32[]{:S(2)}) collective-permute-start(f32[8,512]{1,0:T(8,128)S(1)} %subtract_divide_fusion), channel_id=1, source_target_pairs={{8,128},{24,144},{40,160},{56,176},{72,192},{88,208},{104,224},{12... | collective-permute-start | bytes 49160 | tf_op jit(solution)/shard_map/ppermute | solution.py:142
  145.8 0.6 fusion.27
  146.4 2.0 %collective-permute-done.2 = f32[8,512]{1,0:T(8,128)S(1)} collective-permute-done((f32[8,512]{1,0:T(8,128)S(1)}, f32[8,512]{1,0:T(8,128)S(1)}, u32[]{:S(2)}, u32[]{:S(2)}) %collective-permute-start.2) | collective-permute-done | bytes 16416 | tf_op jit(solution)/shard_map/ppermute | solution.py:142
  148.4 0.6 broadcast_select_fusion.1
  (48 shorter events, 1.7 us)
Async XLA Ops:
  0.6 1.2 copy-start
  0.6 14.3 %copy-start.2 = (s32[1,1536]{1,0:T(1,128)S(1)}, s32[1,1536]{1,0:T(1,128)}, u32[]{:S(2)}) copy-start(s32[1,1536]{1,0:T(1,128)} %param.6) | copy-start | bytes 18436
  3.2 44.0 %all-to-all-start = ((bf16[16,64,640]{2,1,0:T(8,128)(2,1)}), bf16[16,64,640]{2,1,0:T(8,128)(2,1)S(1)}, u32[]{:S(2)}, u32[]{:S(2)}) async-start(bf16[16,64,640]{2,1,0:T(8,128)(2,1)} %broadcast_in_dim.25), calls=%async_computation | async-start | bytes 2621440 | tf_op jit(solution)/shard_map/all_to_all | solution.py:59
  25.4 22.6 %collective-permute-start = (bf16[1536,512]{1,0:T(8,128)(2,1)}, bf16[1536,512]{1,0:T(8,128)(2,1)}, u32[]{:S(2)}, u32[]{:S(2)}) collective-permute-start(bf16[1536,512]{1,0:T(8,128)(2,1)} %fusion.7), channel_id=1, source_target_pairs={{0,128},{128,0},{1,129},{129,1},{2,130},{130,2},{3,131},{131,3},{4... | collective-permute-start | bytes 4718600 | tf_op jit(solution)/shard_map/ppermute | solution.py:71
  26.3 3.4 %collective-permute-start.1 = (s32[1536]{0:T(1024)S(1)}, s32[1536]{0:T(1024)S(1)}, u32[]{:S(2)}, u32[]{:S(2)}) collective-permute-start(s32[1536]{0:T(1024)S(1)} %broadcast_add_fusion), channel_id=1, source_target_pairs={{0,128},{128,0},{1,129},{129,1},{2,130},{130,2},{3,131},{131,3},{4... | collective-permute-start | bytes 18440 | tf_op jit(solution)/shard_map/ppermute | solution.py:72
  71.0 1.2 copy-start.1
  116.3 22.5 %all-to-all-start.2 = ((bf16[16,8,1664]{2,1,0:T(8,128)(2,1)}), bf16[16,8,1664]{2,1,0:T(8,128)(2,1)}, u32[]{:S(2)}, u32[]{:S(2)}) async-start(bf16[16,8,1664]{2,1,0:T(8,128)(2,1)} %maximum_maximum_fusion.1), calls=%async_computation.2 | async-start | bytes 851968 | tf_op jit(solution)/shard_map/all_to_all | solution.py:27
  140.0 5.8 %collective-permute-start.3 = (f32[2,64]{1,0:T(2,128)S(1)}, f32[2,64]{1,0:T(2,128)S(1)}, u32[]{:S(2)}, u32[]{:S(2)}) collective-permute-start(f32[2,64]{1,0:T(2,128)S(1)} %stack.32), channel_id=1, source_target_pairs={{0,128},{128,0},{1,129},{129,1},{2,130},{130,2},{3,131},{131,3},{4... | collective-permute-start | bytes 1544 | tf_op jit(solution)/shard_map/ppermute | solution.py:118
  143.4 5.1 %collective-permute-start.2 = (f32[8,512]{1,0:T(8,128)S(1)}, f32[8,512]{1,0:T(8,128)S(1)}, u32[]{:S(2)}, u32[]{:S(2)}) collective-permute-start(f32[8,512]{1,0:T(8,128)S(1)} %subtract_divide_fusion), channel_id=1, source_target_pairs={{8,128},{24,144},{40,160},{56,176},{72,192},{88,208},{104,224},{12... | collective-permute-start | bytes 49160 | tf_op jit(solution)/shard_map/ppermute | solution.py:142
